TPU v7x, 32 devices: a whole 2x2x4 slice. The times are simulated.
32 devices in a mesh: dp: 8 (over z, core), expert: 4 (over y, x).
Axes of the slice: x: 2, y: 2, z: 4, core: 2. Of those that a mesh axis runs over, the one named last changes fastest.
Arguments:
- activations: bfloat16 [2048, 8, 768], P(('dp', 'expert')), may hold values from -6 to 6
- out_grad: bfloat16 [2048, 2048], P(('dp', 'expert')), may hold values from -0.796875 to 0.796875
- gate_weights: float32 [2048, 8], P(('dp', 'expert')), may hold values from 0.02 to 0.3
- routes: int32 [2048, 8], P(('dp', 'expert')), may hold values from 0 to 15, all different within a row; in each aligned block of 64 rows (0 to 63, 64 to 127, ...) at most 64 rows name the same one
- momentum: float32 [32768, 768], P(('expert', 'dp')), may hold values from -4 to 4
Outputs:
- update: bfloat16 [32768, 768], P(('expert', 'dp'))
- new_momentum: float32 [32768, 768], P(('expert', 'dp'))
Inputs may be any that keep to these rules, and one draw needn't show every extreme that they name: `routes`: each row names 8 different experts. Among the 64 rows of one device no expert is named by more than 64 rows, and in every draw some expert is named by exactly 64 rows of some device.
All inputs are finite; a program needn't handle non-finite values.
Results may differ from a plain program's by a relative error of at most 0.029.
Values may be sent and summed in bfloat16 or wider, within the bound.
No kernel may reach another device: no remote copies, remote signals or barrier semaphores. Data moves between devices by JAX's collectives and lax.ppermute only.
A program may use at most 128 MiB of HBM per device.

v0:
```python
import math

import jax
import jax.numpy as jnp
from jax import lax
from jax.sharding import PartitionSpec as P

EXP_DEV = 4
NS_ITERS = 2


MOMENT = 0.95
COEFF_A = 3.4445
COEFF_B = -4.775
COEFF_C = 2.0315
EPSILON = 1e-07


def swapped(block, axis, apart):
    count = lax.axis_size(axis)
    route = []
    for low in range(count):
        high = low | 1 << apart
        if high != low and high < count:
            route += [(low, high), (high, low)]
    return lax.ppermute(block, axis, route)


def slot_table(routing, expert_total, capacity):
    tokens_here = routing.shape[0]
    slots_token = routing.shape[1]
    numbers = jnp.arange(expert_total, dtype=jnp.int32)
    matched = (routing[:, :, None] == numbers[None, None, :]).astype(jnp.int32)
    named_by = jnp.sum(matched, axis=1)
    position = jnp.sum(matched * jnp.arange(slots_token, dtype=jnp.int32)[None, :, None], axis=1)
    earlier = jnp.cumsum(named_by, axis=0) - named_by
    places = jnp.arange(capacity, dtype=jnp.int32)
    picked = ((named_by[:, :, None] == 1) & (earlier[:, :, None] == places[None, None, :])).astype(
        jnp.int32
    )
    pair_index = jnp.arange(tokens_here, dtype=jnp.int32)[:, None] * slots_token + position
    source = jnp.sum(picked * pair_index[:, :, None], axis=0)
    filled = jnp.sum(picked, axis=0) > 0
    return (source, filled)


def pack_slots(hidden_block, grad_block, gate_block, source, filled, slots_token):
    hidden_rows = hidden_block.reshape(-1, hidden_block.shape[-1])
    picked_rows = jnp.where(
        filled[..., None], jnp.take(hidden_rows, source, axis=0), jnp.zeros((), hidden_rows.dtype)
    )
    scales = jnp.where(filled, jnp.take(gate_block.reshape(-1), source), jnp.zeros((), jnp.float32))
    grad_rows = jnp.take(grad_block, source // slots_token, axis=0).astype(jnp.float32)
    weighted = (scales[..., None] * grad_rows).astype(jnp.bfloat16)
    return (picked_rows, weighted)


def newton_update(scaled, gram):
    square = jnp.dot(gram, gram, preferred_element_type=jnp.float32)
    poly = (COEFF_B * gram.astype(jnp.float32) + COEFF_C * square).astype(jnp.bfloat16)
    product = jnp.dot(scaled, poly, preferred_element_type=jnp.float32)
    return (COEFF_A * scaled.astype(jnp.float32) + product).astype(jnp.bfloat16)


def gram_of(scaled):
    return lax.dot_general(
        scaled, scaled, (((0,), (0,)), ((), ())), preferred_element_type=jnp.float32
    )


def body(activations, out_grad, gate_weights, routes, momentum):
    expert_count = lax.axis_size("expert")
    dp_count = lax.axis_size("dp")
    tokens_here = routes.shape[0]
    slots_token = routes.shape[1]
    expert_total = EXP_DEV * expert_count
    capacity = min(tokens_here, 2 * tokens_here * slots_token // expert_total)
    model_width = out_grad.shape[1]
    hidden_width = activations.shape[2]
    own_rows = momentum.shape[0]
    group_size = dp_count // EXP_DEV
    levels = group_size.bit_length() - 1
    source, filled = slot_table(routes, expert_total, capacity)
    source = (
        source.reshape(expert_count, EXP_DEV, capacity)
        .transpose(1, 0, 2)
        .reshape(EXP_DEV, expert_count * capacity)
    )
    filled = (
        filled.reshape(expert_count, EXP_DEV, capacity)
        .transpose(1, 0, 2)
        .reshape(EXP_DEV, expert_count * capacity)
    )
    hidden_send, weighted_send = pack_slots(
        activations, out_grad, gate_weights, source, filled, slots_token
    )
    hidden_got, weighted_got = (
        lax.all_to_all(hidden_send, "expert", split_axis=1, concat_axis=1, tiled=True),
        lax.all_to_all(weighted_send, "expert", split_axis=1, concat_axis=1, tiled=True),
    )

    def block_rows(block_index):
        begin_row = block_index * own_rows
        expert_local = begin_row // model_width
        column = begin_row % model_width
        hidden_expert = lax.dynamic_index_in_dim(hidden_got, expert_local, 0, keepdims=False)
        weighted_expert = lax.dynamic_index_in_dim(weighted_got, expert_local, 0, keepdims=False)
        columns = lax.dynamic_slice_in_dim(weighted_expert, column, own_rows, 1)
        return lax.dot_general(
            columns, hidden_expert, (((0,), (0,)), ((), ())), preferred_element_type=jnp.float32
        )

    blocks = lax.map(
        block_rows, jnp.arange(own_rows * lax.axis_size("dp") // own_rows, dtype=jnp.int32)
    )
    gradient = lax.psum_scatter(
        blocks.reshape(own_rows * lax.axis_size("dp"), hidden_width).astype(jnp.bfloat16),
        "dp",
        scatter_dimension=0,
        tiled=True,
    ).astype(jnp.float32)
    new_momentum = MOMENT * momentum + gradient
    ahead = gradient + MOMENT * new_momentum
    rank_dp = lax.axis_index("dp")
    part_index = rank_dp % group_size
    gathered = ahead
    for bit_index in range(levels):
        other = swapped(gathered.astype(jnp.bfloat16), "dp", bit_index).astype(gathered.dtype)
        upper = rank_dp // 2**bit_index % 2
        gathered = jnp.where(
            upper == 0, jnp.concatenate([gathered, other], 0), jnp.concatenate([other, gathered], 0)
        )
    norm_value = jnp.sqrt(jnp.sum(gathered * gathered))
    scaled_whole = (gathered / (norm_value + EPSILON)).astype(jnp.bfloat16)
    for turn_index in range(NS_ITERS):
        gram = gram_of(scaled_whole).astype(jnp.bfloat16)
        scaled_whole = newton_update(scaled_whole, gram)
    scaled = lax.dynamic_slice_in_dim(scaled_whole, part_index * own_rows, own_rows, 0)
    update = (math.sqrt(model_width) * scaled.astype(jnp.float32)).astype(jnp.bfloat16)
    return (update, new_momentum)


def solution(mesh):
    in_specs = (
        P(("dp", "expert"), None, None),
        P(("dp", "expert"), None),
        P(("dp", "expert"), None),
        P(("dp", "expert"), None),
        P(("expert", "dp"), None),
    )
    out_specs = (P(("expert", "dp"), None), P(("expert", "dp"), None))
    return jax.shard_map(body, mesh=mesh, in_specs=in_specs, out_specs=out_specs, check_vma=False)
```

profile of v0, /device:TPU:0, one launch (start us, length us, event | category | flops | bytes accessed | tf_op | source)
XLA Modules:
  0.0 328.4 jit_solution(900468146776396719)
XLA Ops:
  7.2 0.8 convert_reduce_fusion.1
  8.4 0.6 convert_reduce_fusion
  9.1 0.8 copy.34
  10.0 6.9 %gather_fusion = f32[1024]{0:T(1024)S(1)} fusion(f32[512]{0:T(512)S(1)} %reshape.202, s32[1024]{0:T(1024)S(1)} %broadcast_clamp_fusion.1), kind=kCustom, calls=%fused_computation | custom fusion | bytes 12288 | tf_op jit(solution)/shard_map/jit(_take)/gather | solution.py:52
  17.0 0.2 copy.39
  17.2 0.2 copy.40
  17.4 4.0 %gather_fusion.2 = bf16[1024,768]{1,0:T(8,128)(2,1)S(1)} fusion(bf16[512,768]{1,0:T(8,128)(2,1)S(1)} %bitcast.45, s32[1024]{0:T(1024)S(1)} %broadcast_clamp_fusion.1), kind=kCustom, calls=%fused_computation.2 | custom fusion | bytes 3149824 | tf_op jit(solution)/shard_map/jit(_take)/gather | solution.py:50
  21.4 4.3 %fusion.6 = bf16[4,256,768]{2,0,1:T(4,128)(2,1)} fusion(bf16[4,256,768]{2,1,0:T(8,128)(2,1)S(1)} %bitcast.48, pred[4,256]{0,1:T(8,128)(4,1)S(1)} %copy.40, pred[4,256]{0,1:T(8,128)(4,1)S(1)} %copy.39), kind=kLoop, calls=%fused_computation.23 | loop fusion | flops 1572864 | bytes 3147776 | tf_op jit(solution)/shard_map/jit(_where)/select_n | solution.py:49
  25.7 5.2 %all-to-all-start.1 = ((bf16[4,256,768]{2,0,1:T(4,128)(2,1)}), bf16[4,256,768]{2,0,1:T(4,128)(2,1)S(1)}, u32[]{:S(2)}, u32[]{:S(2)}) async-start(bf16[4,256,768]{2,0,1:T(4,128)(2,1)} %fusion.6), calls=%async_computation.1 | async-start | bytes 3145728 | tf_op jit(solution)/shard_map/all_to_all | solution.py:98
  30.9 0.1 copy.36
  31.0 0.2 copy.37
  31.2 6.0 %gather_fusion.1 = bf16[1024,2048]{1,0:T(8,128)(2,1)} fusion(bf16[64,2048]{1,0:T(8,128)(2,1)S(1)} %copy-done.2, s32[1024]{0:T(1024)S(1)} %broadcast_clamp_fusion), kind=kCustom, calls=%fused_computation.1 | custom fusion | bytes 8392704 | tf_op jit(solution)/shard_map/jit(_take)/gather | solution.py:53
  37.3 7.7 %multiply_convert_fusion = bf16[4,256,2048]{2,0,1:T(4,128)(2,1)} fusion(bf16[4,256,2048]{2,1,0:T(8,128)(2,1)} %bitcast.46, f32[4,256]{0,1:T(8,128)S(1)} %copy.36, pred[4,256]{0,1:T(8,128)(4,1)S(1)} %copy.37), kind=kLoop, calls=%fused_computation.9 | loop fusion | flops 8388608 | bytes 8393728 | tf_op jit(solution)/shard_map/convert_element_type | solution.py:54
  45.0 5.1 %all-to-all-done.1 = bf16[4,256,768]{2,0,1:T(4,128)(2,1)S(1)} async-done(((bf16[4,256,768]{2,0,1:T(4,128)(2,1)}), bf16[4,256,768]{2,0,1:T(4,128)(2,1)S(1)}, u32[]{:S(2)}, u32[]{:S(2)}) %all-to-all-start.1) | async-done | bytes 1572896 | tf_op jit(solution)/shard_map/all_to_all | solution.py:98
  50.1 4.9 %all-to-all-start = ((bf16[4,256,2048]{2,0,1:T(4,128)(2,1)}), bf16[4,256,2048]{2,0,1:T(4,128)(2,1)}, u32[]{:S(2)}, u32[]{:S(2)}) async-start(bf16[4,256,2048]{2,0,1:T(4,128)(2,1)} %multiply_convert_fusion), calls=%async_computation | async-start | bytes 8388608 | tf_op jit(solution)/shard_map/all_to_all | solution.py:99
  55.0 0.2 copy.43
  55.3 46.7 %all-to-all-done = bf16[4,256,2048]{2,0,1:T(4,128)(2,1)} async-done(((bf16[4,256,2048]{2,0,1:T(4,128)(2,1)}), bf16[4,256,2048]{2,0,1:T(4,128)(2,1)}, u32[]{:S(2)}, u32[]{:S(2)}) %all-to-all-start) | async-done | bytes 4194336 | tf_op jit(solution)/shard_map/all_to_all | solution.py:99
  101.9 6.4 %copy.42 = bf16[4,256,2048]{2,1,0:T(8,128)(2,1)} copy(bf16[4,256,2048]{2,0,1:T(4,128)(2,1)} %all-to-all-done) | data formatting | bytes 8388608 | tf_op jit(solution)/shard_map/while | solution.py:113
  108.3 34.6 %while.13 = (s32[]{:T(128)}, bf16[8,1024,768]{2,1,0:T(8,128)(2,1)}, s32[8]{0:T(128)S(1)}, bf16[4,256,2048]{2,1,0:T(8,128)(2,1)}, bf16[4,256,768]{2,1,0:T(8,128)(...) while((s32[]{:T(128)}, bf16[8,1024,768]{2,1,0:T(8,128)(2,1)}, ...), condition=%wide.region_6.7_spmd, body=%wide.region_5.6_spmd.sunk | while | flops 402653216 | bytes 4064208 | solution.py:113
  108.3 0.6 dynamic_slice.48
  109.6 3.0 bitcast_dynamic-update-slice_fusion.2
  112.7 0.6 dynamic_slice.48
  114.0 3.0 bitcast_dynamic-update-slice_fusion.2
  117.0 0.6 dynamic_slice.48
  118.2 3.0 bitcast_dynamic-update-slice_fusion.2
  121.3 0.6 dynamic_slice.48
  122.6 3.0 bitcast_dynamic-update-slice_fusion.2
  125.6 0.6 dynamic_slice.48
  126.9 3.0 bitcast_dynamic-update-slice_fusion.2
  129.9 0.6 dynamic_slice.48
  131.2 3.1 bitcast_dynamic-update-slice_fusion.2
  134.3 0.6 dynamic_slice.48
  135.6 3.1 bitcast_dynamic-update-slice_fusion.2
  138.6 0.6 dynamic_slice.48
  139.9 3.0 bitcast_dynamic-update-slice_fusion.2
  142.9 129.6 %reduce-scatter.2.cloned.1.call-done = bf16[1024,768]{1,0:T(8,128)(2,1)} async-done(((bf16[8192,768]{1,0:T(8,128)(2,1)}), bf16[1024,768]{1,0:T(8,128)(2,1)}) %reduce-scatter.2.cloned.1.call-update) | async-done | bytes 1572880 | tf_op jit(solution)/shard_map/reduce_scatter | solution.py:116
  272.6 5.3 %fusion.19 = (bf16[1024,768]{1,0:T(8,128)(2,1)}, f32[1024,768]{1,0:T(8,128)}, f32[1024,768]{1,0:T(8,128)}) fusion(bf16[1024,768]{1,0:T(8,128)(2,1)} %reduce-scatter.2.cloned.1.call-done, f32[1024,768]{1,0:T(8,128)S(1)} %copy-done.5), kind=kLoop, calls=%fused_computation.67 | loop fusion | flops 4718592 | bytes 12582912 | tf_op jit(solution)/shard_map/convert_element_type | solution.py:128
  277.9 3.7 %collective-permute-done = bf16[1024,768]{1,0:T(8,128)(2,1)} collective-permute-done((bf16[1024,768]{1,0:T(8,128)(2,1)}, bf16[1024,768]{1,0:T(8,128)(2,1)}, u32[]{:S(2)}, u32[]{:S(2)}) %collective-permute-start) | collective-permute-done | bytes 1572896 | tf_op jit(solution)/shard_map/ppermute | solution.py:26
  281.6 1.6 convert_element_type.74
  283.3 2.2 multiply_reduce_fusion
  286.2 3.7 %divide_convert_fusion = bf16[2048,768]{1,0:T(8,128)(2,1)S(1)} fusion(f32[1024,768]{1,0:T(8,128)} %get-tuple-element.121, f32[1024,768]{1,0:T(8,128)S(1)} %convert_element_type.74, f32[]{:T(128)S(6)} %add.161, pred[]{:T(512)S(6)} %eq.46), kind=kLoop, calls=%fused_computation.12 | loop fusion | flops 7864320 | bytes 9437189 | tf_op jit(solution)/shard_map/convert_element_type | solution.py:134
  290.0 1.7 copy-done.4
  291.6 3.8 %convolution_convert_fusion.1 = bf16[768,768]{1,0:T(8,128)(2,1)} fusion(bf16[2048,768]{1,0:T(8,128)(2,1)S(1)} %divide_convert_fusion), kind=kOutput, calls=%fused_computation.25 | convolution fusion | flops 2416508928 | bytes 4325376 | tf_op jit(solution)/shard_map/dot_general | solution.py:66
  295.4 7.6 %add_convert_fusion = bf16[2048,768]{1,0:T(8,128)(2,1)S(1)} fusion(bf16[2048,768]{1,0:T(8,128)(2,1)} %copy-done.4, bf16[768,768]{1,0:T(8,128)(2,1)} %convolution_convert_fusion.1), kind=kOutput, calls=%fused_computation.11 | convolution fusion | flops 3331129344 | bytes 7471104 | tf_op jit(solution)/shard_map/dot_general | solution.py:61
  303.0 1.7 copy-done.6
  304.7 3.7 %convolution_convert_fusion = bf16[768,768]{1,0:T(8,128)(2,1)} fusion(bf16[2048,768]{1,0:T(8,128)(2,1)S(1)} %add_convert_fusion), kind=kOutput, calls=%fused_computation.24 | convolution fusion | flops 2416508928 | bytes 4325376 | tf_op jit(solution)/shard_map/dot_general | solution.py:66
  308.4 9.2 %fusion.7 = f32[2048,768]{1,0:T(8,128)} fusion(bf16[2048,768]{1,0:T(8,128)(2,1)} %copy-done.6, bf16[768,768]{1,0:T(8,128)(2,1)} %convolution_convert_fusion), kind=kOutput, calls=%fused_computation.26 | convolution fusion | flops 3324837888 | bytes 10616832 | tf_op jit(solution)/shard_map/dot_general | solution.py:61
  317.6 4.0 %multiply_convert_fusion.1 = bf16[1024,768]{1,0:T(8,128)(2,1)} fusion(f32[2048,768]{1,0:T(8,128)} %fusion.7, s32[]{:T(128)S(6)} %select_n.153, bf16[2048,768]{1,0:T(8,128)(2,1)} %copy-done.6), kind=kLoop, calls=%fused_computation.19 | loop fusion | flops 5505024 | bytes 6291460 | tf_op jit(solution)/shard_map/convert_element_type | solution.py:139
  (40 shorter events, 0.9 us)
Async XLA Ops:
  7.2 10.2 %copy-start = (bf16[64,8,768]{2,1,0:T(8,128)(2,1)S(1)}, bf16[64,8,768]{2,1,0:T(8,128)(2,1)}, u32[]{:S(2)}) copy-start(bf16[64,8,768]{2,1,0:T(8,128)(2,1)} %param.7) | copy-start | bytes 2359300
  21.4 9.8 %copy-start.2 = (bf16[64,2048]{1,0:T(8,128)(2,1)S(1)}, bf16[64,2048]{1,0:T(8,128)(2,1)}, u32[]{:S(2)}) copy-start(bf16[64,2048]{1,0:T(8,128)(2,1)} %param.8) | copy-start | bytes 786436
  25.7 24.4 %all-to-all-start.1 = ((bf16[4,256,768]{2,0,1:T(4,128)(2,1)}), bf16[4,256,768]{2,0,1:T(4,128)(2,1)S(1)}, u32[]{:S(2)}, u32[]{:S(2)}) async-start(bf16[4,256,768]{2,0,1:T(4,128)(2,1)} %fusion.6), calls=%async_computation.1 | async-start | bytes 3145728 | tf_op jit(solution)/shard_map/all_to_all | solution.py:98
  50.1 51.8 %all-to-all-start = ((bf16[4,256,2048]{2,0,1:T(4,128)(2,1)}), bf16[4,256,2048]{2,0,1:T(4,128)(2,1)}, u32[]{:S(2)}, u32[]{:S(2)}) async-start(bf16[4,256,2048]{2,0,1:T(4,128)(2,1)} %multiply_convert_fusion), calls=%async_computation | async-start | bytes 8388608 | tf_op jit(solution)/shard_map/all_to_all | solution.py:99
  55.0 217.6 %reduce-scatter.2.cloned.1.call-start = ((), (), s32[]{:S(2)}) async-start(), calls=%async_computation.3 | async-start | bytes 14155776 | tf_op jit(solution)/shard_map/reduce_scatter | solution.py:116
  142.9 129.7 %copy-start.5 = (f32[1024,768]{1,0:T(8,128)S(1)}, f32[1024,768]{1,0:T(8,128)}, u32[]{:S(2)}) copy-start(f32[1024,768]{1,0:T(8,128)} %param.11) | copy-start | bytes 9437188
  277.9 3.8 %collective-permute-start = (bf16[1024,768]{1,0:T(8,128)(2,1)}, bf16[1024,768]{1,0:T(8,128)(2,1)}, u32[]{:S(2)}, u32[]{:S(2)}) collective-permute-start(bf16[1024,768]{1,0:T(8,128)(2,1)} %get-tuple-element.120), channel_id=1, source_target_pairs={{0,4},{4,0},{8,12},{12,8},{16,20},{20,16},{24,28},{28,24},{1,5},{5... | collective-permute-start | bytes 4718600 | tf_op jit(solution)/shard_map/ppermute | solution.py:26
  277.9 5.4 %copy-start.3 = (f32[1024,768]{1,0:T(8,128)S(1)}, f32[1024,768]{1,0:T(8,128)}, u32[]{:S(2)}) copy-start(f32[1024,768]{1,0:T(8,128)} %get-tuple-element.121) | copy-start | bytes 9437188
  289.9 1.7 copy-start.4
  303.0 1.7 copy-start.6
  308.4 13.2 %copy-start.1 = (bf16[64,8,768]{2,1,0:T(8,128)(2,1)S(1)}, bf16[64,8,768]{2,1,0:T(8,128)(2,1)}, u32[]{:S(2)}) copy-start(bf16[64,8,768]{2,1,0:T(8,128)(2,1)} %param.7) | copy-start | bytes 2359300
Sparse Core Ops, SparseCore 0:
  143.1 129.4 reduce-scatter.1
where the time goes:
time: 329 us; the launch traced here: 328 us
  waiting for transfers between devices  185 us (56%)
  matrix products  48.6 us (15%)
  local copies, waits for them, and re-layouts  33.6 us (10%)
  other arithmetic  30.4 us (9%)
  between operations  15 us (5%)
  starting transfers between devices  10.1 us (3%)
  loops' own time  5.54 us (2%)
    reduce_scatter x1, waiting for transfers between devices, body(): lax.psum_scatter(blocks.reshape(own_rows * lax.axis_size('dp'), hidden_wi...  130 us
    all_to_all x1, waiting for transfers between devices, body(): lax.all_to_all(weighted_send, 'expert', split_axis=1, concat_axis=1, tile...  46.7 us
    dot_general x8, matrix products, block_rows(): lax.dot_general(columns, hidden_expert, (((0,), (0,)), ((), ())), preferr...  24.4 us
    dot_general x2, matrix products, newton_update(): product = jnp.dot(scaled, poly, preferred_element_type=jnp.float32)  16.8 us
    convert_element_type x1, other arithmetic, pack_slots(): weighted = (scales[..., None] * grad_rows).astype(jnp.bfloat16)  7.75 us
    dot_general x2, matrix products, gram_of(): lax.dot_general(scaled, scaled, (((0,), (0,)), ((), ())), preferred_eleme...  7.43 us
    gather x2, local copies, waits for them, and re-layouts, pack_slots(): jnp.take(gate_block.reshape(-1), source)  6.87 us
    while x2, local copies, waits for them, and re-layouts, body(): lax.map(block_rows, jnp.arange(own_rows * lax.axis_size('dp') // own_rows...  6.63 us
  transfers between devices with their start and end apart: 4, of which 4 were waited for; matrix products, arithmetic and copies ran while one was open for 4% of the time, Pallas kernels for 0%

commit v1 on v0

v1 whole, which is shorter than its diff:
```python
import math

import jax
import jax.numpy as jnp
import numpy as np
from jax import lax
from jax.sharding import Mesh
from jax.sharding import PartitionSpec as P

EXP_DEV = 4
NS_ITERS = 2


MOMENT = 0.95
COEFF_A = 3.4445
COEFF_B = -4.775
COEFF_C = 2.0315
EPSILON = 1e-07


def newton_update(scaled, gram):
    square = jnp.dot(gram, gram, preferred_element_type=jnp.float32)
    poly = (COEFF_B * gram.astype(jnp.float32) + COEFF_C * square).astype(jnp.bfloat16)
    product = jnp.dot(scaled, poly, preferred_element_type=jnp.float32)
    return (COEFF_A * scaled.astype(jnp.float32) + product).astype(jnp.bfloat16)


def gram_of(scaled):
    return lax.dot_general(
        scaled, scaled, (((0,), (0,)), ((), ())), preferred_element_type=jnp.float32
    )


def body(activations, out_grad, gate_weights, routes, momentum):
    expert_count = lax.axis_size("expert")
    zlo_count = lax.axis_size("zlo")
    zhi_count = lax.axis_size("zhi")
    z_count = zhi_count * zlo_count
    tokens_here, slots_token, hidden_width = activations.shape
    model_width = out_grad.shape[1]
    own_rows = momentum.shape[0]
    expert_total = EXP_DEV * expert_count
    half_blocks = model_width // (2 * own_rows)

    numbers = jnp.arange(expert_total, dtype=jnp.int32)
    matched = routes[:, :, None] == numbers[None, None, :]
    flat_hidden = activations.reshape(tokens_here * slots_token, hidden_width)
    eye = (
        jnp.arange(tokens_here, dtype=jnp.int32)[:, None, None]
        == jnp.arange(tokens_here, dtype=jnp.int32)[None, :, None]
    )
    selector = (matched.transpose(2, 0, 1)[:, :, None, :] & eye[None]).astype(jnp.bfloat16)
    selector = selector.reshape(expert_total * tokens_here, tokens_here * slots_token)
    chosen = jnp.dot(selector, flat_hidden, preferred_element_type=jnp.float32)
    scale = jnp.sum(jnp.where(matched, gate_weights[:, :, None], 0.0), axis=1)
    scale = scale.T.reshape(expert_total * tokens_here, 1)
    scaled_hidden = (scale * chosen).astype(jnp.bfloat16)
    scaled_hidden = scaled_hidden.reshape(expert_count, EXP_DEV, tokens_here, hidden_width)
    scaled_hidden = scaled_hidden.transpose(1, 0, 2, 3)
    got_hidden = lax.all_to_all(scaled_hidden, "expert", split_axis=1, concat_axis=1, tiled=True)
    got_hidden = lax.all_gather(got_hidden, "core", axis=1, tiled=False)
    got_hidden = got_hidden.reshape(EXP_DEV, 2 * expert_count * tokens_here, hidden_width)

    grad_parts = out_grad.reshape(tokens_here, half_blocks, 2, own_rows)
    grad_mine = lax.all_to_all(grad_parts, "core", split_axis=2, concat_axis=2, tiled=True)
    grad_mine = grad_mine.transpose(2, 0, 1, 3).reshape(2, tokens_here, half_blocks * own_rows)
    grad_all = lax.all_gather(grad_mine, "expert", axis=1, tiled=False)
    grad_all = grad_all.reshape(2 * expert_count * tokens_here, half_blocks * own_rows)

    partial = jnp.einsum(
        "td,etf->edf", grad_all, got_hidden, preferred_element_type=jnp.float32
    ).astype(jnp.bfloat16)
    partial = partial.reshape(z_count * own_rows, hidden_width)
    gradient = lax.psum_scatter(
        partial, ("zhi", "zlo"), scatter_dimension=0, tiled=True
    ).astype(jnp.float32)

    new_momentum = MOMENT * momentum + gradient
    ahead = gradient + MOMENT * new_momentum
    group = ("zlo", "core")
    member = lax.axis_index("zlo") * 2 + lax.axis_index("core")
    square_sum = lax.psum(jnp.sum(ahead * ahead), group)
    norm_value = jnp.sqrt(square_sum)
    scaled = (ahead / (norm_value + EPSILON)).astype(jnp.bfloat16)
    scaled_whole = lax.all_gather(scaled, group, axis=0, tiled=True)
    for turn_index in range(NS_ITERS):
        gram = gram_of(scaled_whole).astype(jnp.bfloat16)
        scaled_whole = newton_update(scaled_whole, gram)
    scaled = lax.dynamic_slice_in_dim(scaled_whole, member * own_rows, own_rows, 0)
    update = (math.sqrt(model_width) * scaled.astype(jnp.float32)).astype(jnp.bfloat16)
    return (update, new_momentum)


def solution(mesh):
    dp_count = mesh.shape["dp"]
    expert_count = mesh.shape["expert"]
    group_size = dp_count // EXP_DEV
    zlo = group_size // 2
    zhi = dp_count // 2 // zlo
    devices = np.asarray(mesh.devices).reshape(zhi, zlo, 2, expert_count)
    fine = Mesh(devices, ("zhi", "zlo", "core", "expert"))
    rows = ("zhi", "zlo", "core", "expert")
    cols = ("expert", "zhi", "zlo", "core")
    in_specs = (
        P(rows, None, None),
        P(rows, None),
        P(rows, None),
        P(rows, None),
        P(cols, None),
    )
    out_specs = (P(cols, None), P(cols, None))
    return jax.shard_map(body, mesh=fine, in_specs=in_specs, out_specs=out_specs, check_vma=False)
```

time: 329 us -> 259 us (0.79)
  waiting for transfers between devices: 185 us -> 140 us
  blocking collectives: 0 us -> 39.7 us
  local copies, waits for them, and re-layouts: 33.6 us -> 12.3 us
  other arithmetic: 30.4 us -> 15.1 us
  matrix products: 48.6 us -> 36.6 us
  starting transfers between devices: 10.1 us -> 0.16 us
  loops' own time: 5.54 us -> 0 us
    all_to_all x2 -> x0, waiting for transfers between devices: 51.8 us -> none  [the longest x1 46.7 us: body(): lax.all_to_all(weighted_send, 'expert', split_axis=1, concat_axis=1, tile...]
    all_to_all x0 -> x2, blocking collectives: none -> 36.5 us  [the longest x1 31.8 us: body(): lax.all_to_all(scaled_hidden, 'expert', split_axis=1, concat_axis=1, tile...]
    all_gather x0 -> x3, waiting for transfers between devices: none -> 27.6 us  [the longest x1 13.7 us: body(): got_hidden = lax.all_gather(got_hidden, 'core', axis=1, tiled=False)]
    reduce_scatter x1, waiting for transfers between devices: 130 us -> 112 us  [body(): lax.psum_scatter(partial, ('zhi', 'zlo'), scatter_dimension=0, tiled=True)]
    gather x4 -> x0, local copies, waits for them, and re-layouts: 16.9 us -> none  [the longest x2 6.87 us: pack_slots(): jnp.take(gate_block.reshape(-1), source)]
    dot_general x8 -> x2, matrix products: 24.4 us -> 9.32 us  [the longest x1 8.28 us: body(): jnp.einsum('td,etf->edf', grad_all, got_hidden, preferred_element_type=jn...]
    convert_element_type x4 -> x1, other arithmetic: 18.4 us -> 3.49 us  [body(): scaled = (ahead / (norm_value + EPSILON)).astype(jnp.bfloat16)]
    all_to_all x2 -> x0, starting transfers between devices: 10.1 us -> none  [the longest x1 5.19 us: body(): lax.all_to_all(hidden_send, 'expert', split_axis=1, concat_axis=1, tiled=...]
  transfers between devices with their start and end apart: 4 -> 4, of which waited for: 4 -> 4; matrix products, arithmetic and copies ran while one was open for 4% -> 2% of each run, Pallas kernels for 0% -> 0%
where the time goes in v1:
time: 259 us; the launch traced here: 258 us
  waiting for transfers between devices  140 us (54%)
  blocking collectives  39.7 us (15%)
  matrix products  36.6 us (14%)
  other arithmetic  15.1 us (6%)
  between operations  14.5 us (6%)
  local copies, waits for them, and re-layouts  12.3 us (5%)
    reduce_scatter x1, waiting for transfers between devices, body(): lax.psum_scatter(partial, ('zhi', 'zlo'), scatter_dimension=0, tiled=True)  112 us
    all_to_all x1, blocking collectives, body(): lax.all_to_all(scaled_hidden, 'expert', split_axis=1, concat_axis=1, tile...  31.8 us
    dot_general x2, matrix products, newton_update(): product = jnp.dot(scaled, poly, preferred_element_type=jnp.float32)  16.3 us
    all_gather x1, waiting for transfers between devices, body(): got_hidden = lax.all_gather(got_hidden, 'core', axis=1, tiled=False)  13.7 us
    all_gather x1, waiting for transfers between devices, body(): scaled_whole = lax.all_gather(scaled, group, axis=0, tiled=True)  12.8 us
    dot_general x2, matrix products, gram_of(): lax.dot_general(scaled, scaled, (((0,), (0,)), ((), ())), preferred_eleme...  11 us
    convert_element_type x1, local copies, waits for them, and re-layouts, body(): partial = jnp.einsum('td,etf->edf', grad_all, got_hidden, preferred_eleme...  8.63 us
    dot_general x1, matrix products, body(): jnp.einsum('td,etf->edf', grad_all, got_hidden, preferred_element_type=jn...  8.28 us
  transfers between devices with their start and end apart: 4, of which 4 were waited for; matrix products, arithmetic and copies ran while one was open for 2% of the time, Pallas kernels for 0%

profile of v1, /device:TPU:0, one launch (start us, length us, event | category | flops | bytes accessed | tf_op | source)
XLA Modules:
  0.0 258.2 jit_solution(16073134028554162212)
XLA Ops:
  7.2 0.0 copy-start
  7.2 0.0 all-gather.10.cloned.1.call-start
  7.2 1.2 reshape.59
  8.5 4.7 %all_to_all.10 = bf16[64,1,2,1024]{3,0,1,2:T(8,128)(2,1)} all-to-all(bf16[64,1,2,1024]{3,0,1,2:T(8,128)(2,1)S(1)} %copy.27), channel_id=1, replica_groups=mesh['zhi'=4,'zlo'=1,'core'=2,'expert'=4] {'core'}, dimensions={2} | all-to-all | bytes 524288 | tf_op jit(solution)/shard_map/all_to_all | solution.py:65
  13.2 0.0 all-gather.10.cloned.1.call-update
  13.2 0.0 all-gather.8.cloned.1.call-start
  13.2 0.7 iota_compare_fusion
  14.0 0.6 broadcast_and_fusion
  14.6 0.7 select_reduce_fusion
  15.3 0.1 mul.47
  15.4 2.3 and.28
  17.7 0.0 copy-done
  17.7 1.0 multiply_convert_fusion.1
  18.8 31.8 %all_to_all.11 = bf16[4,4,64,768]{3,2,0,1:T(8,128)(2,1)} all-to-all(bf16[4,4,64,768]{3,2,0,1:T(8,128)(2,1)S(1)} %bitcast.45), channel_id=1, replica_groups=mesh['zhi'=4,'zlo'=1,'core'=2,'expert'=4] {'expert'}, dimensions={1} | all-to-all | bytes 3145728 | tf_op jit(solution)/shard_map/all_to_all | solution.py:60
  50.6 0.0 all-gather.8.cloned.1.call-update
  50.6 0.0 reduce-scatter.2.cloned.1.call-start
  50.7 1.2 all-gather.10.cloned.1.call-done
  51.8 13.7 %all-gather.8.cloned.1.call-done = bf16[4,8,64,768]{3,2,0,1:T(8,128)(2,1)} async-done(((bf16[4,4,64,768]{3,2,0,1:T(8,128)(2,1)}), bf16[4,8,64,768]{3,2,0,1:T(8,128)(2,1)}) %all-gather.8.cloned.1.call-update) | async-done | bytes 3145744 | tf_op jit(solution)/shard_map/all_gather | solution.py:61
  65.5 8.3 %fusion = bf16[4,1024,768]{1,2,0:T(8,128)(2,1)} fusion(bf16[4,2,4,64,768]{4,3,0,2,1:T(8,128)(2,1)} %bitcast.48, bf16[2,4,64,1024,1]{3,2,4,1,0:T(8,128)(2,1)} %bitcast.49), kind=kOutput, calls=%fused_computation.1 | convolution fusion | flops 3224371200 | bytes 10485760 | tf_op jit(solution)/shard_map/td,etf->edf/dot_general | solution.py:70
  73.8 8.6 %copy.29 = bf16[4,1024,768]{2,1,0:T(8,128)(2,1)} copy(bf16[4,1024,768]{1,2,0:T(8,128)(2,1)} %fusion) | data formatting | bytes 12582912 | tf_op jit(solution)/shard_map/convert_element_type | solution.py:72
  82.4 0.0 reduce-scatter.2.cloned.1.call-update
  82.5 0.0 all-gather.6.cloned.1.call-start
  82.5 112.1 %reduce-scatter.2.cloned.1.call-done = bf16[1024,768]{1,0:T(8,128)(2,1)} async-done(((bf16[4096,768]{1,0:T(8,128)(2,1)}), bf16[1024,768]{1,0:T(8,128)(2,1)}) %reduce-scatter.2.cloned.1.call-update) | async-done | bytes 1572880 | tf_op jit(solution)/shard_map/reduce_scatter | solution.py:74
  194.6 0.0 copy-start.1
  194.6 5.5 %multiply_reduce_fusion = (f32[]{:T(128)}, f32[1024,768]{1,0:T(8,128)}) fusion(bf16[1024,768]{1,0:T(8,128)(2,1)} %reduce-scatter.2.cloned.1.call-done, f32[1024,768]{1,0:T(8,128)} %param.9), kind=kLoop, calls=%fused_computation.9 | loop fusion | flops 5505023 | bytes 7864324 | tf_op jit(solution)/shard_map/reduce_sum | solution.py:82
  200.1 3.3 %psum.7 = f32[]{:T(128)} all-reduce(f32[]{:T(128)} %get-tuple-element.2), channel_id=1, replica_groups=mesh['zhi'=4,'zlo'=1,'core'=2,'expert'=4] {'zlo','core'}, use_global_device_ids=true, to_apply=%region_3.4 | all-reduce | flops 1 | bytes 8 | tf_op jit(solution)/shard_map/psum | solution.py:82
  204.0 0.0 copy-done.1
  204.0 3.5 %divide_convert_fusion = bf16[1024,768]{1,0:T(8,128)(2,1)} fusion(f32[1024,768]{1,0:T(8,128)} %get-tuple-element.3, bf16[1024,768]{1,0:T(8,128)(2,1)S(1)} %copy-done.1, f32[]{:T(128)S(6)} %add.31), kind=kLoop, calls=%fused_computation.8 | loop fusion | flops 3932160 | bytes 6291460 | tf_op jit(solution)/shard_map/convert_element_type | solution.py:84
  207.5 0.0 all-gather.6.cloned.1.call-update
  207.6 12.8 %all-gather.6.cloned.1.call-done = bf16[2048,768]{1,0:T(8,128)(2,1)} async-done(((bf16[1024,768]{1,0:T(8,128)(2,1)}), bf16[2048,768]{1,0:T(8,128)(2,1)}) %all-gather.6.cloned.1.call-update) | async-done | bytes 3145744 | tf_op jit(solution)/shard_map/all_gather | solution.py:85
  220.3 5.5 %convolution_convert_fusion.1 = bf16[768,768]{1,0:T(8,128)(2,1)S(1)} fusion(bf16[2048,768]{1,0:T(8,128)(2,1)} %all-gather.6.cloned.1.call-done), kind=kOutput, calls=%fused_computation.15 | convolution fusion | flops 2416508928 | bytes 4325376 | tf_op jit(solution)/shard_map/dot_general | solution.py:29
  225.9 8.2 %add_convert_fusion = bf16[2048,768]{1,0:T(8,128)(2,1)} fusion(bf16[2048,768]{1,0:T(8,128)(2,1)} %all-gather.6.cloned.1.call-done, bf16[768,768]{1,0:T(8,128)(2,1)S(1)} %convolution_convert_fusion.1), kind=kOutput, calls=%fused_computation.2 | convolution fusion | flops 3331129344 | bytes 7471104 | tf_op jit(solution)/shard_map/dot_general | solution.py:24
  234.0 5.5 %convolution_convert_fusion = bf16[768,768]{1,0:T(8,128)(2,1)S(1)} fusion(bf16[2048,768]{1,0:T(8,128)(2,1)} %add_convert_fusion), kind=kOutput, calls=%fused_computation.14 | convolution fusion | flops 2416508928 | bytes 4325376 | tf_op jit(solution)/shard_map/dot_general | solution.py:29
  239.5 8.1 %fusion.3 = f32[2048,768]{1,0:T(8,128)} fusion(bf16[2048,768]{1,0:T(8,128)(2,1)} %add_convert_fusion, bf16[768,768]{1,0:T(8,128)(2,1)S(1)} %convolution_convert_fusion), kind=kOutput, calls=%fused_computation.17 | convolution fusion | flops 3324837888 | bytes 10616832 | tf_op jit(solution)/shard_map/dot_general | solution.py:24
  247.6 4.0 %multiply_convert_fusion = bf16[1024,768]{1,0:T(8,128)(2,1)} fusion(f32[2048,768]{1,0:T(8,128)} %fusion.3, s32[]{:T(128)S(6)} %select_n.8, bf16[2048,768]{1,0:T(8,128)(2,1)} %add_convert_fusion), kind=kLoop, calls=%fused_computation.7 | loop fusion | flops 5505024 | bytes 6291460 | tf_op jit(solution)/shard_map/convert_element_type | solution.py:90
  (2 shorter events, 0.1 us)
Async XLA Ops:
  7.2 10.6 %copy-start = (bf16[64,8,768]{2,1,0:T(8,128)(2,1)S(1)}, bf16[64,8,768]{2,1,0:T(8,128)(2,1)}, u32[]{:S(2)}) copy-start(bf16[64,8,768]{2,1,0:T(8,128)(2,1)} %param.5) | copy-start | bytes 2359300
  7.2 44.7 %all-gather.10.cloned.1.call-start = ((), (), s32[]{:S(2)}) async-start(), calls=%async_computation.6 | async-start | bytes 1310720 | tf_op jit(solution)/shard_map/all_gather | solution.py:67
  13.2 52.4 %all-gather.8.cloned.1.call-start = ((), (), s32[]{:S(2)}) async-start(), calls=%async_computation.5 | async-start | bytes 4718592 | tf_op jit(solution)/shard_map/all_gather | solution.py:61
  50.6 144.0 %reduce-scatter.2.cloned.1.call-start = ((), (), s32[]{:S(2)}) async-start(), calls=%async_computation.3 | async-start | bytes 7864320 | tf_op jit(solution)/shard_map/reduce_scatter | solution.py:74
  82.5 137.9 %all-gather.6.cloned.1.call-start = ((), (), s32[]{:S(2)}) async-start(), calls=%async_computation.4 | async-start | bytes 4718592 | tf_op jit(solution)/shard_map/all_gather | solution.py:85
  194.6 9.5 %copy-start.1 = (bf16[1024,768]{1,0:T(8,128)(2,1)S(1)}, bf16[1024,768]{1,0:T(8,128)(2,1)}, u32[]{:S(2)}) copy-start(bf16[1024,768]{1,0:T(8,128)(2,1)} %reduce-scatter.2.cloned.1.call-done) | copy-start | bytes 4718596
Sparse Core Ops, SparseCore 0:
  13.3 38.4 all-gather.9
  53.4 12.1 all-gather.7
  82.6 111.9 reduce-scatter.1
  207.7 12.6 all-gather.5

commit v2 on v1

--- a/solution.py
+++ b/solution.py
@@ -40,7 +40,8 @@
     model_width = out_grad.shape[1]
     own_rows = momentum.shape[0]
     expert_total = EXP_DEV * expert_count
-    half_blocks = model_width // (2 * own_rows)
+    group_size = zlo_count * 2
+    group = ("zlo", "core")
 
     numbers = jnp.arange(expert_total, dtype=jnp.int32)
     matched = routes[:, :, None] == numbers[None, None, :]
@@ -56,28 +57,25 @@
     scale = scale.T.reshape(expert_total * tokens_here, 1)
     scaled_hidden = (scale * chosen).astype(jnp.bfloat16)
     scaled_hidden = scaled_hidden.reshape(expert_count, EXP_DEV, tokens_here, hidden_width)
-    scaled_hidden = scaled_hidden.transpose(1, 0, 2, 3)
-    got_hidden = lax.all_to_all(scaled_hidden, "expert", split_axis=1, concat_axis=1, tiled=True)
-    got_hidden = lax.all_gather(got_hidden, "core", axis=1, tiled=False)
-    got_hidden = got_hidden.reshape(EXP_DEV, 2 * expert_count * tokens_here, hidden_width)
+    scaled_hidden = scaled_hidden.transpose(1, 0, 2, 3).reshape(expert_total, tokens_here, hidden_width)
+    got_hidden = lax.all_to_all(
+        scaled_hidden, ("zhi", "expert"), split_axis=0, concat_axis=0, tiled=True
+    )
+    got_hidden = lax.all_gather(got_hidden, group, axis=1, tiled=False)
+    got_hidden = got_hidden.reshape(-1, hidden_width)
 
-    grad_parts = out_grad.reshape(tokens_here, half_blocks, 2, own_rows)
-    grad_mine = lax.all_to_all(grad_parts, "core", split_axis=2, concat_axis=2, tiled=True)
-    grad_mine = grad_mine.transpose(2, 0, 1, 3).reshape(2, tokens_here, half_blocks * own_rows)
-    grad_all = lax.all_gather(grad_mine, "expert", axis=1, tiled=False)
-    grad_all = grad_all.reshape(2 * expert_count * tokens_here, half_blocks * own_rows)
+    grad_parts = out_grad.reshape(tokens_here, group_size, own_rows)
+    grad_mine = lax.all_to_all(grad_parts, group, split_axis=1, concat_axis=1, tiled=True)
+    grad_mine = grad_mine.transpose(1, 0, 2)
+    grad_all = lax.all_gather(grad_mine, ("zhi", "expert"), axis=0, tiled=False)
+    grad_all = grad_all.reshape(-1, own_rows)
 
-    partial = jnp.einsum(
-        "td,etf->edf", grad_all, got_hidden, preferred_element_type=jnp.float32
-    ).astype(jnp.bfloat16)
-    partial = partial.reshape(z_count * own_rows, hidden_width)
-    gradient = lax.psum_scatter(
-        partial, ("zhi", "zlo"), scatter_dimension=0, tiled=True
-    ).astype(jnp.float32)
+    gradient = lax.dot_general(
+        grad_all, got_hidden, (((0,), (0,)), ((), ())), preferred_element_type=jnp.float32
+    )
 
     new_momentum = MOMENT * momentum + gradient
     ahead = gradient + MOMENT * new_momentum
-    group = ("zlo", "core")
     member = lax.axis_index("zlo") * 2 + lax.axis_index("core")
     square_sum = lax.psum(jnp.sum(ahead * ahead), group)
     norm_value = jnp.sqrt(square_sum)

time: 259 us -> 220 us (0.85)
  waiting for transfers between devices: 140 us -> 88.6 us
  blocking collectives: 39.7 us -> 53.7 us
  other arithmetic: 15.1 us -> 11.3 us
  matrix products: 36.6 us -> 39.8 us
    reduce_scatter x1 -> x0, waiting for transfers between devices: 112 us -> none  [body(): lax.psum_scatter(partial, ('zhi', 'zlo'), scatter_dimension=0, tiled=True)]
    all_gather x2, waiting for transfers between devices: 14.9 us -> 81.4 us  [the longest x1 79.6 us: body(): grad_all = lax.all_gather(grad_mine, ('zhi', 'expert'), axis=0, tiled=False)]
    all_to_all x2, blocking collectives: 36.5 us -> 50.6 us  [the longest x1 45.9 us: body(): lax.all_to_all(scaled_hidden, ('zhi', 'expert'), split_axis=0, concat_axi...]
    unnamed x4 -> x7, local copies, waits for them, and re-layouts: 0.01 us -> 9.26 us
    convert_element_type x1 -> x0, local copies, waits for them, and re-layouts: 8.63 us -> none  [body(): partial = jnp.einsum('td,etf->edf', grad_all, got_hidden, preferred_eleme...]
    add x0 -> x1, other arithmetic: none -> 6.23 us  [body(): new_momentum = MOMENT * momentum + gradient]
    all_gather x1, waiting for transfers between devices: 12.8 us -> 7.14 us  [body(): scaled_whole = lax.all_gather(scaled, group, axis=0, tiled=True)]
    reduce_sum x1 -> x0, other arithmetic: 5.5 us -> none  [body(): square_sum = lax.psum(jnp.sum(ahead * ahead), group)]
  transfers between devices with their start and end apart: 4 -> 3, of which waited for: 4 -> 3; matrix products, arithmetic and copies ran while one was open for 2% -> 4% of each run, Pallas kernels for 0% -> 0%
where the time goes in v2:
time: 220 us
  waiting for transfers between devices  88.6 us (40%)
  blocking collectives  53.7 us (24%)
  matrix products  39.8 us (18%)
  between operations  14.5 us (7%)
  local copies, waits for them, and re-layouts  11.8 us (5%)
  other arithmetic  11.3 us (5%)
    all_gather x1, waiting for transfers between devices, body(): grad_all = lax.all_gather(grad_mine, ('zhi', 'expert'), axis=0, tiled=False)  79.6 us
    all_to_all x1, blocking collectives, body(): lax.all_to_all(scaled_hidden, ('zhi', 'expert'), split_axis=0, concat_axi...  45.9 us
    dot_general x2, matrix products, newton_update(): product = jnp.dot(scaled, poly, preferred_element_type=jnp.float32)  17.7 us
    dot_general x2, matrix products, gram_of(): lax.dot_general(scaled, scaled, (((0,), (0,)), ((), ())), preferred_eleme...  11 us
    dot_general x1, matrix products, body(): lax.dot_general(grad_all, got_hidden, (((0,), (0,)), ((), ())), preferred...  10.1 us
    unnamed x7, local copies, waits for them, and re-layouts  9.26 us
    all_gather x1, waiting for transfers between devices, body(): scaled_whole = lax.all_gather(scaled, group, axis=0, tiled=True)  7.14 us
    add x1, other arithmetic, body(): new_momentum = MOMENT * momentum + gradient  6.23 us
  transfers between devices with their start and end apart: 3, of which 3 were waited for; matrix products, arithmetic and copies ran while one was open for 4% of the time, Pallas kernels for 0%

profile of v2, /device:TPU:0, one launch (start us, length us, event | category | flops | bytes accessed | tf_op | source)
XLA Modules:
  0.0 219.8 jit_solution(16698243984189065966)
XLA Ops:
  7.2 0.0 copy-start
  7.2 0.0 all-gather.8.cloned.1.call-start
  7.2 0.8 iota_compare_fusion
  8.0 0.7 select_reduce_fusion
  8.7 0.1 mul.47
  8.8 0.6 broadcast_and_fusion
  9.4 2.4 %and.28 = pred[1024,512]{0,1:T(32,128)(4,1)S(1)} reshape(pred[16,64,64,8]{1,0,3,2:T(8,128)(4,1)S(1)} %broadcast_and_fusion) | data formatting | bytes 1048576 | tf_op jit(solution)/shard_map/and | solution.py:53
  11.8 0.0 copy-done
  11.8 1.0 multiply_convert_fusion.1
  12.8 0.1 copy.51
  13.0 0.0 copy-start.1
  13.0 45.9 %all_to_all.10 = bf16[16,64,768]{2,1,0:T(8,128)(2,1)} all-to-all(bf16[16,64,768]{2,1,0:T(8,128)(2,1)S(1)} %bitcast.47), channel_id=1, replica_groups=mesh['zhi'=4,'zlo'=1,'core'=2,'expert'=4] {'zhi','expert'}, dimensions={0} | all-to-all | bytes 3145728 | tf_op jit(solution)/shard_map/all_to_all | solution.py:61
  58.9 0.0 all-gather.8.cloned.1.call-update
  59.0 0.0 all-gather.10.cloned.1.call-start
  59.0 0.0 copy-done.1
  59.1 4.7 %all_to_all.11 = bf16[64,2,1024]{2,0,1:T(8,128)(2,1)} all-to-all(bf16[64,2,1024]{2,0,1:T(8,128)(2,1)S(1)} %bitcast.52), channel_id=1, replica_groups=mesh['zhi'=4,'zlo'=1,'core'=2,'expert'=4] {'zlo','core'}, dimensions={1} | all-to-all | bytes 524288 | tf_op jit(solution)/shard_map/all_to_all | solution.py:68
  63.7 0.0 all-gather.10.cloned.1.call-update
  63.7 0.0 all-gather.6.cloned.1.call-start
  63.8 3.9 %copy.53 = f32[1024,768]{0,1:T(8,128)} copy(f32[1024,768]{1,0:T(8,128)} %param.9) | data formatting | bytes 6291456 | tf_op args[4]
  67.7 1.8 all-gather.8.cloned.1.call-done
  69.6 79.6 %all-gather.10.cloned.1.call-done = bf16[32,64,1024]{2,1,0:T(8,128)(2,1)} async-done(((bf16[2,64,1024]{2,1,0:T(8,128)(2,1)}), bf16[32,64,1024]{2,1,0:T(8,128)(2,1)}) %all-gather.10.cloned.1.call-update) | async-done | bytes 4194320 | tf_op jit(solution)/shard_map/all_gather | solution.py:70
  149.1 10.1 %multiply_reduce_fusion = (f32[]{:T(128)}, f32[768,1024,1,1]{1,0,3,2:T(8,128)}) fusion(f32[1024,768]{0,1:T(8,128)} %copy.53, bf16[16,2,64,768]{3,2,1,0:T(8,128)(2,1)} %bitcast.49, bf16[16,2,64,1024]{3,2,1,0:T(8,128)(2,1)} %bitcast.48), kind=kOutput, calls=%fused_computation.7 | convolution fusion | flops 3225944064 | bytes 13631492 | tf_op jit(solution)/shard_map/dot_general | solution.py:73
  159.2 3.1 %psum.7 = f32[]{:T(128)} all-reduce(f32[]{:T(128)} %get-tuple-element.16), channel_id=1, replica_groups=mesh['zhi'=4,'zlo'=1,'core'=2,'expert'=4] {'zlo','core'}, use_global_device_ids=true, to_apply=%region_2.3 | all-reduce | flops 1 | bytes 8 | tf_op jit(solution)/shard_map/psum | solution.py:80
  163.0 6.2 %bitcast_add_fusion.1 = (f32[1024,768]{0,1:T(8,128)}, bf16[1024,768]{0,1:T(8,128)(2,1)}) fusion(f32[768,1024,1,1]{1,0,3,2:T(8,128)} %get-tuple-element.17, f32[1024,768]{0,1:T(8,128)} %copy.53, f32[]{:T(128)S(6)} %add.29), kind=kLoop, calls=%fused_computation.4 | loop fusion | flops 4718592 | bytes 11010052 | tf_op jit(solution)/shard_map/add | solution.py:77
  169.2 0.0 all-gather.6.cloned.1.call-update
  169.3 3.7 %copy.57 = f32[1024,768]{1,0:T(8,128)} copy(f32[1024,768]{0,1:T(8,128)} %get-tuple-element.14) | data formatting | bytes 6291456
  173.0 7.1 %all-gather.6.cloned.1.call-done = bf16[2048,768]{0,1:T(8,128)(2,1)} async-done(((bf16[1024,768]{0,1:T(8,128)(2,1)}), bf16[2048,768]{0,1:T(8,128)(2,1)}) %all-gather.6.cloned.1.call-update) | async-done | bytes 3145744 | tf_op jit(solution)/shard_map/all_gather | solution.py:83
  180.1 5.5 %convolution_convert_fusion.1 = bf16[768,768]{1,0:T(8,128)(2,1)S(1)} fusion(bf16[2048,768]{0,1:T(8,128)(2,1)} %all-gather.6.cloned.1.call-done), kind=kOutput, calls=%fused_computation.13 | convolution fusion | flops 2416508928 | bytes 4325376 | tf_op jit(solution)/shard_map/dot_general | solution.py:29
  185.6 8.5 %add_convert_fusion = bf16[2048,768]{0,1:T(8,128)(2,1)} fusion(bf16[2048,768]{0,1:T(8,128)(2,1)} %all-gather.6.cloned.1.call-done, bf16[768,768]{1,0:T(8,128)(2,1)S(1)} %convolution_convert_fusion.1), kind=kOutput, calls=%fused_computation | convolution fusion | flops 3331129344 | bytes 7471104 | tf_op jit(solution)/shard_map/dot_general | solution.py:24
  194.1 5.5 %convolution_convert_fusion = bf16[768,768]{1,0:T(8,128)(2,1)S(1)} fusion(bf16[2048,768]{0,1:T(8,128)(2,1)} %add_convert_fusion), kind=kOutput, calls=%fused_computation.12 | convolution fusion | flops 2416508928 | bytes 4325376 | tf_op jit(solution)/shard_map/dot_general | solution.py:29
  199.6 9.2 %fusion.2 = f32[2048,768]{0,1:T(8,128)} fusion(bf16[2048,768]{0,1:T(8,128)(2,1)} %add_convert_fusion, bf16[768,768]{1,0:T(8,128)(2,1)S(1)} %convolution_convert_fusion), kind=kOutput, calls=%fused_computation.15 | convolution fusion | flops 3324837888 | bytes 10616832 | tf_op jit(solution)/shard_map/dot_general | solution.py:24
  208.8 3.0 %multiply_convert_fusion = bf16[1024,768]{0,1:T(8,128)(2,1)S(1)} fusion(f32[2048,768]{0,1:T(8,128)} %fusion.2, s32[]{:T(128)S(6)} %select_n.8, bf16[2048,768]{0,1:T(8,128)(2,1)} %add_convert_fusion), kind=kLoop, calls=%fused_computation.5 | loop fusion | flops 5505024 | bytes 6291460 | tf_op jit(solution)/shard_map/convert_element_type | solution.py:88
  211.7 1.6 copy.56
  (2 shorter events, 0.0 us)
Async XLA Ops:
  7.2 4.6 %copy-start = (bf16[64,8,768]{2,1,0:T(8,128)(2,1)S(1)}, bf16[64,8,768]{2,1,0:T(8,128)(2,1)}, u32[]{:S(2)}) copy-start(bf16[64,8,768]{2,1,0:T(8,128)(2,1)} %param.5) | copy-start | bytes 2359300
  7.2 62.4 %all-gather.8.cloned.1.call-start = ((), (), s32[]{:S(2)}) async-start(), calls=%async_computation.3 | async-start | bytes 4718592 | tf_op jit(solution)/shard_map/all_gather | solution.py:64
  13.0 46.0 %copy-start.1 = (bf16[64,2048]{1,0:T(8,128)(2,1)S(1)}, bf16[64,2048]{1,0:T(8,128)(2,1)}, u32[]{:S(2)}) copy-start(bf16[64,2048]{1,0:T(8,128)(2,1)} %param.6) | copy-start | bytes 786436
  59.0 90.2 %all-gather.10.cloned.1.call-start = ((), (), s32[]{:S(2)}) async-start(), calls=%async_computation.4 | async-start | bytes 4456448 | tf_op jit(solution)/shard_map/all_gather | solution.py:70
  63.7 116.4 %all-gather.6.cloned.1.call-start = ((), (), s32[]{:S(2)}) async-start(), calls=%async_computation.2 | async-start | bytes 4718592 | tf_op jit(solution)/shard_map/all_gather | solution.py:83
Sparse Core Ops, SparseCore 0:
  59.1 10.4 all-gather.7
  72.3 76.7 all-gather.9
  169.4 10.7 all-gather.5

commit v3 on v2

--- a/solution.py
+++ b/solution.py
@@ -31,6 +31,17 @@
     )
 
 
+def group_gather(block, axes, count):
+    member = lax.axis_index(axes)
+    parts = [block]
+    for shift in range(1, count):
+        route = [(source, (source + shift) % count) for source in range(count)]
+        parts.append(lax.ppermute(block, axes, route))
+    stacked = jnp.stack(parts)
+    order = (member - jnp.arange(count, dtype=jnp.int32)) % count
+    return jnp.take(stacked, order, axis=0)
+
+
 def body(activations, out_grad, gate_weights, routes, momentum):
     expert_count = lax.axis_size("expert")
     zlo_count = lax.axis_size("zlo")
@@ -42,6 +53,13 @@
     expert_total = EXP_DEV * expert_count
     group_size = zlo_count * 2
     group = ("zlo", "core")
+
+    grad_parts = out_grad.reshape(tokens_here, group_size, own_rows)
+    grad_mine = lax.all_to_all(grad_parts, group, split_axis=1, concat_axis=1, tiled=True)
+    grad_mine = grad_mine.transpose(1, 0, 2)
+    grad_mine, activations = lax.optimization_barrier((grad_mine, activations))
+    grad_all = lax.all_gather(grad_mine, ("zhi", "expert"), axis=0, tiled=False)
+    grad_all = grad_all.reshape(-1, own_rows)
 
     numbers = jnp.arange(expert_total, dtype=jnp.int32)
     matched = routes[:, :, None] == numbers[None, None, :]
@@ -61,14 +79,8 @@
     got_hidden = lax.all_to_all(
         scaled_hidden, ("zhi", "expert"), split_axis=0, concat_axis=0, tiled=True
     )
-    got_hidden = lax.all_gather(got_hidden, group, axis=1, tiled=False)
-    got_hidden = got_hidden.reshape(-1, hidden_width)
-
-    grad_parts = out_grad.reshape(tokens_here, group_size, own_rows)
-    grad_mine = lax.all_to_all(grad_parts, group, split_axis=1, concat_axis=1, tiled=True)
-    grad_mine = grad_mine.transpose(1, 0, 2)
-    grad_all = lax.all_gather(grad_mine, ("zhi", "expert"), axis=0, tiled=False)
-    grad_all = grad_all.reshape(-1, own_rows)
+    got_hidden = group_gather(got_hidden, group, group_size)
+    got_hidden = got_hidden.transpose(1, 0, 2, 3).reshape(-1, hidden_width)
 
     gradient = lax.dot_general(
         grad_all, got_hidden, (((0,), (0,)), ((), ())), preferred_element_type=jnp.float32

time: 220 us -> 175 us (0.80)
  waiting for transfers between devices: 88.6 us -> 29.7 us
  blocking collectives: 53.7 us -> 68.6 us
  local copies, waits for them, and re-layouts: 11.8 us -> 7.92 us
  other arithmetic: 11.3 us -> 13.9 us
    all_gather x1, waiting for transfers between devices: 79.6 us -> 15.3 us  [body(): grad_all = lax.all_gather(grad_mine, ('zhi', 'expert'), axis=0, tiled=False)]
    all_to_all x1, blocking collectives: 45.9 us -> 60.6 us  [body(): lax.all_to_all(scaled_hidden, ('zhi', 'expert'), split_axis=0, concat_axi...]
    unnamed x7 -> x2, local copies, waits for them, and re-layouts: 9.26 us -> 0.01 us
    add x1 -> x0, other arithmetic: 6.23 us -> none  [body(): new_momentum = MOMENT * momentum + gradient]
    convert_element_type x0 -> x1, other arithmetic: none -> 4.43 us  [body(): scaled = (ahead / (norm_value + EPSILON)).astype(jnp.bfloat16)]
    gather x0 -> x1, local copies, waits for them, and re-layouts: none -> 4.31 us  [group_gather(): return jnp.take(stacked, order, axis=0)]
    all_gather x1, waiting for transfers between devices: 7.14 us -> 10.9 us  [body(): scaled_whole = lax.all_gather(scaled, group, axis=0, tiled=True)]
    ppermute x0 -> x1, waiting for transfers between devices: none -> 3.49 us  [group_gather(): parts.append(lax.ppermute(block, axes, route))]
  transfers between devices with their start and end apart: 3 -> 3, of which waited for: 3 -> 3; matrix products, arithmetic and copies ran while one was open for 4% -> 8% of each run, Pallas kernels for 0% -> 0%
where the time goes in v3:
time: 175 us
  blocking collectives  68.6 us (39%)
  matrix products  39.6 us (23%)
  waiting for transfers between devices  29.7 us (17%)
  between operations  14.8 us (8%)
  other arithmetic  13.9 us (8%)
  local copies, waits for them, and re-layouts  7.92 us (5%)
    all_to_all x1, blocking collectives, body(): lax.all_to_all(scaled_hidden, ('zhi', 'expert'), split_axis=0, concat_axi...  60.6 us
    dot_general x2, matrix products, newton_update(): product = jnp.dot(scaled, poly, preferred_element_type=jnp.float32)  16.3 us
    all_gather x1, waiting for transfers between devices, body(): grad_all = lax.all_gather(grad_mine, ('zhi', 'expert'), axis=0, tiled=False)  15.3 us
    dot_general x1, matrix products, body(): lax.dot_general(grad_all, got_hidden, (((0,), (0,)), ((), ())), preferred...  11.3 us
    dot_general x2, matrix products, gram_of(): lax.dot_general(scaled, scaled, (((0,), (0,)), ((), ())), preferred_eleme...  11 us
    all_gather x1, waiting for transfers between devices, body(): scaled_whole = lax.all_gather(scaled, group, axis=0, tiled=True)  10.9 us
    all_to_all x1, blocking collectives, body(): lax.all_to_all(grad_parts, group, split_axis=1, concat_axis=1, tiled=True)  4.67 us
    convert_element_type x1, other arithmetic, body(): scaled = (ahead / (norm_value + EPSILON)).astype(jnp.bfloat16)  4.43 us
  transfers between devices with their start and end apart: 3, of which 3 were waited for; matrix products, arithmetic and copies ran while one was open for 8% of the time, Pallas kernels for 0%

profile of v3, /device:TPU:0, one launch (start us, length us, event | category | flops | bytes accessed | tf_op | source)
XLA Modules:
  0.0 174.6 jit_solution(1805076580215652085)
XLA Ops:
  7.2 0.0 copy-start
  7.2 0.0 all-gather.6.cloned.1.call-start
  7.2 1.0 copy.40
  8.3 4.7 %all_to_all.10 = bf16[64,2,1024]{2,0,1:T(8,128)(2,1)} all-to-all(bf16[64,2,1024]{2,0,1:T(8,128)(2,1)S(1)} %bitcast.52), channel_id=1, replica_groups=mesh['zhi'=4,'zlo'=1,'core'=2,'expert'=4] {'zlo','core'}, dimensions={1} | all-to-all | bytes 524288 | tf_op jit(solution)/shard_map/all_to_all | solution.py:58
  12.9 0.0 all-gather.6.cloned.1.call-update
  13.0 0.0 all-gather.4.cloned.1.call-start
  13.0 0.7 select_reduce_fusion
  13.7 0.1 mul.48
  13.8 0.7 iota_compare_fusion
  14.5 0.6 broadcast_and_fusion
  15.1 2.4 %and.60 = pred[1024,512]{0,1:T(32,128)(4,1)S(1)} reshape(pred[16,64,64,8]{1,0,3,2:T(8,128)(4,1)S(1)} %broadcast_and_fusion) | data formatting | bytes 1048576 | tf_op jit(solution)/shard_map/and | solution.py:71
  17.5 0.0 copy-done
  17.5 1.0 multiply_convert_fusion.1
  18.6 0.1 copy.31
  18.7 60.6 %all_to_all.11 = bf16[16,64,768]{2,1,0:T(8,128)(2,1)S(1)} all-to-all(bf16[16,64,768]{2,1,0:T(8,128)(2,1)S(1)} %bitcast.48), channel_id=1, replica_groups=mesh['zhi'=4,'zlo'=1,'core'=2,'expert'=4] {'zhi','expert'}, dimensions={0} | all-to-all | bytes 3145728 | tf_op jit(solution)/shard_map/all_to_all | solution.py:79
  79.4 0.0 collective-permute-start
  79.4 3.5 %collective-permute-done = bf16[16,64,768]{2,1,0:T(8,128)(2,1)} collective-permute-done((bf16[16,64,768]{2,1,0:T(8,128)(2,1)S(1)}, bf16[16,64,768]{2,1,0:T(8,128)(2,1)}, u32[]{:S(2)}, u32[]{:S(2)}) %collective-permute-start) | collective-permute-done | bytes 1572896 | tf_op jit(solution)/shard_map/ppermute | solution.py:39
  82.9 3.4 %pad_maximum_fusion = bf16[2,16,64,768]{3,2,1,0:T(8,128)(2,1)} fusion(bf16[1,16,64,768]{3,2,1,0:T(8,128)(2,1)} %bitcast.8, bf16[1,16,64,768]{3,2,1,0:T(8,128)(2,1)S(1)} %bitcast.49), kind=kLoop, calls=%fused_computation.4 | loop fusion | flops 1572864 | bytes 6291456 | tf_op jit(solution)/shard_map/stack | solution.py:40
  86.3 4.3 %gather_fusion = bf16[2,16,64,768]{3,2,1,0:T(8,128)(2,1)} fusion(bf16[2,16,64,768]{3,2,1,0:T(8,128)(2,1)} %pad_maximum_fusion, s32[1024]{0:T(1024)S(1)} %pad_clamp_fusion), kind=kCustom, calls=%fused_computation | custom fusion | bytes 6291464 | tf_op jit(solution)/shard_map/jit(_take)/gather | solution.py:42
  90.6 15.3 %all-gather.6.cloned.1.call-done = bf16[32,64,1024]{2,1,0:T(8,128)(2,1)} async-done(((bf16[2,64,1024]{2,1,0:T(8,128)(2,1)}), bf16[32,64,1024]{2,1,0:T(8,128)(2,1)}) %all-gather.6.cloned.1.call-update) | async-done | bytes 4194320 | tf_op jit(solution)/shard_map/all_gather | solution.py:61
  105.9 11.3 %multiply_reduce_fusion = (f32[]{:T(128)}, f32[1024,768]{1,0:T(8,128)}, f32[1024,768,1,1]{1,0,3,2:T(8,128)}) fusion(f32[1024,768]{1,0:T(8,128)} %param.9, bf16[16,2,64,1024]{3,2,1,0:T(8,128)(2,1)} %bitcast.55, bf16[2,16,64,768]{3,2,1,0:T(8,128)(2,1)} %gather_fusion, pred[2]{0:T(512)(128)(4,1)S(1)} %compare_and_fusion), kind=kOutput, calls=%fused_computation.11 | convolution fusion | flops 3227516928 | bytes 16777222 | tf_op jit(solution)/shard_map/dot_general | solution.py:85
  117.2 3.3 %psum.7 = f32[]{:T(128)} all-reduce(f32[]{:T(128)} %get-tuple-element.6), channel_id=1, replica_groups=mesh['zhi'=4,'zlo'=1,'core'=2,'expert'=4] {'zlo','core'}, use_global_device_ids=true, to_apply=%region_2.3 | all-reduce | flops 1 | bytes 8 | tf_op jit(solution)/shard_map/psum | solution.py:92
  121.1 4.4 %divide_convert_fusion = bf16[1024,768]{1,0:T(8,128)(2,1)} fusion(f32[]{:T(128)S(6)} %add.66, f32[1024,768]{1,0:T(8,128)} %get-tuple-element.7, f32[1024,768,1,1]{1,0,3,2:T(8,128)} %get-tuple-element.8), kind=kLoop, calls=%fused_computation.10 | loop fusion | flops 3145728 | bytes 7864324 | tf_op jit(solution)/shard_map/convert_element_type | solution.py:94
  125.6 0.0 all-gather.4.cloned.1.call-update
  125.6 10.9 %all-gather.4.cloned.1.call-done = bf16[2048,768]{1,0:T(8,128)(2,1)} async-done(((bf16[1024,768]{1,0:T(8,128)(2,1)}), bf16[2048,768]{1,0:T(8,128)(2,1)}) %all-gather.4.cloned.1.call-update) | async-done | bytes 3145744 | tf_op jit(solution)/shard_map/all_gather | solution.py:95
  136.5 5.5 %convolution_convert_fusion.1 = bf16[768,768]{1,0:T(8,128)(2,1)S(1)} fusion(bf16[2048,768]{1,0:T(8,128)(2,1)} %all-gather.4.cloned.1.call-done), kind=kOutput, calls=%fused_computation.18 | convolution fusion | flops 2416508928 | bytes 4325376 | tf_op jit(solution)/shard_map/dot_general | solution.py:29
  142.0 8.2 %add_convert_fusion = bf16[2048,768]{1,0:T(8,128)(2,1)} fusion(bf16[2048,768]{1,0:T(8,128)(2,1)} %all-gather.4.cloned.1.call-done, bf16[768,768]{1,0:T(8,128)(2,1)S(1)} %convolution_convert_fusion.1), kind=kOutput, calls=%fused_computation.1 | convolution fusion | flops 3331129344 | bytes 7471104 | tf_op jit(solution)/shard_map/dot_general | solution.py:24
  150.2 5.5 %convolution_convert_fusion = bf16[768,768]{1,0:T(8,128)(2,1)S(1)} fusion(bf16[2048,768]{1,0:T(8,128)(2,1)} %add_convert_fusion), kind=kOutput, calls=%fused_computation.17 | convolution fusion | flops 2416508928 | bytes 4325376 | tf_op jit(solution)/shard_map/dot_general | solution.py:29
  155.7 8.1 %fusion.4 = f32[2048,768]{1,0:T(8,128)} fusion(bf16[2048,768]{1,0:T(8,128)(2,1)} %add_convert_fusion, bf16[768,768]{1,0:T(8,128)(2,1)S(1)} %convolution_convert_fusion), kind=kOutput, calls=%fused_computation.20 | convolution fusion | flops 3324837888 | bytes 10616832 | tf_op jit(solution)/shard_map/dot_general | solution.py:24
  163.8 4.0 %multiply_convert_fusion = bf16[1024,768]{1,0:T(8,128)(2,1)} fusion(f32[2048,768]{1,0:T(8,128)} %fusion.4, s32[]{:T(128)S(6)} %select_n.56, bf16[2048,768]{1,0:T(8,128)(2,1)} %add_convert_fusion), kind=kLoop, calls=%fused_computation.9 | loop fusion | flops 5505024 | bytes 6291460 | tf_op jit(solution)/shard_map/convert_element_type | solution.py:100
  (4 shorter events, 0.0 us)
Async XLA Ops:
  7.2 10.4 %copy-start = (bf16[64,8,768]{2,1,0:T(8,128)(2,1)S(1)}, bf16[64,8,768]{2,1,0:T(8,128)(2,1)}, u32[]{:S(2)}) copy-start(bf16[64,8,768]{2,1,0:T(8,128)(2,1)} %param.5) | copy-start | bytes 2359300
  7.2 98.7 %all-gather.6.cloned.1.call-start = ((), (), s32[]{:S(2)}) async-start(), calls=%async_computation.3 | async-start | bytes 4456448 | tf_op jit(solution)/shard_map/all_gather | solution.py:61
  13.0 123.5 %all-gather.4.cloned.1.call-start = ((), (), s32[]{:S(2)}) async-start(), calls=%async_computation.2 | async-start | bytes 4718592 | tf_op jit(solution)/shard_map/all_gather | solution.py:95
  79.4 3.5 %collective-permute-start = (bf16[16,64,768]{2,1,0:T(8,128)(2,1)S(1)}, bf16[16,64,768]{2,1,0:T(8,128)(2,1)}, u32[]{:S(2)}, u32[]{:S(2)}) collective-permute-start(bf16[16,64,768]{2,1,0:T(8,128)(2,1)S(1)} %all_to_all.11), channel_id=1, source_target_pairs={{0,4},{4,0},{1,5},{5,1},{2,6},{6,2},{3,7},{7,3},{8,12},{12,8},{9,1... | collective-permute-start | bytes 4718600 | tf_op jit(solution)/shard_map/ppermute | solution.py:39
Sparse Core Ops, SparseCore 0:
  13.1 92.7 all-gather.5
  125.7 10.7 all-gather.3

commit v4 on v3

--- a/solution.py
+++ b/solution.py
@@ -42,6 +42,22 @@
     return jnp.take(stacked, order, axis=0)
 
 
+def group_exchange(parts, axes, count):
+    member = lax.axis_index(axes)
+    got = [lax.dynamic_index_in_dim(parts, member, 0, keepdims=False)]
+    for shift in range(1, count):
+        route = [(source, (source + shift) % count) for source in range(count)]
+        send = lax.dynamic_index_in_dim(parts, (member + shift) % count, 0, keepdims=False)
+        got.append(lax.ppermute(send, axes, route))
+    stacked = jnp.stack(got)
+    order = (member - jnp.arange(count, dtype=jnp.int32)) % count
+    return jnp.take(stacked, order, axis=0)
+
+
+def group_sum(value, axes, count):
+    return jnp.sum(group_gather(value, axes, count), axis=0)
+
+
 def body(activations, out_grad, gate_weights, routes, momentum):
     expert_count = lax.axis_size("expert")
     zlo_count = lax.axis_size("zlo")
@@ -54,9 +70,8 @@
     group_size = zlo_count * 2
     group = ("zlo", "core")
 
-    grad_parts = out_grad.reshape(tokens_here, group_size, own_rows)
-    grad_mine = lax.all_to_all(grad_parts, group, split_axis=1, concat_axis=1, tiled=True)
-    grad_mine = grad_mine.transpose(1, 0, 2)
+    grad_parts = out_grad.reshape(tokens_here, group_size, own_rows).transpose(1, 0, 2)
+    grad_mine = group_exchange(grad_parts, group, group_size)
     grad_mine, activations = lax.optimization_barrier((grad_mine, activations))
     grad_all = lax.all_gather(grad_mine, ("zhi", "expert"), axis=0, tiled=False)
     grad_all = grad_all.reshape(-1, own_rows)
@@ -88,15 +103,12 @@
 
     new_momentum = MOMENT * momentum + gradient
     ahead = gradient + MOMENT * new_momentum
-    member = lax.axis_index("zlo") * 2 + lax.axis_index("core")
-    square_sum = lax.psum(jnp.sum(ahead * ahead), group)
+    square_sum = group_sum(jnp.sum(ahead * ahead), group, group_size)
     norm_value = jnp.sqrt(square_sum)
     scaled = (ahead / (norm_value + EPSILON)).astype(jnp.bfloat16)
-    scaled_whole = lax.all_gather(scaled, group, axis=0, tiled=True)
     for turn_index in range(NS_ITERS):
-        gram = gram_of(scaled_whole).astype(jnp.bfloat16)
-        scaled_whole = newton_update(scaled_whole, gram)
-    scaled = lax.dynamic_slice_in_dim(scaled_whole, member * own_rows, own_rows, 0)
+        gram = group_sum(gram_of(scaled), group, group_size).astype(jnp.bfloat16)
+        scaled = newton_update(scaled, gram)
     update = (math.sqrt(model_width) * scaled.astype(jnp.float32)).astype(jnp.bfloat16)
     return (update, new_momentum)
 

time: 175 us -> 173 us (0.989)
  matrix products: 39.6 us -> 24.3 us
  local copies, waits for them, and re-layouts: 7.92 us -> 20.7 us
  blocking collectives: 68.6 us -> 61.4 us
  other arithmetic: 13.9 us -> 19.4 us
    gather x1 -> x4, local copies, waits for them, and re-layouts: 4.31 us -> 15.7 us  [group_gather(): return jnp.take(stacked, order, axis=0)]
    all_gather x1 -> x0, waiting for transfers between devices: 10.9 us -> none  [body(): scaled_whole = lax.all_gather(scaled, group, axis=0, tiled=True)]
    ppermute x1 -> x4, waiting for transfers between devices: 3.49 us -> 13.3 us  [group_gather(): parts.append(lax.ppermute(block, axes, route))]
    dot_general x2, matrix products: 16.3 us -> 7.11 us  [newton_update(): product = jnp.dot(scaled, poly, preferred_element_type=jnp.float32)]
    reduce_sum x0 -> x3, other arithmetic: none -> 6.33 us  [group_sum(): return jnp.sum(group_gather(value, axes, count), axis=0)]
    dot_general x2, matrix products: 11 us -> 4.84 us  [gram_of(): lax.dot_general(scaled, scaled, (((0,), (0,)), ((), ())), preferred_eleme...]
    another operation x1 -> x4, other arithmetic: 3.36 us -> 8.2 us  [group_gather(): stacked = jnp.stack(parts)]
    all_to_all x1 -> x0, blocking collectives: 4.67 us -> none  [body(): lax.all_to_all(grad_parts, group, split_axis=1, concat_axis=1, tiled=True)]
  transfers between devices with their start and end apart: 3 -> 6, of which waited for: 3 -> 6; matrix products, arithmetic and copies ran while one was open for 8% -> 6% of each run, Pallas kernels for 0% -> 0%
where the time goes in v4:
time: 173 us
  blocking collectives  61.4 us (35%)
  waiting for transfers between devices  31.2 us (18%)
  matrix products  24.3 us (14%)
  local copies, waits for them, and re-layouts  20.7 us (12%)
  other arithmetic  19.4 us (11%)
  between operations  14.9 us (9%)
    all_to_all x1, blocking collectives, body(): lax.all_to_all(scaled_hidden, ('zhi', 'expert'), split_axis=0, concat_axi...  61.4 us
    all_gather x1, waiting for transfers between devices, body(): grad_all = lax.all_gather(grad_mine, ('zhi', 'expert'), axis=0, tiled=False)  17 us
    gather x4, local copies, waits for them, and re-layouts, group_gather(): return jnp.take(stacked, order, axis=0)  15.7 us
    ppermute x4, waiting for transfers between devices, group_gather(): parts.append(lax.ppermute(block, axes, route))  13.3 us
    dot_general x1, matrix products, body(): lax.dot_general(grad_all, got_hidden, (((0,), (0,)), ((), ())), preferred...  11.3 us
    another operation x4, other arithmetic, group_gather(): stacked = jnp.stack(parts)  8.2 us
    dot_general x2, matrix products, newton_update(): product = jnp.dot(scaled, poly, preferred_element_type=jnp.float32)  7.11 us
    reduce_sum x3, other arithmetic, group_sum(): return jnp.sum(group_gather(value, axes, count), axis=0)  6.33 us
  transfers between devices with their start and end apart: 6, of which 6 were waited for; matrix products, arithmetic and copies ran while one was open for 6% of the time, Pallas kernels for 0%

profile of v4, /device:TPU:0, one launch (start us, length us, event | category | flops | bytes accessed | tf_op | source)
XLA Modules:
  0.0 173.1 jit_solution(4777523621432985994)
XLA Ops:
  7.2 0.0 copy-start
  7.2 0.0 copy-start.1
  7.2 0.0 copy-start.2
  7.2 0.0 all-gather.3.cloned.1.call-start
  7.3 1.2 reshape.119
  8.5 0.5 constant_dynamic-slice_fusion.1
  9.1 0.6 collective-permute-start
  9.7 0.9 collective-permute-done
  10.7 0.6 gather_fusion
  11.2 0.8 broadcast_select_fusion
  12.0 0.0 all-gather.3.cloned.1.call-update
  12.0 0.0 copy-done.1
  12.1 0.0 copy-done.2
  12.1 0.1 mul.48
  12.2 0.6 broadcast_and_fusion
  12.8 2.4 %and.79 = pred[1024,512]{0,1:T(32,128)(4,1)S(1)} reshape(pred[16,64,64,8]{1,0,3,2:T(8,128)(4,1)S(1)} %broadcast_and_fusion) | data formatting | bytes 1048576 | tf_op jit(solution)/shard_map/and | solution.py:86
  15.2 0.0 copy-done
  15.2 1.0 multiply_convert_fusion.1
  16.2 0.1 copy.22
  16.4 61.4 %all_to_all.5 = bf16[16,64,768]{2,1,0:T(8,128)(2,1)S(1)} all-to-all(bf16[16,64,768]{2,1,0:T(8,128)(2,1)S(1)} %bitcast.56), channel_id=1, replica_groups=mesh['zhi'=4,'zlo'=1,'core'=2,'expert'=4] {'zhi','expert'}, dimensions={0} | all-to-all | bytes 3145728 | tf_op jit(solution)/shard_map/all_to_all | solution.py:94
  77.8 0.0 collective-permute-start.1
  77.8 3.4 %collective-permute-done.1 = bf16[16,64,768]{2,1,0:T(8,128)(2,1)S(1)} collective-permute-done((bf16[16,64,768]{2,1,0:T(8,128)(2,1)S(1)}, bf16[16,64,768]{2,1,0:T(8,128)(2,1)S(1)}, u32[]{:S(2)}, u32[]{:S(2)}) %collective-permute-start.1) | collective-permute-done | bytes 1572896 | tf_op jit(solution)/shard_map/ppermute | solution.py:39
  81.2 1.9 %pad_maximum_fusion.2 = bf16[2,16,64,768]{3,2,1,0:T(8,128)(2,1)} fusion(bf16[1,16,64,768]{3,2,1,0:T(8,128)(2,1)S(1)} %bitcast.63, bf16[1,16,64,768]{3,2,1,0:T(8,128)(2,1)S(1)} %bitcast.57), kind=kLoop, calls=%fused_computation.9 | loop fusion | flops 1572864 | bytes 6291456 | tf_op jit(solution)/shard_map/stack | solution.py:40
  83.1 4.4 %gather_fusion.1 = bf16[2,16,64,768]{3,2,1,0:T(8,128)(2,1)} fusion(bf16[2,16,64,768]{3,2,1,0:T(8,128)(2,1)} %pad_maximum_fusion.2, s32[1024]{0:T(1024)S(1)} %pad_clamp_fusion.1), kind=kCustom, calls=%fused_computation.3 | custom fusion | bytes 6291464 | tf_op jit(solution)/shard_map/jit(_take)/gather | solution.py:42
  87.5 17.0 %all-gather.3.cloned.1.call-done = bf16[32,64,1024]{2,1,0:T(8,128)(2,1)} async-done(((bf16[2,64,1024]{2,1,0:T(8,128)(2,1)}), bf16[32,64,1024]{2,1,0:T(8,128)(2,1)}) %all-gather.3.cloned.1.call-update) | async-done | bytes 4194320 | tf_op jit(solution)/shard_map/all_gather | solution.py:76
  104.5 11.3 %multiply_reduce_fusion = (f32[]{:T(128)}, f32[1024,768]{1,0:T(8,128)}, f32[1024,768,1,1]{1,0,3,2:T(8,128)}) fusion(f32[1024,768]{1,0:T(8,128)} %param.11, bf16[16,2,64,1024]{3,2,1,0:T(8,128)(2,1)} %bitcast.68, bf16[2,16,64,768]{3,2,1,0:T(8,128)(2,1)} %gather_fusion.1, pred[2]{0:T(512)(128)(4,1)S(1)} %compare_and_fusion), kind=kOutput, calls=%fused_computation.18 | convolution fusion | flops 3227516928 | bytes 16777222 | tf_op jit(solution)/shard_map/dot_general | solution.py:100
  115.8 0.0 collective-permute-start.2
  115.8 1.3 collective-permute-done.2
  117.1 1.4 pad_maximum_fusion.4
  118.5 0.6 gather_fusion.2
  119.2 0.6 select_reduce_fusion.3
  120.5 3.3 %divide_convert_fusion = bf16[1024,768]{1,0:T(8,128)(2,1)S(1)} fusion(f32[]{:T(128)S(6)} %add.97, f32[1024,768]{1,0:T(8,128)} %get-tuple-element.8, f32[1024,768,1,1]{1,0,3,2:T(8,128)} %get-tuple-element.11), kind=kLoop, calls=%fused_computation.17 | loop fusion | flops 3145728 | bytes 7864324 | tf_op jit(solution)/shard_map/convert_element_type | solution.py:108
  123.8 1.4 fusion.16
  125.2 0.3 collective-permute-start.3
  125.5 4.3 %collective-permute-done.3 = f32[768,768]{1,0:T(8,128)S(1)} collective-permute-done((f32[768,768]{1,0:T(8,128)S(1)}, f32[768,768]{1,0:T(8,128)S(1)}, u32[]{:S(2)}, u32[]{:S(2)}) %collective-permute-start.3) | collective-permute-done | bytes 2359328 | tf_op jit(solution)/shard_map/ppermute | solution.py:39
  129.8 2.4 %pad_maximum_fusion = f32[2,768,768]{2,1,0:T(8,128)} fusion(f32[1,768,768]{2,1,0:T(8,128)S(1)} %bitcast.59, f32[1,768,768]{2,1,0:T(8,128)S(1)} %bitcast.58), kind=kLoop, calls=%fused_computation.5 | loop fusion | flops 1179648 | bytes 9437184 | tf_op jit(solution)/shard_map/stack | solution.py:40
  132.2 5.4 %gather_fusion.3 = f32[2,768,768]{2,1,0:T(8,128)} fusion(f32[2,768,768]{2,1,0:T(8,128)} %pad_maximum_fusion, s32[1024]{0:T(1024)S(1)} %pad_clamp_fusion), kind=kCustom, calls=%fused_computation.clone | custom fusion | bytes 9437192 | tf_op jit(solution)/shard_map/jit(_take)/gather | solution.py:42
  137.6 2.8 %select_reduce_fusion.1 = bf16[768,768]{1,0:T(8,128)(2,1)S(1)} fusion(f32[2,768,768]{2,1,0:T(8,128)} %gather_fusion.3, pred[2]{0:T(512)(128)(4,1)S(1)} %compare_and_fusion), kind=kLoop, calls=%fused_computation.8 | loop fusion | flops 1769472 | bytes 5898242 | tf_op jit(solution)/shard_map/reduce_sum | solution.py:58
  140.4 3.5 %add_convert_fusion.1 = bf16[1024,768]{1,0:T(8,128)(2,1)} fusion(bf16[1024,768]{1,0:T(8,128)(2,1)S(1)} %divide_convert_fusion, bf16[768,768]{1,0:T(8,128)(2,1)S(1)} %select_reduce_fusion.1), kind=kOutput, calls=%fused_computation.16 | convolution fusion | flops 2120024064 | bytes 4325376 | tf_op jit(solution)/shard_map/dot_general | solution.py:24
  143.9 3.4 %fusion.17 = f32[768,768]{1,0:T(8,128)S(1)} fusion(bf16[1024,768]{1,0:T(8,128)(2,1)} %add_convert_fusion.1), kind=kOutput, calls=%fused_computation.58 | convolution fusion | flops 1207959552 | bytes 3932160 | tf_op jit(solution)/shard_map/dot_general | solution.py:29
  147.3 0.3 collective-permute-start.4
  147.6 4.3 %collective-permute-done.4 = f32[768,768]{1,0:T(8,128)S(1)} collective-permute-done((f32[768,768]{1,0:T(8,128)S(1)}, f32[768,768]{1,0:T(8,128)S(1)}, u32[]{:S(2)}, u32[]{:S(2)}) %collective-permute-start.4) | collective-permute-done | bytes 2359328 | tf_op jit(solution)/shard_map/ppermute | solution.py:39
  151.9 2.4 %pad_maximum_fusion.1 = f32[2,768,768]{2,1,0:T(8,128)} fusion(f32[1,768,768]{2,1,0:T(8,128)S(1)} %bitcast.61, f32[1,768,768]{2,1,0:T(8,128)S(1)} %bitcast.60), kind=kLoop, calls=%fused_computation.6 | loop fusion | flops 1179648 | bytes 9437184 | tf_op jit(solution)/shard_map/stack | solution.py:40
  154.4 5.4 %gather_fusion.4 = f32[2,768,768]{2,1,0:T(8,128)} fusion(f32[2,768,768]{2,1,0:T(8,128)} %pad_maximum_fusion.1, s32[1024]{0:T(1024)S(1)} %pad_clamp_fusion), kind=kCustom, calls=%fused_computation.1.clone | custom fusion | bytes 9437192 | tf_op jit(solution)/shard_map/jit(_take)/gather | solution.py:42
  159.7 0.0 copy-start.3
  159.7 2.9 %select_reduce_fusion = bf16[768,768]{1,0:T(8,128)(2,1)S(1)} fusion(f32[2,768,768]{2,1,0:T(8,128)} %gather_fusion.4, pred[2]{0:T(512)(128)(4,1)S(1)} %compare_and_fusion), kind=kLoop, calls=%fused_computation.7 | loop fusion | flops 1769472 | bytes 5898242 | tf_op jit(solution)/shard_map/reduce_sum | solution.py:58
  162.6 0.0 copy-done.3
  162.7 3.6 %multiply_convert_fusion = bf16[1024,768]{1,0:T(8,128)(2,1)} fusion(bf16[1024,768]{1,0:T(8,128)(2,1)S(1)} %copy-done.3, bf16[768,768]{1,0:T(8,128)(2,1)S(1)} %select_reduce_fusion), kind=kOutput, calls=%fused_computation.14 | convolution fusion | flops 2122383360 | bytes 4325376 | tf_op jit(solution)/shard_map/dot_general | solution.py:24
  (11 shorter events, 0.2 us)
Async XLA Ops:
  7.2 8.0 %copy-start = (bf16[64,8,768]{2,1,0:T(8,128)(2,1)S(1)}, bf16[64,8,768]{2,1,0:T(8,128)(2,1)}, u32[]{:S(2)}) copy-start(bf16[64,8,768]{2,1,0:T(8,128)(2,1)} %param.7) | copy-start | bytes 2359300
  7.2 4.9 %copy-start.1 = (s32[64,8]{0,1:T(8,128)S(1)}, s32[64,8]{0,1:T(8,128)}, u32[]{:S(2)}) copy-start(s32[64,8]{0,1:T(8,128)} %param.10) | copy-start | bytes 6148
  7.2 4.9 %copy-start.2 = (f32[64,8]{0,1:T(8,128)S(1)}, f32[64,8]{0,1:T(8,128)}, u32[]{:S(2)}) copy-start(f32[64,8]{0,1:T(8,128)} %param.9) | copy-start | bytes 6148
  7.2 97.3 %all-gather.3.cloned.1.call-start = ((), (), s32[]{:S(2)}) async-start(), calls=%async_computation.1 | async-start | bytes 4456448 | tf_op jit(solution)/shard_map/all_gather | solution.py:76
  9.1 1.5 collective-permute-start
  77.8 3.4 %collective-permute-start.1 = (bf16[16,64,768]{2,1,0:T(8,128)(2,1)S(1)}, bf16[16,64,768]{2,1,0:T(8,128)(2,1)S(1)}, u32[]{:S(2)}, u32[]{:S(2)}) collective-permute-start(bf16[16,64,768]{2,1,0:T(8,128)(2,1)S(1)} %all_to_all.5), channel_id=1, source_target_pairs={{0,4},{4,0},{1,5},{5,1},{2,6},{6,2},{3,7},{7,3},{8,12},{12,8},{9,1... | collective-permute-start | bytes 4718600 | tf_op jit(solution)/shard_map/ppermute | solution.py:39
  115.8 1.3 collective-permute-start.2
  125.2 4.6 %collective-permute-start.3 = (f32[768,768]{1,0:T(8,128)S(1)}, f32[768,768]{1,0:T(8,128)S(1)}, u32[]{:S(2)}, u32[]{:S(2)}) collective-permute-start(f32[768,768]{1,0:T(8,128)S(1)} %fusion.16), channel_id=1, source_target_pairs={{0,4},{4,0},{1,5},{5,1},{2,6},{6,2},{3,7},{7,3},{8,12},{12,8},{9,1... | collective-permute-start | bytes 7077896 | tf_op jit(solution)/shard_map/ppermute | solution.py:39
  147.3 4.6 %collective-permute-start.4 = (f32[768,768]{1,0:T(8,128)S(1)}, f32[768,768]{1,0:T(8,128)S(1)}, u32[]{:S(2)}, u32[]{:S(2)}) collective-permute-start(f32[768,768]{1,0:T(8,128)S(1)} %fusion.17), channel_id=1, source_target_pairs={{0,4},{4,0},{1,5},{5,1},{2,6},{6,2},{3,7},{7,3},{8,12},{12,8},{9,1... | collective-permute-start | bytes 7077896 | tf_op jit(solution)/shard_map/ppermute | solution.py:39
  159.7 2.9 %copy-start.3 = (bf16[1024,768]{1,0:T(8,128)(2,1)S(1)}, bf16[1024,768]{1,0:T(8,128)(2,1)}, u32[]{:S(2)}) copy-start(bf16[1024,768]{1,0:T(8,128)(2,1)} %add_convert_fusion.1) | copy-start | bytes 4718596
Sparse Core Ops, SparseCore 0:
  12.2 92.2 all-gather.2

commit v5 on v4

--- a/solution.py
+++ b/solution.py
@@ -32,14 +32,11 @@
 
 
 def group_gather(block, axes, count):
-    member = lax.axis_index(axes)
     parts = [block]
     for shift in range(1, count):
         route = [(source, (source + shift) % count) for source in range(count)]
         parts.append(lax.ppermute(block, axes, route))
-    stacked = jnp.stack(parts)
-    order = (member - jnp.arange(count, dtype=jnp.int32)) % count
-    return jnp.take(stacked, order, axis=0)
+    return jnp.stack(parts)
 
 
 def group_exchange(parts, axes, count):
@@ -49,13 +46,15 @@
         route = [(source, (source + shift) % count) for source in range(count)]
         send = lax.dynamic_index_in_dim(parts, (member + shift) % count, 0, keepdims=False)
         got.append(lax.ppermute(send, axes, route))
-    stacked = jnp.stack(got)
-    order = (member - jnp.arange(count, dtype=jnp.int32)) % count
-    return jnp.take(stacked, order, axis=0)
+    return jnp.stack(got)
 
 
 def group_sum(value, axes, count):
-    return jnp.sum(group_gather(value, axes, count), axis=0)
+    total = value
+    for shift in range(1, count):
+        route = [(source, (source + shift) % count) for source in range(count)]
+        total = total + lax.ppermute(value, axes, route)
+    return total
 
 
 def body(activations, out_grad, gate_weights, routes, momentum):

time: 173 us -> 160 us (0.925)
  local copies, waits for them, and re-layouts: 20.7 us -> 5.84 us
  other arithmetic: 19.4 us -> 4.68 us
  matrix products: 24.3 us -> 33.3 us
  waiting for transfers between devices: 31.2 us -> 37.9 us
    gather x5 -> x0, local copies, waits for them, and re-layouts: 16.3 us -> none  [the longest x4 15.7 us: group_gather(): return jnp.take(stacked, order, axis=0)]
    ppermute x0 -> x3, waiting for transfers between devices: none -> 10.2 us  [group_sum(): total = total + lax.ppermute(value, axes, route)]
    ppermute x4 -> x1, waiting for transfers between devices: 13.3 us -> 3.54 us  [group_gather(): parts.append(lax.ppermute(block, axes, route))]
    dot_general x2, matrix products: 7.11 us -> 16.8 us  [newton_update(): product = jnp.dot(scaled, poly, preferred_element_type=jnp.float32)]
    another operation x5 -> x1, other arithmetic: 8.23 us -> 0.73 us  [group_exchange(): return jnp.stack(got)]
    reduce_sum x3 -> x0, other arithmetic: 6.33 us -> none  [group_sum(): return jnp.sum(group_gather(value, axes, count), axis=0)]
    all_gather x1, waiting for transfers between devices: 17 us -> 23.2 us  [body(): grad_all = lax.all_gather(grad_mine, ('zhi', 'expert'), axis=0, tiled=False)]
  transfers between devices with their start and end apart: 6 -> 6, of which waited for: 6 -> 6; matrix products, arithmetic and copies ran while one was open for 6% -> 3% of each run, Pallas kernels for 0% -> 0%
where the time goes in v5:
time: 160 us
  blocking collectives  61.4 us (38%)
  waiting for transfers between devices  37.9 us (24%)
  matrix products  33.3 us (21%)
  between operations  15.6 us (10%)
  local copies, waits for them, and re-layouts  5.84 us (4%)
  other arithmetic  4.68 us (3%)
    all_to_all x1, blocking collectives, body(): lax.all_to_all(scaled_hidden, ('zhi', 'expert'), split_axis=0, concat_axi...  61.4 us
    all_gather x1, waiting for transfers between devices, body(): grad_all = lax.all_gather(grad_mine, ('zhi', 'expert'), axis=0, tiled=False)  23.2 us
    dot_general x2, matrix products, newton_update(): product = jnp.dot(scaled, poly, preferred_element_type=jnp.float32)  16.8 us
    dot_general x1, matrix products, body(): lax.dot_general(grad_all, got_hidden, (((0,), (0,)), ((), ())), preferred...  10.7 us
    ppermute x3, waiting for transfers between devices, group_sum(): total = total + lax.ppermute(value, axes, route)  10.2 us
    dot_general x2, matrix products, gram_of(): lax.dot_general(scaled, scaled, (((0,), (0,)), ((), ())), preferred_eleme...  4.83 us
    ppermute x1, waiting for transfers between devices, group_gather(): parts.append(lax.ppermute(block, axes, route))  3.54 us
    convert_element_type x1, other arithmetic, body(): scaled = (ahead / (norm_value + EPSILON)).astype(jnp.bfloat16)  3.29 us
  transfers between devices with their start and end apart: 6, of which 6 were waited for; matrix products, arithmetic and copies ran while one was open for 3% of the time, Pallas kernels for 0%

profile of v5, /device:TPU:0, one launch (start us, length us, event | category | flops | bytes accessed | tf_op | source)
XLA Modules:
  0.0 159.8 jit_solution(11006402289292754380)
XLA Ops:
  7.2 0.0 copy-start
  7.2 0.0 copy-start.1
  7.2 0.0 copy-start.2
  7.2 0.0 all-gather.3.cloned.1.call-start
  7.3 1.2 reshape.60
  8.5 0.6 constant_dynamic-slice_fusion.1
  9.1 0.6 collective-permute-start
  9.7 0.9 collective-permute-done
  10.6 0.7 pad_maximum_fusion
  11.4 0.0 all-gather.3.cloned.1.call-update
  11.4 0.0 copy-done.1
  11.4 0.0 copy-done.2
  11.4 0.1 mul.44
  11.5 0.6 broadcast_and_fusion
  12.2 2.4 %and.34 = pred[1024,512]{0,1:T(32,128)(4,1)S(1)} reshape(pred[16,64,64,8]{1,0,3,2:T(8,128)(4,1)S(1)} %broadcast_and_fusion) | data formatting | bytes 1048576 | tf_op jit(solution)/shard_map/and | solution.py:85
  14.5 0.0 copy-done
  14.5 1.0 multiply_convert_fusion.1
  15.6 0.1 copy.24
  15.7 61.4 %all_to_all.5 = bf16[16,64,768]{2,1,0:T(8,128)(2,1)S(1)} all-to-all(bf16[16,64,768]{2,1,0:T(8,128)(2,1)S(1)} %bitcast.47), channel_id=1, replica_groups=mesh['zhi'=4,'zlo'=1,'core'=2,'expert'=4] {'zhi','expert'}, dimensions={0} | all-to-all | bytes 3145728 | tf_op jit(solution)/shard_map/all_to_all | solution.py:93
  77.1 0.0 collective-permute-start.1
  77.1 3.5 %collective-permute-done.1 = bf16[16,64,768]{2,1,0:T(8,128)(2,1)} collective-permute-done((bf16[16,64,768]{2,1,0:T(8,128)(2,1)S(1)}, bf16[16,64,768]{2,1,0:T(8,128)(2,1)}, u32[]{:S(2)}, u32[]{:S(2)}) %collective-permute-start.1) | collective-permute-done | bytes 1572896 | tf_op jit(solution)/shard_map/ppermute | solution.py:38
  80.7 23.2 %all-gather.3.cloned.1.call-done = bf16[32,64,1024]{2,1,0:T(8,128)(2,1)} async-done(((bf16[2,64,1024]{2,1,0:T(8,128)(2,1)}), bf16[32,64,1024]{2,1,0:T(8,128)(2,1)}) %all-gather.3.cloned.1.call-update) | async-done | bytes 4194320 | tf_op jit(solution)/shard_map/all_gather | solution.py:75
  103.8 10.7 %multiply_reduce_fusion = (f32[]{:T(128)}, f32[1024,768]{1,0:T(8,128)}, f32[1024,768,1,1]{1,0,3,2:T(8,128)}) fusion(f32[1024,768]{1,0:T(8,128)} %param.9, bf16[16,2,64,1024]{3,2,1,0:T(8,128)(2,1)} %bitcast.54, bf16[1,16,64,768]{3,2,0,1:T(8,128)(2,1)} %bitcast.9, bf16[1,16,64,768]{3,2,0,1:T(8,128)(2,1)S(1)} %bitcast.48), kind=kOutput, calls=%fused_computation.10 | convolution fusion | flops 3227516928 | bytes 16777220 | tf_op jit(solution)/shard_map/dot_general | solution.py:99
  114.5 0.0 collective-permute-start.2
  114.5 1.3 collective-permute-done.2
  117.2 3.3 %divide_convert_fusion = bf16[1024,768]{1,0:T(8,128)(2,1)S(1)} fusion(f32[]{:T(128)S(6)} %add.52, f32[1024,768]{1,0:T(8,128)} %get-tuple-element.7, f32[1024,768,1,1]{1,0,3,2:T(8,128)} %get-tuple-element.10), kind=kLoop, calls=%fused_computation.9 | loop fusion | flops 3145728 | bytes 7864324 | tf_op jit(solution)/shard_map/convert_element_type | solution.py:107
  120.4 1.5 fusion.9
  121.9 0.0 copy-start.3
  121.9 1.4 copy-done.3
  123.3 0.2 collective-permute-start.3
  123.5 4.5 %collective-permute-done.3 = f32[768,768]{1,0:T(8,128)} collective-permute-done((f32[768,768]{1,0:T(8,128)S(1)}, f32[768,768]{1,0:T(8,128)}, u32[]{:S(2)}, u32[]{:S(2)}) %collective-permute-start.3) | collective-permute-done | bytes 2359328 | tf_op jit(solution)/shard_map/ppermute | solution.py:56
  128.0 8.9 %add_convert_fusion.1 = bf16[1024,768]{1,0:T(8,128)(2,1)} fusion(bf16[1024,768]{1,0:T(8,128)(2,1)S(1)} %divide_convert_fusion, f32[768,768]{1,0:T(8,128)} %copy-done.3, f32[768,768]{1,0:T(8,128)} %collective-permute-done.3), kind=kOutput, calls=%fused_computation.8 | convolution fusion | flops 2122383360 | bytes 7864320 | tf_op jit(solution)/shard_map/dot_general | solution.py:24
  136.9 3.4 %fusion.10 = f32[768,768]{1,0:T(8,128)S(1)} fusion(bf16[1024,768]{1,0:T(8,128)(2,1)} %add_convert_fusion.1), kind=kOutput, calls=%fused_computation.33 | convolution fusion | flops 1207959552 | bytes 3932160 | tf_op jit(solution)/shard_map/dot_general | solution.py:29
  140.2 0.3 collective-permute-start.4
  140.5 4.5 %collective-permute-done.4 = f32[768,768]{1,0:T(8,128)} collective-permute-done((f32[768,768]{1,0:T(8,128)S(1)}, f32[768,768]{1,0:T(8,128)}, u32[]{:S(2)}, u32[]{:S(2)}) %collective-permute-start.4) | collective-permute-done | bytes 2359328 | tf_op jit(solution)/shard_map/ppermute | solution.py:56
  145.0 7.9 %multiply_convert_fusion = bf16[1024,768]{1,0:T(8,128)(2,1)} fusion(bf16[1024,768]{1,0:T(8,128)(2,1)} %add_convert_fusion.1, f32[768,768]{1,0:T(8,128)S(1)} %fusion.10, f32[768,768]{1,0:T(8,128)} %collective-permute-done.4), kind=kOutput, calls=%fused_computation.6 | convolution fusion | flops 2124742656 | bytes 7864320 | tf_op jit(solution)/shard_map/dot_general | solution.py:24
  (5 shorter events, 0.1 us)
Async XLA Ops:
  7.2 7.4 %copy-start = (bf16[64,8,768]{2,1,0:T(8,128)(2,1)S(1)}, bf16[64,8,768]{2,1,0:T(8,128)(2,1)}, u32[]{:S(2)}) copy-start(bf16[64,8,768]{2,1,0:T(8,128)(2,1)} %param.5) | copy-start | bytes 2359300
  7.2 4.2 %copy-start.1 = (s32[64,8]{0,1:T(8,128)S(1)}, s32[64,8]{0,1:T(8,128)}, u32[]{:S(2)}) copy-start(s32[64,8]{0,1:T(8,128)} %param.8) | copy-start | bytes 6148
  7.2 4.2 %copy-start.2 = (f32[64,8]{0,1:T(8,128)S(1)}, f32[64,8]{0,1:T(8,128)}, u32[]{:S(2)}) copy-start(f32[64,8]{0,1:T(8,128)} %param.7) | copy-start | bytes 6148
  7.2 96.6 %all-gather.3.cloned.1.call-start = ((), (), s32[]{:S(2)}) async-start(), calls=%async_computation.1 | async-start | bytes 4456448 | tf_op jit(solution)/shard_map/all_gather | solution.py:75
  9.1 1.5 collective-permute-start
  77.1 3.5 %collective-permute-start.1 = (bf16[16,64,768]{2,1,0:T(8,128)(2,1)S(1)}, bf16[16,64,768]{2,1,0:T(8,128)(2,1)}, u32[]{:S(2)}, u32[]{:S(2)}) collective-permute-start(bf16[16,64,768]{2,1,0:T(8,128)(2,1)S(1)} %all_to_all.5), channel_id=1, source_target_pairs={{0,4},{4,0},{1,5},{5,1},{2,6},{6,2},{3,7},{7,3},{8,12},{12,8},{9,1... | collective-permute-start | bytes 4718600 | tf_op jit(solution)/shard_map/ppermute | solution.py:38
  114.5 1.3 collective-permute-start.2
  121.9 1.4 copy-start.3
  123.3 4.7 %collective-permute-start.3 = (f32[768,768]{1,0:T(8,128)S(1)}, f32[768,768]{1,0:T(8,128)}, u32[]{:S(2)}, u32[]{:S(2)}) collective-permute-start(f32[768,768]{1,0:T(8,128)S(1)} %fusion.9), channel_id=1, source_target_pairs={{0,4},{4,0},{1,5},{5,1},{2,6},{6,2},{3,7},{7,3},{8,12},{12,8},{9,1... | collective-permute-start | bytes 7077896 | tf_op jit(solution)/shard_map/ppermute | solution.py:56
  140.2 4.7 %collective-permute-start.4 = (f32[768,768]{1,0:T(8,128)S(1)}, f32[768,768]{1,0:T(8,128)}, u32[]{:S(2)}, u32[]{:S(2)}) collective-permute-start(f32[768,768]{1,0:T(8,128)S(1)} %fusion.10), channel_id=1, source_target_pairs={{0,4},{4,0},{1,5},{5,1},{2,6},{6,2},{3,7},{7,3},{8,12},{12,8},{9,1... | collective-permute-start | bytes 7077896 | tf_op jit(solution)/shard_map/ppermute | solution.py:56
Sparse Core Ops, SparseCore 0:
  11.5 92.2 all-gather.2

commit v6 on v5

--- a/solution.py
+++ b/solution.py
@@ -21,6 +21,7 @@
 def newton_update(scaled, gram):
     square = jnp.dot(gram, gram, preferred_element_type=jnp.float32)
     poly = (COEFF_B * gram.astype(jnp.float32) + COEFF_C * square).astype(jnp.bfloat16)
+    poly = lax.optimization_barrier(poly)
     product = jnp.dot(scaled, poly, preferred_element_type=jnp.float32)
     return (COEFF_A * scaled.astype(jnp.float32) + product).astype(jnp.bfloat16)
 
@@ -72,7 +73,7 @@
     grad_parts = out_grad.reshape(tokens_here, group_size, own_rows).transpose(1, 0, 2)
     grad_mine = group_exchange(grad_parts, group, group_size)
     grad_mine, activations = lax.optimization_barrier((grad_mine, activations))
-    grad_all = lax.all_gather(grad_mine, ("zhi", "expert"), axis=0, tiled=False)
+    grad_all = lax.all_gather(grad_mine, ("zhi", "expert"), axis=1, tiled=False)
     grad_all = grad_all.reshape(-1, own_rows)
 
     numbers = jnp.arange(expert_total, dtype=jnp.int32)
@@ -94,8 +95,9 @@
         scaled_hidden, ("zhi", "expert"), split_axis=0, concat_axis=0, tiled=True
     )
     got_hidden = group_gather(got_hidden, group, group_size)
-    got_hidden = got_hidden.transpose(1, 0, 2, 3).reshape(-1, hidden_width)
+    got_hidden = got_hidden.reshape(-1, hidden_width)
 
+    grad_all, got_hidden = lax.optimization_barrier((grad_all, got_hidden))
     gradient = lax.dot_general(
         grad_all, got_hidden, (((0,), (0,)), ((), ())), preferred_element_type=jnp.float32
     )

time: 160 us -> 147 us (0.919)
  matrix products: 33.3 us -> 21.4 us
  other arithmetic: 4.68 us -> 6.65 us
  waiting for transfers between devices: 37.9 us -> 36.1 us
    dot_general x2, matrix products: 16.8 us -> 3.94 us  [newton_update(): product = jnp.dot(scaled, poly, preferred_element_type=jnp.float32)]
    dot_general x0 -> x2, matrix products: none -> 2.46 us  [newton_update(): square = jnp.dot(gram, gram, preferred_element_type=jnp.float32)]
    another operation x0 -> x1, other arithmetic: none -> 1.97 us  [group_gather(): return jnp.stack(parts)]
    dot_general x2, matrix products: 4.83 us -> 2.88 us  [gram_of(): lax.dot_general(scaled, scaled, (((0,), (0,)), ((), ())), preferred_eleme...]
    all_gather x1, waiting for transfers between devices: 23.2 us -> 21.6 us  [body(): grad_all = lax.all_gather(grad_mine, ('zhi', 'expert'), axis=1, tiled=False)]
  transfers between devices with their start and end apart: 6 -> 6, of which waited for: 6 -> 6; matrix products, arithmetic and copies ran while one was open for 3% -> 4% of each run, Pallas kernels for 0% -> 0%
where the time goes in v6:
time: 147 us
  blocking collectives  61.5 us (42%)
  waiting for transfers between devices  36.1 us (25%)
  matrix products  21.4 us (15%)
  between operations  15.5 us (11%)
  other arithmetic  6.65 us (5%)
  local copies, waits for them, and re-layouts  4.45 us (3%)
    all_to_all x1, blocking collectives, body(): lax.all_to_all(scaled_hidden, ('zhi', 'expert'), split_axis=0, concat_axi...  61.5 us
    all_gather x1, waiting for transfers between devices, body(): grad_all = lax.all_gather(grad_mine, ('zhi', 'expert'), axis=1, tiled=False)  21.6 us
    dot_general x1, matrix products, body(): lax.dot_general(grad_all, got_hidden, (((0,), (0,)), ((), ())), preferred...  11 us
    ppermute x3, waiting for transfers between devices, group_sum(): total = total + lax.ppermute(value, axes, route)  10.2 us
    dot_general x2, matrix products, newton_update(): product = jnp.dot(scaled, poly, preferred_element_type=jnp.float32)  3.94 us
    ppermute x1, waiting for transfers between devices, group_gather(): parts.append(lax.ppermute(block, axes, route))  3.41 us
    convert_element_type x1, other arithmetic, body(): scaled = (ahead / (norm_value + EPSILON)).astype(jnp.bfloat16)  3.29 us
  transfers between devices with their start and end apart: 6, of which 6 were waited for; matrix products, arithmetic and copies ran while one was open for 4% of the time, Pallas kernels for 0%

profile of v6, /device:TPU:0, one launch (start us, length us, event | category | flops | bytes accessed | tf_op | source)
XLA Modules:
  0.0 146.5 jit_solution(11995122934300035014)
XLA Ops:
  7.2 0.0 copy-start
  7.2 0.0 copy-start.1
  7.2 0.0 copy-start.2
  7.2 0.0 all-gather.3.cloned.1.call-start
  7.3 1.2 reshape.64
  8.5 0.6 constant_dynamic-slice_fusion.1
  9.1 0.6 collective-permute-start
  9.7 0.9 collective-permute-done
  10.6 0.7 pad_maximum_fusion.1
  11.4 0.0 all-gather.3.cloned.1.call-update
  11.4 0.0 copy-done.1
  11.4 0.0 copy-done.2
  11.4 0.1 mul.44
  11.5 0.6 broadcast_and_fusion
  12.2 2.4 %and.34 = pred[1024,512]{0,1:T(32,128)(4,1)S(1)} reshape(pred[16,64,64,8]{1,0,3,2:T(8,128)(4,1)S(1)} %broadcast_and_fusion) | data formatting | bytes 1048576 | tf_op jit(solution)/shard_map/and | solution.py:86
  14.5 0.0 copy-done
  14.6 1.0 multiply_convert_fusion.1
  15.6 0.1 copy.16
  15.7 61.5 %all_to_all.5 = bf16[16,64,768]{2,1,0:T(8,128)(2,1)S(1)} all-to-all(bf16[16,64,768]{2,1,0:T(8,128)(2,1)S(1)} %bitcast.34), channel_id=1, replica_groups=mesh['zhi'=4,'zlo'=1,'core'=2,'expert'=4] {'zhi','expert'}, dimensions={0} | all-to-all | bytes 3145728 | tf_op jit(solution)/shard_map/all_to_all | solution.py:94
  77.2 0.0 collective-permute-start.1
  77.2 3.4 %collective-permute-done.1 = bf16[16,64,768]{2,1,0:T(8,128)(2,1)S(1)} collective-permute-done((bf16[16,64,768]{2,1,0:T(8,128)(2,1)S(1)}, bf16[16,64,768]{2,1,0:T(8,128)(2,1)S(1)}, u32[]{:S(2)}, u32[]{:S(2)}) %collective-permute-start.1) | collective-permute-done | bytes 1572896 | tf_op jit(solution)/shard_map/ppermute | solution.py:39
  80.6 2.0 %pad_maximum_fusion = bf16[2,16,64,768]{3,2,1,0:T(8,128)(2,1)} fusion(bf16[1,16,64,768]{3,2,1,0:T(8,128)(2,1)S(1)} %bitcast.38, bf16[1,16,64,768]{3,2,1,0:T(8,128)(2,1)S(1)} %bitcast.35), kind=kLoop, calls=%fused_computation | loop fusion | flops 1572864 | bytes 6291456 | tf_op jit(solution)/shard_map/stack | solution.py:40
  82.6 21.6 %all-gather.3.cloned.1.call-done = bf16[2,1024,1024]{2,1,0:T(8,128)(2,1)} async-done(((bf16[2,64,1024]{2,1,0:T(8,128)(2,1)}), bf16[2,1024,1024]{2,1,0:T(8,128)(2,1)}) %all-gather.3.cloned.1.call-update) | async-done | bytes 4194320 | tf_op jit(solution)/shard_map/all_gather | solution.py:76
  104.1 11.0 %multiply_reduce_fusion = (f32[]{:T(128)}, f32[1024,768]{1,0:T(8,128)}, f32[1024,768]{1,0:T(8,128)}) fusion(f32[1024,768]{1,0:T(8,128)} %param.9, bf16[2048,1024]{1,0:T(8,128)(2,1)} %bitcast.43, bf16[2048,768]{1,0:T(8,128)(2,1)} %bitcast.36), kind=kOutput, calls=%fused_computation.5 | convolution fusion | flops 3225944064 | bytes 16777220 | tf_op jit(solution)/shard_map/dot_general | solution.py:101
  115.2 0.0 collective-permute-start.2
  115.2 1.4 collective-permute-done.2
  117.9 3.3 %divide_convert_fusion = bf16[1024,768]{1,0:T(8,128)(2,1)S(1)} fusion(f32[]{:T(128)S(6)} %add.52, f32[1024,768]{1,0:T(8,128)} %get-tuple-element.14, f32[1024,768]{1,0:T(8,128)} %get-tuple-element.11), kind=kLoop, calls=%fused_computation.4 | loop fusion | flops 3145728 | bytes 7864324 | tf_op jit(solution)/shard_map/convert_element_type | solution.py:109
  121.2 1.4 fusion.1
  122.6 0.2 collective-permute-start.3
  122.8 4.4 %collective-permute-done.3 = f32[768,768]{1,0:T(8,128)S(1)} collective-permute-done((f32[768,768]{1,0:T(8,128)S(1)}, f32[768,768]{1,0:T(8,128)S(1)}, u32[]{:S(2)}, u32[]{:S(2)}) %collective-permute-start.3) | collective-permute-done | bytes 2359328 | tf_op jit(solution)/shard_map/ppermute | solution.py:57
  127.2 1.2 add_convert_fusion.4
  128.4 1.4 add_convert_fusion.1
  129.8 1.4 fusion.2
  131.3 0.2 collective-permute-start.4
  131.5 4.4 %collective-permute-done.4 = f32[768,768]{1,0:T(8,128)S(1)} collective-permute-done((f32[768,768]{1,0:T(8,128)S(1)}, f32[768,768]{1,0:T(8,128)S(1)}, u32[]{:S(2)}, u32[]{:S(2)}) %collective-permute-start.4) | collective-permute-done | bytes 2359328 | tf_op jit(solution)/shard_map/ppermute | solution.py:57
  135.9 1.2 add_convert_fusion.2
  137.1 2.6 %multiply_convert_fusion = bf16[1024,768]{1,0:T(8,128)(2,1)} fusion(bf16[1024,768]{1,0:T(8,128)(2,1)S(1)} %add_convert_fusion.1, bf16[768,768]{1,0:T(8,128)(2,1)S(1)} %add_convert_fusion.2), kind=kOutput, calls=%fused_computation.1 | convolution fusion | flops 1213464576 | bytes 4325376 | tf_op jit(solution)/shard_map/dot_general | solution.py:25
  (5 shorter events, 0.1 us)
Async XLA Ops:
  7.2 7.4 %copy-start = (bf16[64,8,768]{2,1,0:T(8,128)(2,1)S(1)}, bf16[64,8,768]{2,1,0:T(8,128)(2,1)}, u32[]{:S(2)}) copy-start(bf16[64,8,768]{2,1,0:T(8,128)(2,1)} %param.5) | copy-start | bytes 2359300
  7.2 4.2 %copy-start.1 = (s32[64,8]{0,1:T(8,128)S(1)}, s32[64,8]{0,1:T(8,128)}, u32[]{:S(2)}) copy-start(s32[64,8]{0,1:T(8,128)} %param.8) | copy-start | bytes 6148
  7.2 4.2 %copy-start.2 = (f32[64,8]{0,1:T(8,128)S(1)}, f32[64,8]{0,1:T(8,128)}, u32[]{:S(2)}) copy-start(f32[64,8]{0,1:T(8,128)} %param.7) | copy-start | bytes 6148
  7.2 96.9 %all-gather.3.cloned.1.call-start = ((), (), s32[]{:S(2)}) async-start(), calls=%async_computation.1 | async-start | bytes 4456448 | tf_op jit(solution)/shard_map/all_gather | solution.py:76
  9.1 1.5 %collective-permute-start = (bf16[64,1024]{1,0:T(8,128)(2,1)S(1)}, bf16[64,1024]{1,0:T(8,128)(2,1)S(1)}, u32[]{:S(2)}, u32[]{:S(2)}) collective-permute-start(bf16[64,1024]{1,0:T(8,128)(2,1)S(1)} %bitcast.40), channel_id=1, source_target_pairs={{0,4},{4,0},{1,5},{5,1},{2,6},{6,2},{3,7},{7,3},{8,12},{12,8},{9,1... | collective-permute-start | bytes 393224 | tf_op jit(solution)/shard_map/ppermute | solution.py:49
  77.2 3.4 %collective-permute-start.1 = (bf16[16,64,768]{2,1,0:T(8,128)(2,1)S(1)}, bf16[16,64,768]{2,1,0:T(8,128)(2,1)S(1)}, u32[]{:S(2)}, u32[]{:S(2)}) collective-permute-start(bf16[16,64,768]{2,1,0:T(8,128)(2,1)S(1)} %all_to_all.5), channel_id=1, source_target_pairs={{0,4},{4,0},{1,5},{5,1},{2,6},{6,2},{3,7},{7,3},{8,12},{12,8},{9,1... | collective-permute-start | bytes 4718600 | tf_op jit(solution)/shard_map/ppermute | solution.py:39
  115.2 1.4 collective-permute-start.2
  122.6 4.6 %collective-permute-start.3 = (f32[768,768]{1,0:T(8,128)S(1)}, f32[768,768]{1,0:T(8,128)S(1)}, u32[]{:S(2)}, u32[]{:S(2)}) collective-permute-start(f32[768,768]{1,0:T(8,128)S(1)} %fusion.1), channel_id=1, source_target_pairs={{0,4},{4,0},{1,5},{5,1},{2,6},{6,2},{3,7},{7,3},{8,12},{12,8},{9,1... | collective-permute-start | bytes 7077896 | tf_op jit(solution)/shard_map/ppermute | solution.py:57
  131.3 4.6 %collective-permute-start.4 = (f32[768,768]{1,0:T(8,128)S(1)}, f32[768,768]{1,0:T(8,128)S(1)}, u32[]{:S(2)}, u32[]{:S(2)}) collective-permute-start(f32[768,768]{1,0:T(8,128)S(1)} %fusion.2), channel_id=1, source_target_pairs={{0,4},{4,0},{1,5},{5,1},{2,6},{6,2},{3,7},{7,3},{8,12},{12,8},{9,1... | collective-permute-start | bytes 7077896 | tf_op jit(solution)/shard_map/ppermute | solution.py:57
Sparse Core Ops, SparseCore 0:
  11.5 92.5 all-gather.2

commit v7 on v6

--- a/solution.py
+++ b/solution.py
@@ -101,6 +101,7 @@
     gradient = lax.dot_general(
         grad_all, got_hidden, (((0,), (0,)), ((), ())), preferred_element_type=jnp.float32
     )
+    gradient = lax.optimization_barrier(gradient)
 
     new_momentum = MOMENT * momentum + gradient
     ahead = gradient + MOMENT * new_momentum

time: 147 us -> 145 us (0.986)
  matrix products: 21.4 us -> 16.7 us
  other arithmetic: 6.65 us -> 9.9 us
    dot_general x1, matrix products: 11 us -> 6.4 us  [body(): lax.dot_general(grad_all, got_hidden, (((0,), (0,)), ((), ())), preferred...]
    reduce_sum x0 -> x1, other arithmetic: none -> 3.29 us  [body(): square_sum = group_sum(jnp.sum(ahead * ahead), group, group_size)]
where the time goes in v7:
time: 145 us
  blocking collectives  61.5 us (42%)
  waiting for transfers between devices  35.9 us (25%)
  matrix products  16.7 us (12%)
  between operations  15.6 us (11%)
  other arithmetic  9.9 us (7%)
  local copies, waits for them, and re-layouts  4.46 us (3%)
    all_to_all x1, blocking collectives, body(): lax.all_to_all(scaled_hidden, ('zhi', 'expert'), split_axis=0, concat_axi...  61.5 us
    all_gather x1, waiting for transfers between devices, body(): grad_all = lax.all_gather(grad_mine, ('zhi', 'expert'), axis=1, tiled=False)  21.6 us
    ppermute x3, waiting for transfers between devices, group_sum(): total = total + lax.ppermute(value, axes, route)  9.95 us
    dot_general x1, matrix products, body(): lax.dot_general(grad_all, got_hidden, (((0,), (0,)), ((), ())), preferred...  6.4 us
    dot_general x2, matrix products, newton_update(): product = jnp.dot(scaled, poly, preferred_element_type=jnp.float32)  3.94 us
    ppermute x1, waiting for transfers between devices, group_gather(): parts.append(lax.ppermute(block, axes, route))  3.41 us
    convert_element_type x1, other arithmetic, body(): scaled = (ahead / (norm_value + EPSILON)).astype(jnp.bfloat16)  3.29 us
    reduce_sum x1, other arithmetic, body(): square_sum = group_sum(jnp.sum(ahead * ahead), group, group_size)  3.29 us
  transfers between devices with their start and end apart: 6, of which 6 were waited for; matrix products, arithmetic and copies ran while one was open for 4% of the time, Pallas kernels for 0%

profile of v7, /device:TPU:0, one launch (start us, length us, event | category | flops | bytes accessed | tf_op | source)
XLA Modules:
  0.0 145.1 jit_solution(13061579572473308823)
XLA Ops:
  7.2 0.0 copy-start
  7.2 0.0 copy-start.3
  7.2 0.0 copy-start.4
  7.2 0.0 all-gather.3.cloned.1.call-start
  7.3 1.2 reshape.64
  8.5 0.6 constant_dynamic-slice_fusion.1
  9.1 0.6 collective-permute-start
  9.7 0.9 collective-permute-done
  10.6 0.7 pad_maximum_fusion.1
  11.4 0.0 all-gather.3.cloned.1.call-update
  11.4 0.0 copy-done.3
  11.4 0.0 copy-done.4
  11.4 0.1 mul.44
  11.5 0.6 broadcast_and_fusion
  12.2 2.4 %and.34 = pred[1024,512]{0,1:T(32,128)(4,1)S(1)} reshape(pred[16,64,64,8]{1,0,3,2:T(8,128)(4,1)S(1)} %broadcast_and_fusion) | data formatting | bytes 1048576 | tf_op jit(solution)/shard_map/and | solution.py:86
  14.5 0.0 copy-done
  14.6 1.0 multiply_convert_fusion.1
  15.6 0.1 copy.16
  15.7 61.5 %all_to_all.5 = bf16[16,64,768]{2,1,0:T(8,128)(2,1)S(1)} all-to-all(bf16[16,64,768]{2,1,0:T(8,128)(2,1)S(1)} %bitcast.34), channel_id=1, replica_groups=mesh['zhi'=4,'zlo'=1,'core'=2,'expert'=4] {'zhi','expert'}, dimensions={0} | all-to-all | bytes 3145728 | tf_op jit(solution)/shard_map/all_to_all | solution.py:94
  77.2 0.0 collective-permute-start.1
  77.2 3.4 %collective-permute-done.1 = bf16[16,64,768]{2,1,0:T(8,128)(2,1)S(1)} collective-permute-done((bf16[16,64,768]{2,1,0:T(8,128)(2,1)S(1)}, bf16[16,64,768]{2,1,0:T(8,128)(2,1)S(1)}, u32[]{:S(2)}, u32[]{:S(2)}) %collective-permute-start.1) | collective-permute-done | bytes 1572896 | tf_op jit(solution)/shard_map/ppermute | solution.py:39
  80.6 1.9 %pad_maximum_fusion = bf16[2,16,64,768]{3,2,1,0:T(8,128)(2,1)} fusion(bf16[1,16,64,768]{3,2,1,0:T(8,128)(2,1)S(1)} %bitcast.38, bf16[1,16,64,768]{3,2,1,0:T(8,128)(2,1)S(1)} %bitcast.35), kind=kLoop, calls=%fused_computation | loop fusion | flops 1572864 | bytes 6291456 | tf_op jit(solution)/shard_map/stack | solution.py:40
  82.6 21.6 %all-gather.3.cloned.1.call-done = bf16[2,1024,1024]{2,1,0:T(8,128)(2,1)} async-done(((bf16[2,64,1024]{2,1,0:T(8,128)(2,1)}), bf16[2,1024,1024]{2,1,0:T(8,128)(2,1)}) %all-gather.3.cloned.1.call-update) | async-done | bytes 4194320 | tf_op jit(solution)/shard_map/all_gather | solution.py:76
  104.1 0.0 copy-start.2
  104.1 6.4 %fusion.1 = f32[1024,768]{1,0:T(8,128)S(1)} fusion(bf16[2048,1024]{1,0:T(8,128)(2,1)} %bitcast.43, bf16[2048,768]{1,0:T(8,128)(2,1)} %bitcast.36), kind=kOutput, calls=%fused_computation.24 | convolution fusion | flops 3221225472 | bytes 10485760 | tf_op jit(solution)/shard_map/dot_general | solution.py:101
  110.6 0.0 copy-done.2
  110.6 0.0 copy-start.1
  110.6 3.3 %multiply_reduce_fusion = (f32[]{:T(128)}, f32[1024,768]{1,0:T(8,128)}) fusion(f32[1024,768]{1,0:T(8,128)S(1)} %fusion.1, f32[1024,768]{1,0:T(8,128)S(1)} %copy-done.2), kind=kLoop, calls=%fused_computation.5 | loop fusion | flops 4718591 | bytes 9437188 | tf_op jit(solution)/shard_map/reduce_sum | solution.py:108
  113.9 0.0 copy-done.1
  113.9 0.0 collective-permute-start.2
  113.9 1.3 collective-permute-done.2
  116.5 3.3 %divide_convert_fusion = bf16[1024,768]{1,0:T(8,128)(2,1)S(1)} fusion(f32[]{:T(128)S(6)} %add.52, f32[1024,768]{1,0:T(8,128)} %copy-done.1, f32[1024,768]{1,0:T(8,128)} %get-tuple-element.11), kind=kLoop, calls=%fused_computation.4 | loop fusion | flops 3145728 | bytes 7864324 | tf_op jit(solution)/shard_map/convert_element_type | solution.py:110
  119.8 1.4 fusion.2
  121.2 0.3 collective-permute-start.3
  121.5 4.3 %collective-permute-done.3 = f32[768,768]{1,0:T(8,128)S(1)} collective-permute-done((f32[768,768]{1,0:T(8,128)S(1)}, f32[768,768]{1,0:T(8,128)S(1)}, u32[]{:S(2)}, u32[]{:S(2)}) %collective-permute-start.3) | collective-permute-done | bytes 2359328 | tf_op jit(solution)/shard_map/ppermute | solution.py:57
  125.8 1.2 add_convert_fusion.4
  127.0 1.4 add_convert_fusion.1
  128.4 1.4 fusion.3
  129.9 0.3 collective-permute-start.4
  130.1 4.3 %collective-permute-done.4 = f32[768,768]{1,0:T(8,128)S(1)} collective-permute-done((f32[768,768]{1,0:T(8,128)S(1)}, f32[768,768]{1,0:T(8,128)S(1)}, u32[]{:S(2)}, u32[]{:S(2)}) %collective-permute-start.4) | collective-permute-done | bytes 2359328 | tf_op jit(solution)/shard_map/ppermute | solution.py:57
  134.5 1.2 add_convert_fusion.2
  135.7 2.6 %multiply_convert_fusion = bf16[1024,768]{1,0:T(8,128)(2,1)} fusion(bf16[1024,768]{1,0:T(8,128)(2,1)S(1)} %add_convert_fusion.1, bf16[768,768]{1,0:T(8,128)(2,1)S(1)} %add_convert_fusion.2), kind=kOutput, calls=%fused_computation.1 | convolution fusion | flops 1213464576 | bytes 4325376 | tf_op jit(solution)/shard_map/dot_general | solution.py:25
  (5 shorter events, 0.1 us)
Async XLA Ops:
  7.2 7.4 %copy-start = (bf16[64,8,768]{2,1,0:T(8,128)(2,1)S(1)}, bf16[64,8,768]{2,1,0:T(8,128)(2,1)}, u32[]{:S(2)}) copy-start(bf16[64,8,768]{2,1,0:T(8,128)(2,1)} %param.5) | copy-start | bytes 2359300
  7.2 4.2 %copy-start.3 = (s32[64,8]{0,1:T(8,128)S(1)}, s32[64,8]{0,1:T(8,128)}, u32[]{:S(2)}) copy-start(s32[64,8]{0,1:T(8,128)} %param.8) | copy-start | bytes 6148
  7.2 4.2 %copy-start.4 = (f32[64,8]{0,1:T(8,128)S(1)}, f32[64,8]{0,1:T(8,128)}, u32[]{:S(2)}) copy-start(f32[64,8]{0,1:T(8,128)} %param.7) | copy-start | bytes 6148
  7.2 96.9 %all-gather.3.cloned.1.call-start = ((), (), s32[]{:S(2)}) async-start(), calls=%async_computation.1 | async-start | bytes 4456448 | tf_op jit(solution)/shard_map/all_gather | solution.py:76
  9.1 1.5 %collective-permute-start = (bf16[64,1024]{1,0:T(8,128)(2,1)S(1)}, bf16[64,1024]{1,0:T(8,128)(2,1)S(1)}, u32[]{:S(2)}, u32[]{:S(2)}) collective-permute-start(bf16[64,1024]{1,0:T(8,128)(2,1)S(1)} %bitcast.40), channel_id=1, source_target_pairs={{0,4},{4,0},{1,5},{5,1},{2,6},{6,2},{3,7},{7,3},{8,12},{12,8},{9,1... | collective-permute-start | bytes 393224 | tf_op jit(solution)/shard_map/ppermute | solution.py:49
  77.2 3.4 %collective-permute-start.1 = (bf16[16,64,768]{2,1,0:T(8,128)(2,1)S(1)}, bf16[16,64,768]{2,1,0:T(8,128)(2,1)S(1)}, u32[]{:S(2)}, u32[]{:S(2)}) collective-permute-start(bf16[16,64,768]{2,1,0:T(8,128)(2,1)S(1)} %all_to_all.5), channel_id=1, source_target_pairs={{0,4},{4,0},{1,5},{5,1},{2,6},{6,2},{3,7},{7,3},{8,12},{12,8},{9,1... | collective-permute-start | bytes 4718600 | tf_op jit(solution)/shard_map/ppermute | solution.py:39
  104.1 6.4 %copy-start.2 = (f32[1024,768]{1,0:T(8,128)S(1)}, f32[1024,768]{1,0:T(8,128)}, u32[]{:S(2)}) copy-start(f32[1024,768]{1,0:T(8,128)} %param.9) | copy-start | bytes 9437188
  110.6 3.3 %copy-start.1 = (f32[1024,768]{1,0:T(8,128)}, f32[1024,768]{1,0:T(8,128)S(1)}, u32[]{:S(2)}) copy-start(f32[1024,768]{1,0:T(8,128)S(1)} %fusion.1) | copy-start | bytes 9437188
  113.9 1.3 collective-permute-start.2
  121.2 4.6 %collective-permute-start.3 = (f32[768,768]{1,0:T(8,128)S(1)}, f32[768,768]{1,0:T(8,128)S(1)}, u32[]{:S(2)}, u32[]{:S(2)}) collective-permute-start(f32[768,768]{1,0:T(8,128)S(1)} %fusion.2), channel_id=1, source_target_pairs={{0,4},{4,0},{1,5},{5,1},{2,6},{6,2},{3,7},{7,3},{8,12},{12,8},{9,1... | collective-permute-start | bytes 7077896 | tf_op jit(solution)/shard_map/ppermute | solution.py:57
  129.9 4.6 %collective-permute-start.4 = (f32[768,768]{1,0:T(8,128)S(1)}, f32[768,768]{1,0:T(8,128)S(1)}, u32[]{:S(2)}, u32[]{:S(2)}) collective-permute-start(f32[768,768]{1,0:T(8,128)S(1)} %fusion.3), channel_id=1, source_target_pairs={{0,4},{4,0},{1,5},{5,1},{2,6},{6,2},{3,7},{7,3},{8,12},{12,8},{9,1... | collective-permute-start | bytes 7077896 | tf_op jit(solution)/shard_map/ppermute | solution.py:57
Sparse Core Ops, SparseCore 0:
  11.5 92.5 all-gather.2

commit v8 on v7

--- a/solution.py
+++ b/solution.py
@@ -73,8 +73,10 @@
     grad_parts = out_grad.reshape(tokens_here, group_size, own_rows).transpose(1, 0, 2)
     grad_mine = group_exchange(grad_parts, group, group_size)
     grad_mine, activations = lax.optimization_barrier((grad_mine, activations))
-    grad_all = lax.all_gather(grad_mine, ("zhi", "expert"), axis=1, tiled=False)
-    grad_all = grad_all.reshape(-1, own_rows)
+    grad_all = [
+        lax.all_gather(grad_mine[shift], ("zhi", "expert"), axis=0, tiled=False)
+        for shift in range(group_size)
+    ]
 
     numbers = jnp.arange(expert_total, dtype=jnp.int32)
     matched = routes[:, :, None] == numbers[None, None, :]
@@ -95,12 +97,16 @@
         scaled_hidden, ("zhi", "expert"), split_axis=0, concat_axis=0, tiled=True
     )
     got_hidden = group_gather(got_hidden, group, group_size)
-    got_hidden = got_hidden.reshape(-1, hidden_width)
 
-    grad_all, got_hidden = lax.optimization_barrier((grad_all, got_hidden))
-    gradient = lax.dot_general(
-        grad_all, got_hidden, (((0,), (0,)), ((), ())), preferred_element_type=jnp.float32
-    )
+    gradient = None
+    for shift in range(group_size):
+        grad_part = grad_all[shift].reshape(-1, own_rows)
+        hidden_part = got_hidden[shift].reshape(-1, hidden_width)
+        grad_part, hidden_part = lax.optimization_barrier((grad_part, hidden_part))
+        product = lax.dot_general(
+            grad_part, hidden_part, (((0,), (0,)), ((), ())), preferred_element_type=jnp.float32
+        )
+        gradient = product if gradient is None else gradient + product
     gradient = lax.optimization_barrier(gradient)
 
     new_momentum = MOMENT * momentum + gradient

time: 145 us -> 189 us (1.30)
  waiting for transfers between devices: 35.9 us -> 129 us
  blocking collectives: 61.5 us -> 0 us
  starting transfers between devices: 1.12 us -> 9.49 us
  matrix products: 16.7 us -> 20.7 us
  other arithmetic: 9.9 us -> 7.26 us
    all_to_all x1 -> x0, blocking collectives: 61.5 us -> none  [body(): lax.all_to_all(scaled_hidden, ('zhi', 'expert'), split_axis=0, concat_axi...]
    all_gather x1 -> x2, waiting for transfers between devices: 21.6 us -> 77.5 us  [body(): lax.all_gather(grad_mine[shift], ('zhi', 'expert'), axis=0, tiled=False)]
    all_to_all x0 -> x1, waiting for transfers between devices: none -> 40.3 us  [body(): lax.all_to_all(scaled_hidden, ('zhi', 'expert'), split_axis=0, concat_axi...]
    all_to_all x0 -> x1, starting transfers between devices: none -> 8.21 us  [body(): lax.all_to_all(scaled_hidden, ('zhi', 'expert'), split_axis=0, concat_axi...]
    dot_general x1 -> x2, matrix products: 6.4 us -> 10.1 us  [body(): lax.dot_general(grad_part, hidden_part, (((0,), (0,)), ((), ())), preferr...]
    ppermute x1, waiting for transfers between devices: 3.41 us -> 0.01 us  [group_gather(): parts.append(lax.ppermute(block, axes, route))]
    another operation x1 -> x0, other arithmetic: 1.94 us -> none  [group_gather(): return jnp.stack(parts)]
  transfers between devices with their start and end apart: 6 -> 8, of which waited for: 6 -> 7; matrix products, arithmetic and copies ran while one was open for 4% -> 6% of each run, Pallas kernels for 0% -> 0%
where the time goes in v8:
time: 189 us
  waiting for transfers between devices  129 us (68%)
  matrix products  20.7 us (11%)
  between operations  15.5 us (8%)
  starting transfers between devices  9.49 us (5%)
  other arithmetic  7.26 us (4%)
  local copies, waits for them, and re-layouts  6.3 us (3%)
    all_gather x2, waiting for transfers between devices, body(): lax.all_gather(grad_mine[shift], ('zhi', 'expert'), axis=0, tiled=False)  77.5 us
    all_to_all x1, waiting for transfers between devices, body(): lax.all_to_all(scaled_hidden, ('zhi', 'expert'), split_axis=0, concat_axi...  40.3 us
    ppermute x3, waiting for transfers between devices, group_sum(): total = total + lax.ppermute(value, axes, route)  10.2 us
    dot_general x2, matrix products, body(): lax.dot_general(grad_part, hidden_part, (((0,), (0,)), ((), ())), preferr...  10.1 us
    all_to_all x1, starting transfers between devices, body(): lax.all_to_all(scaled_hidden, ('zhi', 'expert'), split_axis=0, concat_axi...  8.21 us
    dot_general x2, matrix products, newton_update(): product = jnp.dot(scaled, poly, preferred_element_type=jnp.float32)  3.97 us
  transfers between devices with their start and end apart: 8, of which 7 were waited for; matrix products, arithmetic and copies ran while one was open for 6% of the time, Pallas kernels for 0%

profile of v8, /device:TPU:0, one launch (start us, length us, event | category | flops | bytes accessed | tf_op | source)
XLA Modules:
  0.0 188.7 jit_solution(5815145121500655167)
XLA Ops:
  7.2 0.0 copy-start
  7.2 0.0 copy-start.3
  7.2 0.0 copy-start.4
  7.2 0.0 all-gather.3.cloned.1.call-start
  7.3 1.2 reshape.64
  8.5 0.6 constant_dynamic-slice_fusion.1
  9.1 0.6 collective-permute-start
  9.7 0.9 collective-permute-done
  10.7 0.7 fusion.1
  11.4 0.0 all-gather.3.cloned.1.call-update
  11.4 0.0 copy-done.3
  11.4 0.0 copy-done.4
  11.4 0.1 mul.44
  11.5 0.6 broadcast_and_fusion
  12.2 2.4 %and.34 = pred[1024,512]{0,1:T(32,128)(4,1)S(1)} reshape(pred[16,64,64,8]{1,0,3,2:T(8,128)(4,1)S(1)} %broadcast_and_fusion) | data formatting | bytes 1048576 | tf_op jit(solution)/shard_map/and | solution.py:88
  14.6 0.0 copy-done
  14.6 1.0 multiply_convert_fusion.1
  15.6 1.3 copy.19
  16.9 8.2 %all-to-all-start = ((bf16[16,64,768]{2,1,0:T(8,128)(2,1)}), bf16[16,64,768]{2,1,0:T(8,128)(2,1)S(1)}, u32[]{:S(2)}, u32[]{:S(2)}) async-start(bf16[16,64,768]{2,1,0:T(8,128)(2,1)} %bitcast.6), calls=%async_computation | async-start | bytes 3145728 | tf_op jit(solution)/shard_map/all_to_all | solution.py:96
  25.1 0.2 all-gather.5.cloned.1.call-start
  25.3 0.5 all-gather.5.cloned.1.call-update
  25.9 40.3 %all-to-all-done = bf16[16,64,768]{2,1,0:T(8,128)(2,1)S(1)} async-done(((bf16[16,64,768]{2,1,0:T(8,128)(2,1)}), bf16[16,64,768]{2,1,0:T(8,128)(2,1)S(1)}, u32[]{:S(2)}, u32[]{:S(2)}) %all-to-all-start) | async-done | bytes 1572896 | tf_op jit(solution)/shard_map/all_to_all | solution.py:96
  66.2 0.0 collective-permute-start.1
  66.2 20.7 %all-gather.3.cloned.1.call-done = bf16[16,64,1024]{2,1,0:T(8,128)(2,1)} async-done(((bf16[1,64,1024]{2,1,0:T(8,128)(2,1)}), bf16[16,64,1024]{2,1,0:T(8,128)(2,1)}) %all-gather.3.cloned.1.call-update) | async-done | bytes 2097168 | tf_op jit(solution)/shard_map/all_gather | solution.py:77
  86.8 5.1 %fusion.2 = f32[1024,768]{1,0:T(8,128)} fusion(bf16[1024,1024]{1,0:T(8,128)(2,1)} %bitcast.42, bf16[1024,768]{1,0:T(8,128)(2,1)S(1)} %bitcast.36), kind=kOutput, calls=%fused_computation.25 | convolution fusion | flops 1610612736 | bytes 6815744 | tf_op jit(solution)/shard_map/dot_general | solution.py:106
  91.9 56.9 %all-gather.5.cloned.1.call-done = bf16[16,64,1024]{2,1,0:T(8,128)(2,1)} async-done(((bf16[1,64,1024]{2,1,0:T(8,128)(2,1)}), bf16[16,64,1024]{2,1,0:T(8,128)(2,1)}) %all-gather.5.cloned.1.call-update) | async-done | bytes 2097168 | tf_op jit(solution)/shard_map/all_gather | solution.py:77
  148.8 0.0 collective-permute-done.1
  148.8 0.0 copy-start.2
  148.8 5.0 %convolution_add_fusion = f32[1024,768]{1,0:T(8,128)S(1)} fusion(f32[1024,768]{1,0:T(8,128)} %fusion.2, bf16[1024,1024]{1,0:T(8,128)(2,1)} %bitcast.43, bf16[1024,768]{1,0:T(8,128)(2,1)} %bitcast.9), kind=kOutput, calls=%fused_computation.13 | convolution fusion | flops 1611399168 | bytes 9961472 | tf_op jit(solution)/shard_map/dot_general | solution.py:106
  153.8 0.0 copy-done.2
  153.8 0.0 copy-start.1
  153.8 3.3 %multiply_reduce_fusion = (f32[]{:T(128)}, f32[1024,768]{1,0:T(8,128)}) fusion(f32[1024,768]{1,0:T(8,128)S(1)} %convolution_add_fusion, f32[1024,768]{1,0:T(8,128)S(1)} %copy-done.2), kind=kLoop, calls=%fused_computation.4 | loop fusion | flops 4718591 | bytes 9437188 | tf_op jit(solution)/shard_map/reduce_sum | solution.py:114
  157.1 0.0 copy-done.1
  157.1 0.0 collective-permute-start.2
  157.1 1.4 collective-permute-done.2
  159.8 3.3 %divide_convert_fusion = bf16[1024,768]{1,0:T(8,128)(2,1)S(1)} fusion(f32[]{:T(128)S(6)} %add.56, f32[1024,768]{1,0:T(8,128)} %copy-done.1, f32[1024,768]{1,0:T(8,128)} %get-tuple-element.15), kind=kLoop, calls=%fused_computation.3 | loop fusion | flops 3145728 | bytes 7864324 | tf_op jit(solution)/shard_map/convert_element_type | solution.py:116
  163.1 1.5 fusion.3
  164.6 0.2 collective-permute-start.3
  164.8 4.4 %collective-permute-done.3 = f32[768,768]{1,0:T(8,128)S(1)} collective-permute-done((f32[768,768]{1,0:T(8,128)S(1)}, f32[768,768]{1,0:T(8,128)S(1)}, u32[]{:S(2)}, u32[]{:S(2)}) %collective-permute-start.3) | collective-permute-done | bytes 2359328 | tf_op jit(solution)/shard_map/ppermute | solution.py:57
  169.2 1.3 add_convert_fusion.4
  170.5 1.4 add_convert_fusion.1
  171.9 1.5 fusion.4
  173.4 0.2 collective-permute-start.4
  173.6 4.4 %collective-permute-done.4 = f32[768,768]{1,0:T(8,128)S(1)} collective-permute-done((f32[768,768]{1,0:T(8,128)S(1)}, f32[768,768]{1,0:T(8,128)S(1)}, u32[]{:S(2)}, u32[]{:S(2)}) %collective-permute-start.4) | collective-permute-done | bytes 2359328 | tf_op jit(solution)/shard_map/ppermute | solution.py:57
  178.0 1.3 add_convert_fusion.2
  179.3 2.6 %multiply_convert_fusion = bf16[1024,768]{1,0:T(8,128)(2,1)} fusion(bf16[1024,768]{1,0:T(8,128)(2,1)S(1)} %add_convert_fusion.1, bf16[768,768]{1,0:T(8,128)(2,1)S(1)} %add_convert_fusion.2), kind=kOutput, calls=%fused_computation | convolution fusion | flops 1213464576 | bytes 4325376 | tf_op jit(solution)/shard_map/dot_general | solution.py:25
  (6 shorter events, 0.2 us)
Async XLA Ops:
  7.2 7.4 %copy-start = (bf16[64,8,768]{2,1,0:T(8,128)(2,1)S(1)}, bf16[64,8,768]{2,1,0:T(8,128)(2,1)}, u32[]{:S(2)}) copy-start(bf16[64,8,768]{2,1,0:T(8,128)(2,1)} %param.5) | copy-start | bytes 2359300
  7.2 4.2 %copy-start.3 = (s32[64,8]{0,1:T(8,128)S(1)}, s32[64,8]{0,1:T(8,128)}, u32[]{:S(2)}) copy-start(s32[64,8]{0,1:T(8,128)} %param.8) | copy-start | bytes 6148
  7.2 4.2 %copy-start.4 = (f32[64,8]{0,1:T(8,128)S(1)}, f32[64,8]{0,1:T(8,128)}, u32[]{:S(2)}) copy-start(f32[64,8]{0,1:T(8,128)} %param.7) | copy-start | bytes 6148
  7.2 79.6 %all-gather.3.cloned.1.call-start = ((), (), s32[]{:S(2)}) async-start(), calls=%async_computation.1 | async-start | bytes 2228224 | tf_op jit(solution)/shard_map/all_gather | solution.py:77
  9.1 1.5 collective-permute-start
  16.9 49.3 %all-to-all-start = ((bf16[16,64,768]{2,1,0:T(8,128)(2,1)}), bf16[16,64,768]{2,1,0:T(8,128)(2,1)S(1)}, u32[]{:S(2)}, u32[]{:S(2)}) async-start(bf16[16,64,768]{2,1,0:T(8,128)(2,1)} %bitcast.6), calls=%async_computation | async-start | bytes 3145728 | tf_op jit(solution)/shard_map/all_to_all | solution.py:96
  25.1 123.7 %all-gather.5.cloned.1.call-start = ((), (), s32[]{:S(2)}) async-start(), calls=%async_computation.2 | async-start | bytes 2228224 | tf_op jit(solution)/shard_map/all_gather | solution.py:77
  66.2 82.6 %collective-permute-start.1 = (bf16[16,64,768]{2,1,0:T(8,128)(2,1)S(1)}, bf16[16,64,768]{2,1,0:T(8,128)(2,1)}, u32[]{:S(2)}, u32[]{:S(2)}) collective-permute-start(bf16[16,64,768]{2,1,0:T(8,128)(2,1)S(1)} %all-to-all-done), channel_id=1, source_target_pairs={{0,4},{4,0},{1,5},{5,1},{2,6},{6,2},{3,7},{7,3},{8,12},{12,8},{9,1... | collective-permute-start | bytes 4718600 | tf_op jit(solution)/shard_map/ppermute | solution.py:39
  148.8 5.0 %copy-start.2 = (f32[1024,768]{1,0:T(8,128)S(1)}, f32[1024,768]{1,0:T(8,128)}, u32[]{:S(2)}) copy-start(f32[1024,768]{1,0:T(8,128)} %param.9) | copy-start | bytes 9437188
  153.8 3.3 %copy-start.1 = (f32[1024,768]{1,0:T(8,128)}, f32[1024,768]{1,0:T(8,128)S(1)}, u32[]{:S(2)}) copy-start(f32[1024,768]{1,0:T(8,128)S(1)} %convolution_add_fusion) | copy-start | bytes 9437188
  157.1 1.4 collective-permute-start.2
  164.6 4.6 %collective-permute-start.3 = (f32[768,768]{1,0:T(8,128)S(1)}, f32[768,768]{1,0:T(8,128)S(1)}, u32[]{:S(2)}, u32[]{:S(2)}) collective-permute-start(f32[768,768]{1,0:T(8,128)S(1)} %fusion.3), channel_id=1, source_target_pairs={{0,4},{4,0},{1,5},{5,1},{2,6},{6,2},{3,7},{7,3},{8,12},{12,8},{9,1... | collective-permute-start | bytes 7077896 | tf_op jit(solution)/shard_map/ppermute | solution.py:57
  173.4 4.6 %collective-permute-start.4 = (f32[768,768]{1,0:T(8,128)S(1)}, f32[768,768]{1,0:T(8,128)S(1)}, u32[]{:S(2)}, u32[]{:S(2)}) collective-permute-start(f32[768,768]{1,0:T(8,128)S(1)} %fusion.4), channel_id=1, source_target_pairs={{0,4},{4,0},{1,5},{5,1},{2,6},{6,2},{3,7},{7,3},{8,12},{12,8},{9,1... | collective-permute-start | bytes 7077896 | tf_op jit(solution)/shard_map/ppermute | solution.py:57
Sparse Core Ops, SparseCore 0:
  11.5 75.2 all-gather.2
  89.6 59.1 all-gather.4

commit v9 on v7

--- a/solution.py
+++ b/solution.py
@@ -50,11 +50,12 @@
     return jnp.stack(got)
 
 
-def group_sum(value, axes, count):
-    total = value
+def group_sum(value, axes, count, wire=None):
+    sent = value if wire is None else value.astype(wire)
+    total = sent.astype(value.dtype)
     for shift in range(1, count):
         route = [(source, (source + shift) % count) for source in range(count)]
-        total = total + lax.ppermute(value, axes, route)
+        total = total + lax.ppermute(sent, axes, route).astype(value.dtype)
     return total
 
 
@@ -109,7 +110,7 @@
     norm_value = jnp.sqrt(square_sum)
     scaled = (ahead / (norm_value + EPSILON)).astype(jnp.bfloat16)
     for turn_index in range(NS_ITERS):
-        gram = group_sum(gram_of(scaled), group, group_size).astype(jnp.bfloat16)
+        gram = group_sum(gram_of(scaled), group, group_size, jnp.bfloat16).astype(jnp.bfloat16)
         scaled = newton_update(scaled, gram)
     update = (math.sqrt(model_width) * scaled.astype(jnp.float32)).astype(jnp.bfloat16)
     return (update, new_momentum)

time: 145 us -> 142 us (0.979)
  waiting for transfers between devices: 35.9 us -> 32.5 us
    ppermute x3, waiting for transfers between devices: 9.95 us -> 6.58 us  [group_sum(): total = total + lax.ppermute(sent, axes, route).astype(value.dtype)]
where the time goes in v9:
time: 142 us
  blocking collectives  61.5 us (43%)
  waiting for transfers between devices  32.5 us (23%)
  matrix products  17.1 us (12%)
  between operations  15.6 us (11%)
  other arithmetic  9.9 us (7%)
  local copies, waits for them, and re-layouts  4.46 us (3%)
    all_to_all x1, blocking collectives, body(): lax.all_to_all(scaled_hidden, ('zhi', 'expert'), split_axis=0, concat_axi...  61.5 us
    all_gather x1, waiting for transfers between devices, body(): grad_all = lax.all_gather(grad_mine, ('zhi', 'expert'), axis=1, tiled=False)  21.6 us
    ppermute x3, waiting for transfers between devices, group_sum(): total = total + lax.ppermute(sent, axes, route).astype(value.dtype)  6.58 us
    dot_general x1, matrix products, body(): lax.dot_general(grad_all, got_hidden, (((0,), (0,)), ((), ())), preferred...  6.4 us
    dot_general x2, matrix products, newton_update(): product = jnp.dot(scaled, poly, preferred_element_type=jnp.float32)  3.97 us
    ppermute x1, waiting for transfers between devices, group_gather(): parts.append(lax.ppermute(block, axes, route))  3.41 us
    convert_element_type x1, other arithmetic, body(): scaled = (ahead / (norm_value + EPSILON)).astype(jnp.bfloat16)  3.29 us
    reduce_sum x1, other arithmetic, body(): square_sum = group_sum(jnp.sum(ahead * ahead), group, group_size)  3.29 us
  transfers between devices with their start and end apart: 6, of which 6 were waited for; matrix products, arithmetic and copies ran while one was open for 4% of the time, Pallas kernels for 0%

profile of v9, /device:TPU:0, one launch (start us, length us, event | category | flops | bytes accessed | tf_op | source)
XLA Modules:
  0.0 142.1 jit_solution(4336360466863545494)
XLA Ops:
  7.2 0.0 copy-start
  7.2 0.0 copy-start.3
  7.2 0.0 copy-start.4
  7.2 0.0 all-gather.3.cloned.1.call-start
  7.3 1.2 reshape.64
  8.5 0.6 constant_dynamic-slice_fusion.1
  9.1 0.6 collective-permute-start
  9.7 0.9 collective-permute-done
  10.6 0.7 pad_maximum_fusion.1
  11.4 0.0 all-gather.3.cloned.1.call-update
  11.4 0.0 copy-done.3
  11.4 0.0 copy-done.4
  11.4 0.1 mul.44
  11.5 0.6 broadcast_and_fusion
  12.2 2.4 %and.34 = pred[1024,512]{0,1:T(32,128)(4,1)S(1)} reshape(pred[16,64,64,8]{1,0,3,2:T(8,128)(4,1)S(1)} %broadcast_and_fusion) | data formatting | bytes 1048576 | tf_op jit(solution)/shard_map/and | solution.py:87
  14.5 0.0 copy-done
  14.6 1.0 multiply_convert_fusion.1
  15.6 0.1 copy.16
  15.7 61.5 %all_to_all.5 = bf16[16,64,768]{2,1,0:T(8,128)(2,1)S(1)} all-to-all(bf16[16,64,768]{2,1,0:T(8,128)(2,1)S(1)} %bitcast.34), channel_id=1, replica_groups=mesh['zhi'=4,'zlo'=1,'core'=2,'expert'=4] {'zhi','expert'}, dimensions={0} | all-to-all | bytes 3145728 | tf_op jit(solution)/shard_map/all_to_all | solution.py:95
  77.2 0.0 collective-permute-start.1
  77.2 3.4 %collective-permute-done.1 = bf16[16,64,768]{2,1,0:T(8,128)(2,1)S(1)} collective-permute-done((bf16[16,64,768]{2,1,0:T(8,128)(2,1)S(1)}, bf16[16,64,768]{2,1,0:T(8,128)(2,1)S(1)}, u32[]{:S(2)}, u32[]{:S(2)}) %collective-permute-start.1) | collective-permute-done | bytes 1572896 | tf_op jit(solution)/shard_map/ppermute | solution.py:39
  80.6 1.9 %pad_maximum_fusion = bf16[2,16,64,768]{3,2,1,0:T(8,128)(2,1)} fusion(bf16[1,16,64,768]{3,2,1,0:T(8,128)(2,1)S(1)} %bitcast.38, bf16[1,16,64,768]{3,2,1,0:T(8,128)(2,1)S(1)} %bitcast.35), kind=kLoop, calls=%fused_computation | loop fusion | flops 1572864 | bytes 6291456 | tf_op jit(solution)/shard_map/stack | solution.py:40
  82.6 21.6 %all-gather.3.cloned.1.call-done = bf16[2,1024,1024]{2,1,0:T(8,128)(2,1)} async-done(((bf16[2,64,1024]{2,1,0:T(8,128)(2,1)}), bf16[2,1024,1024]{2,1,0:T(8,128)(2,1)}) %all-gather.3.cloned.1.call-update) | async-done | bytes 4194320 | tf_op jit(solution)/shard_map/all_gather | solution.py:77
  104.1 0.0 copy-start.2
  104.1 6.4 %fusion.1 = f32[1024,768]{1,0:T(8,128)S(1)} fusion(bf16[2048,1024]{1,0:T(8,128)(2,1)} %bitcast.43, bf16[2048,768]{1,0:T(8,128)(2,1)} %bitcast.36), kind=kOutput, calls=%fused_computation.26 | convolution fusion | flops 3221225472 | bytes 10485760 | tf_op jit(solution)/shard_map/dot_general | solution.py:102
  110.6 0.0 copy-done.2
  110.6 0.0 copy-start.1
  110.6 3.3 %multiply_reduce_fusion = (f32[]{:T(128)}, f32[1024,768]{1,0:T(8,128)}) fusion(f32[1024,768]{1,0:T(8,128)S(1)} %fusion.1, f32[1024,768]{1,0:T(8,128)S(1)} %copy-done.2), kind=kLoop, calls=%fused_computation.5 | loop fusion | flops 4718591 | bytes 9437188 | tf_op jit(solution)/shard_map/reduce_sum | solution.py:109
  113.9 0.0 copy-done.1
  113.9 0.0 collective-permute-start.2
  113.9 1.3 collective-permute-done.2
  116.5 3.3 %divide_convert_fusion = bf16[1024,768]{1,0:T(8,128)(2,1)S(1)} fusion(f32[]{:T(128)S(6)} %add.52, f32[1024,768]{1,0:T(8,128)} %copy-done.1, f32[1024,768]{1,0:T(8,128)} %get-tuple-element.11), kind=kLoop, calls=%fused_computation.4 | loop fusion | flops 3145728 | bytes 7864324 | tf_op jit(solution)/shard_map/convert_element_type | solution.py:111
  119.8 1.4 %convolution_convert_fusion.1 = bf16[768,768]{1,0:T(8,128)(2,1)S(1)} fusion(bf16[1024,768]{1,0:T(8,128)(2,1)S(1)} %divide_convert_fusion), kind=kOutput, calls=%fused_computation.15 | convolution fusion | flops 1208549376 | bytes 2752512 | tf_op jit(solution)/shard_map/dot_general | solution.py:30
  121.2 0.3 collective-permute-start.3
  121.5 2.7 %collective-permute-done.3 = bf16[768,768]{1,0:T(8,128)(2,1)S(1)} collective-permute-done((bf16[768,768]{1,0:T(8,128)(2,1)S(1)}, bf16[768,768]{1,0:T(8,128)(2,1)S(1)}, u32[]{:S(2)}, u32[]{:S(2)}) %collective-permute-start.3) | collective-permute-done | bytes 1179680 | tf_op jit(solution)/shard_map/ppermute | solution.py:58
  124.1 1.4 add_convert_fusion.4
  125.5 1.4 add_convert_fusion.1
  126.9 1.5 %convolution_convert_fusion = bf16[768,768]{1,0:T(8,128)(2,1)S(1)} fusion(bf16[1024,768]{1,0:T(8,128)(2,1)S(1)} %add_convert_fusion.1), kind=kOutput, calls=%fused_computation.14 | convolution fusion | flops 1208549376 | bytes 2752512 | tf_op jit(solution)/shard_map/dot_general | solution.py:30
  128.4 0.3 collective-permute-start.4
  128.6 2.7 %collective-permute-done.4 = bf16[768,768]{1,0:T(8,128)(2,1)S(1)} collective-permute-done((bf16[768,768]{1,0:T(8,128)(2,1)S(1)}, bf16[768,768]{1,0:T(8,128)(2,1)S(1)}, u32[]{:S(2)}, u32[]{:S(2)}) %collective-permute-start.4) | collective-permute-done | bytes 1179680 | tf_op jit(solution)/shard_map/ppermute | solution.py:58
  131.3 1.4 add_convert_fusion.2
  132.7 2.6 %multiply_convert_fusion = bf16[1024,768]{1,0:T(8,128)(2,1)} fusion(bf16[1024,768]{1,0:T(8,128)(2,1)S(1)} %add_convert_fusion.1, bf16[768,768]{1,0:T(8,128)(2,1)S(1)} %add_convert_fusion.2), kind=kOutput, calls=%fused_computation.1 | convolution fusion | flops 1213464576 | bytes 4325376 | tf_op jit(solution)/shard_map/dot_general | solution.py:25
  (5 shorter events, 0.1 us)
Async XLA Ops:
  7.2 7.4 %copy-start = (bf16[64,8,768]{2,1,0:T(8,128)(2,1)S(1)}, bf16[64,8,768]{2,1,0:T(8,128)(2,1)}, u32[]{:S(2)}) copy-start(bf16[64,8,768]{2,1,0:T(8,128)(2,1)} %param.5) | copy-start | bytes 2359300
  7.2 4.2 %copy-start.3 = (s32[64,8]{0,1:T(8,128)S(1)}, s32[64,8]{0,1:T(8,128)}, u32[]{:S(2)}) copy-start(s32[64,8]{0,1:T(8,128)} %param.8) | copy-start | bytes 6148
  7.2 4.2 %copy-start.4 = (f32[64,8]{0,1:T(8,128)S(1)}, f32[64,8]{0,1:T(8,128)}, u32[]{:S(2)}) copy-start(f32[64,8]{0,1:T(8,128)} %param.7) | copy-start | bytes 6148
  7.2 96.9 %all-gather.3.cloned.1.call-start = ((), (), s32[]{:S(2)}) async-start(), calls=%async_computation.1 | async-start | bytes 4456448 | tf_op jit(solution)/shard_map/all_gather | solution.py:77
  9.1 1.5 %collective-permute-start = (bf16[64,1024]{1,0:T(8,128)(2,1)S(1)}, bf16[64,1024]{1,0:T(8,128)(2,1)S(1)}, u32[]{:S(2)}, u32[]{:S(2)}) collective-permute-start(bf16[64,1024]{1,0:T(8,128)(2,1)S(1)} %bitcast.40), channel_id=1, source_target_pairs={{0,4},{4,0},{1,5},{5,1},{2,6},{6,2},{3,7},{7,3},{8,12},{12,8},{9,1... | collective-permute-start | bytes 393224 | tf_op jit(solution)/shard_map/ppermute | solution.py:49
  77.2 3.4 %collective-permute-start.1 = (bf16[16,64,768]{2,1,0:T(8,128)(2,1)S(1)}, bf16[16,64,768]{2,1,0:T(8,128)(2,1)S(1)}, u32[]{:S(2)}, u32[]{:S(2)}) collective-permute-start(bf16[16,64,768]{2,1,0:T(8,128)(2,1)S(1)} %all_to_all.5), channel_id=1, source_target_pairs={{0,4},{4,0},{1,5},{5,1},{2,6},{6,2},{3,7},{7,3},{8,12},{12,8},{9,1... | collective-permute-start | bytes 4718600 | tf_op jit(solution)/shard_map/ppermute | solution.py:39
  104.1 6.4 %copy-start.2 = (f32[1024,768]{1,0:T(8,128)S(1)}, f32[1024,768]{1,0:T(8,128)}, u32[]{:S(2)}) copy-start(f32[1024,768]{1,0:T(8,128)} %param.9) | copy-start | bytes 9437188
  110.6 3.3 %copy-start.1 = (f32[1024,768]{1,0:T(8,128)}, f32[1024,768]{1,0:T(8,128)S(1)}, u32[]{:S(2)}) copy-start(f32[1024,768]{1,0:T(8,128)S(1)} %fusion.1) | copy-start | bytes 9437188
  113.9 1.3 collective-permute-start.2
  121.2 2.9 %collective-permute-start.3 = (bf16[768,768]{1,0:T(8,128)(2,1)S(1)}, bf16[768,768]{1,0:T(8,128)(2,1)S(1)}, u32[]{:S(2)}, u32[]{:S(2)}) collective-permute-start(bf16[768,768]{1,0:T(8,128)(2,1)S(1)} %convolution_convert_fusion.1), channel_id=1, source_target_pairs={{0,4},{4,0},{1,5},{5,1},{2,6},{6,2},{3,7},{7,3},{8,12},{12,8},{9,1... | collective-permute-start | bytes 3538952 | tf_op jit(solution)/shard_map/ppermute | solution.py:58
  128.4 2.9 %collective-permute-start.4 = (bf16[768,768]{1,0:T(8,128)(2,1)S(1)}, bf16[768,768]{1,0:T(8,128)(2,1)S(1)}, u32[]{:S(2)}, u32[]{:S(2)}) collective-permute-start(bf16[768,768]{1,0:T(8,128)(2,1)S(1)} %convolution_convert_fusion), channel_id=1, source_target_pairs={{0,4},{4,0},{1,5},{5,1},{2,6},{6,2},{3,7},{7,3},{8,12},{12,8},{9,1... | collective-permute-start | bytes 3538952 | tf_op jit(solution)/shard_map/ppermute | solution.py:58
Sparse Core Ops, SparseCore 0:
  11.5 92.5 all-gather.2

commit v10 on v9

--- a/solution.py
+++ b/solution.py
@@ -40,12 +40,12 @@
     return jnp.stack(parts)
 
 
-def group_exchange(parts, axes, count):
+def group_exchange(parts, axes, count, axis=0):
     member = lax.axis_index(axes)
-    got = [lax.dynamic_index_in_dim(parts, member, 0, keepdims=False)]
+    got = [lax.dynamic_index_in_dim(parts, member, axis, keepdims=False)]
     for shift in range(1, count):
         route = [(source, (source + shift) % count) for source in range(count)]
-        send = lax.dynamic_index_in_dim(parts, (member + shift) % count, 0, keepdims=False)
+        send = lax.dynamic_index_in_dim(parts, (member + shift) % count, axis, keepdims=False)
         got.append(lax.ppermute(send, axes, route))
     return jnp.stack(got)
 
@@ -71,8 +71,8 @@
     group_size = zlo_count * 2
     group = ("zlo", "core")
 
-    grad_parts = out_grad.reshape(tokens_here, group_size, own_rows).transpose(1, 0, 2)
-    grad_mine = group_exchange(grad_parts, group, group_size)
+    grad_parts = out_grad.reshape(tokens_here, group_size, own_rows)
+    grad_mine = group_exchange(grad_parts, group, group_size, axis=1)
     grad_mine, activations = lax.optimization_barrier((grad_mine, activations))
     grad_all = lax.all_gather(grad_mine, ("zhi", "expert"), axis=1, tiled=False)
     grad_all = grad_all.reshape(-1, own_rows)

time: 142 us -> 142 us (level)
  no operation moved by 1% of the time
where the time goes in v10:
time: 142 us
  blocking collectives  61.5 us (43%)
  waiting for transfers between devices  32.5 us (23%)
  matrix products  17.1 us (12%)
  between operations  15.6 us (11%)
  other arithmetic  9.9 us (7%)
  local copies, waits for them, and re-layouts  4.46 us (3%)
    all_to_all x1, blocking collectives, body(): lax.all_to_all(scaled_hidden, ('zhi', 'expert'), split_axis=0, concat_axi...  61.5 us
    all_gather x1, waiting for transfers between devices, body(): grad_all = lax.all_gather(grad_mine, ('zhi', 'expert'), axis=1, tiled=False)  21.6 us
    ppermute x3, waiting for transfers between devices, group_sum(): total = total + lax.ppermute(sent, axes, route).astype(value.dtype)  6.58 us
    dot_general x1, matrix products, body(): lax.dot_general(grad_all, got_hidden, (((0,), (0,)), ((), ())), preferred...  6.4 us
    dot_general x2, matrix products, newton_update(): product = jnp.dot(scaled, poly, preferred_element_type=jnp.float32)  3.97 us
    ppermute x1, waiting for transfers between devices, group_gather(): parts.append(lax.ppermute(block, axes, route))  3.41 us
    convert_element_type x1, other arithmetic, body(): scaled = (ahead / (norm_value + EPSILON)).astype(jnp.bfloat16)  3.29 us
    reduce_sum x1, other arithmetic, body(): square_sum = group_sum(jnp.sum(ahead * ahead), group, group_size)  3.29 us
  transfers between devices with their start and end apart: 6, of which 6 were waited for; matrix products, arithmetic and copies ran while one was open for 4% of the time, Pallas kernels for 0%

profile of v10, /device:TPU:0, one launch (start us, length us, event | category | flops | bytes accessed | tf_op | source)
XLA Modules:
  0.0 142.1 jit_solution(4336360466863545494)
XLA Ops:
  7.2 0.0 copy-start
  7.2 0.0 copy-start.3
  7.2 0.0 copy-start.4
  7.2 0.0 all-gather.3.cloned.1.call-start
  7.3 1.2 reshape.62
  8.5 0.6 constant_dynamic-slice_fusion.1
  9.1 0.6 collective-permute-start
  9.7 0.9 collective-permute-done
  10.6 0.7 pad_maximum_fusion.1
  11.4 0.0 all-gather.3.cloned.1.call-update
  11.4 0.0 copy-done.3
  11.4 0.0 copy-done.4
  11.4 0.1 mul.44
  11.5 0.6 broadcast_and_fusion
  12.2 2.4 %and.34 = pred[1024,512]{0,1:T(32,128)(4,1)S(1)} reshape(pred[16,64,64,8]{1,0,3,2:T(8,128)(4,1)S(1)} %broadcast_and_fusion) | data formatting | bytes 1048576 | tf_op jit(solution)/shard_map/and | solution.py:87
  14.5 0.0 copy-done
  14.6 1.0 multiply_convert_fusion.1
  15.6 0.1 copy.16
  15.7 61.5 %all_to_all.5 = bf16[16,64,768]{2,1,0:T(8,128)(2,1)S(1)} all-to-all(bf16[16,64,768]{2,1,0:T(8,128)(2,1)S(1)} %bitcast.34), channel_id=1, replica_groups=mesh['zhi'=4,'zlo'=1,'core'=2,'expert'=4] {'zhi','expert'}, dimensions={0} | all-to-all | bytes 3145728 | tf_op jit(solution)/shard_map/all_to_all | solution.py:95
  77.2 0.0 collective-permute-start.1
  77.2 3.4 %collective-permute-done.1 = bf16[16,64,768]{2,1,0:T(8,128)(2,1)S(1)} collective-permute-done((bf16[16,64,768]{2,1,0:T(8,128)(2,1)S(1)}, bf16[16,64,768]{2,1,0:T(8,128)(2,1)S(1)}, u32[]{:S(2)}, u32[]{:S(2)}) %collective-permute-start.1) | collective-permute-done | bytes 1572896 | tf_op jit(solution)/shard_map/ppermute | solution.py:39
  80.6 1.9 %pad_maximum_fusion = bf16[2,16,64,768]{3,2,1,0:T(8,128)(2,1)} fusion(bf16[1,16,64,768]{3,2,1,0:T(8,128)(2,1)S(1)} %bitcast.38, bf16[1,16,64,768]{3,2,1,0:T(8,128)(2,1)S(1)} %bitcast.35), kind=kLoop, calls=%fused_computation | loop fusion | flops 1572864 | bytes 6291456 | tf_op jit(solution)/shard_map/stack | solution.py:40
  82.6 21.6 %all-gather.3.cloned.1.call-done = bf16[2,1024,1024]{2,1,0:T(8,128)(2,1)} async-done(((bf16[2,64,1024]{2,1,0:T(8,128)(2,1)}), bf16[2,1024,1024]{2,1,0:T(8,128)(2,1)}) %all-gather.3.cloned.1.call-update) | async-done | bytes 4194320 | tf_op jit(solution)/shard_map/all_gather | solution.py:77
  104.1 0.0 copy-start.2
  104.1 6.4 %fusion.1 = f32[1024,768]{1,0:T(8,128)S(1)} fusion(bf16[2048,1024]{1,0:T(8,128)(2,1)} %bitcast.43, bf16[2048,768]{1,0:T(8,128)(2,1)} %bitcast.36), kind=kOutput, calls=%fused_computation.26 | convolution fusion | flops 3221225472 | bytes 10485760 | tf_op jit(solution)/shard_map/dot_general | solution.py:102
  110.6 0.0 copy-done.2
  110.6 0.0 copy-start.1
  110.6 3.3 %multiply_reduce_fusion = (f32[]{:T(128)}, f32[1024,768]{1,0:T(8,128)}) fusion(f32[1024,768]{1,0:T(8,128)S(1)} %fusion.1, f32[1024,768]{1,0:T(8,128)S(1)} %copy-done.2), kind=kLoop, calls=%fused_computation.5 | loop fusion | flops 4718591 | bytes 9437188 | tf_op jit(solution)/shard_map/reduce_sum | solution.py:109
  113.9 0.0 copy-done.1
  113.9 0.0 collective-permute-start.2
  113.9 1.3 collective-permute-done.2
  116.5 3.3 %divide_convert_fusion = bf16[1024,768]{1,0:T(8,128)(2,1)S(1)} fusion(f32[]{:T(128)S(6)} %add.52, f32[1024,768]{1,0:T(8,128)} %copy-done.1, f32[1024,768]{1,0:T(8,128)} %get-tuple-element.11), kind=kLoop, calls=%fused_computation.4 | loop fusion | flops 3145728 | bytes 7864324 | tf_op jit(solution)/shard_map/convert_element_type | solution.py:111
  119.8 1.4 %convolution_convert_fusion.1 = bf16[768,768]{1,0:T(8,128)(2,1)S(1)} fusion(bf16[1024,768]{1,0:T(8,128)(2,1)S(1)} %divide_convert_fusion), kind=kOutput, calls=%fused_computation.15 | convolution fusion | flops 1208549376 | bytes 2752512 | tf_op jit(solution)/shard_map/dot_general | solution.py:30
  121.2 0.3 collective-permute-start.3
  121.5 2.7 %collective-permute-done.3 = bf16[768,768]{1,0:T(8,128)(2,1)S(1)} collective-permute-done((bf16[768,768]{1,0:T(8,128)(2,1)S(1)}, bf16[768,768]{1,0:T(8,128)(2,1)S(1)}, u32[]{:S(2)}, u32[]{:S(2)}) %collective-permute-start.3) | collective-permute-done | bytes 1179680 | tf_op jit(solution)/shard_map/ppermute | solution.py:58
  124.1 1.4 add_convert_fusion.4
  125.5 1.4 add_convert_fusion.1
  126.9 1.5 %convolution_convert_fusion = bf16[768,768]{1,0:T(8,128)(2,1)S(1)} fusion(bf16[1024,768]{1,0:T(8,128)(2,1)S(1)} %add_convert_fusion.1), kind=kOutput, calls=%fused_computation.14 | convolution fusion | flops 1208549376 | bytes 2752512 | tf_op jit(solution)/shard_map/dot_general | solution.py:30
  128.4 0.3 collective-permute-start.4
  128.6 2.7 %collective-permute-done.4 = bf16[768,768]{1,0:T(8,128)(2,1)S(1)} collective-permute-done((bf16[768,768]{1,0:T(8,128)(2,1)S(1)}, bf16[768,768]{1,0:T(8,128)(2,1)S(1)}, u32[]{:S(2)}, u32[]{:S(2)}) %collective-permute-start.4) | collective-permute-done | bytes 1179680 | tf_op jit(solution)/shard_map/ppermute | solution.py:58
  131.3 1.4 add_convert_fusion.2
  132.7 2.6 %multiply_convert_fusion = bf16[1024,768]{1,0:T(8,128)(2,1)} fusion(bf16[1024,768]{1,0:T(8,128)(2,1)S(1)} %add_convert_fusion.1, bf16[768,768]{1,0:T(8,128)(2,1)S(1)} %add_convert_fusion.2), kind=kOutput, calls=%fused_computation.1 | convolution fusion | flops 1213464576 | bytes 4325376 | tf_op jit(solution)/shard_map/dot_general | solution.py:25
  (5 shorter events, 0.1 us)
Async XLA Ops:
  7.2 7.4 %copy-start = (bf16[64,8,768]{2,1,0:T(8,128)(2,1)S(1)}, bf16[64,8,768]{2,1,0:T(8,128)(2,1)}, u32[]{:S(2)}) copy-start(bf16[64,8,768]{2,1,0:T(8,128)(2,1)} %param.5) | copy-start | bytes 2359300
  7.2 4.2 %copy-start.3 = (s32[64,8]{0,1:T(8,128)S(1)}, s32[64,8]{0,1:T(8,128)}, u32[]{:S(2)}) copy-start(s32[64,8]{0,1:T(8,128)} %param.8) | copy-start | bytes 6148
  7.2 4.2 %copy-start.4 = (f32[64,8]{0,1:T(8,128)S(1)}, f32[64,8]{0,1:T(8,128)}, u32[]{:S(2)}) copy-start(f32[64,8]{0,1:T(8,128)} %param.7) | copy-start | bytes 6148
  7.2 96.9 %all-gather.3.cloned.1.call-start = ((), (), s32[]{:S(2)}) async-start(), calls=%async_computation.1 | async-start | bytes 4456448 | tf_op jit(solution)/shard_map/all_gather | solution.py:77
  9.1 1.5 %collective-permute-start = (bf16[64,1024]{1,0:T(8,128)(2,1)S(1)}, bf16[64,1024]{1,0:T(8,128)(2,1)S(1)}, u32[]{:S(2)}, u32[]{:S(2)}) collective-permute-start(bf16[64,1024]{1,0:T(8,128)(2,1)S(1)} %bitcast.40), channel_id=1, source_target_pairs={{0,4},{4,0},{1,5},{5,1},{2,6},{6,2},{3,7},{7,3},{8,12},{12,8},{9,1... | collective-permute-start | bytes 393224 | tf_op jit(solution)/shard_map/ppermute | solution.py:49
  77.2 3.4 %collective-permute-start.1 = (bf16[16,64,768]{2,1,0:T(8,128)(2,1)S(1)}, bf16[16,64,768]{2,1,0:T(8,128)(2,1)S(1)}, u32[]{:S(2)}, u32[]{:S(2)}) collective-permute-start(bf16[16,64,768]{2,1,0:T(8,128)(2,1)S(1)} %all_to_all.5), channel_id=1, source_target_pairs={{0,4},{4,0},{1,5},{5,1},{2,6},{6,2},{3,7},{7,3},{8,12},{12,8},{9,1... | collective-permute-start | bytes 4718600 | tf_op jit(solution)/shard_map/ppermute | solution.py:39
  104.1 6.4 %copy-start.2 = (f32[1024,768]{1,0:T(8,128)S(1)}, f32[1024,768]{1,0:T(8,128)}, u32[]{:S(2)}) copy-start(f32[1024,768]{1,0:T(8,128)} %param.9) | copy-start | bytes 9437188
  110.6 3.3 %copy-start.1 = (f32[1024,768]{1,0:T(8,128)}, f32[1024,768]{1,0:T(8,128)S(1)}, u32[]{:S(2)}) copy-start(f32[1024,768]{1,0:T(8,128)S(1)} %fusion.1) | copy-start | bytes 9437188
  113.9 1.3 collective-permute-start.2
  121.2 2.9 %collective-permute-start.3 = (bf16[768,768]{1,0:T(8,128)(2,1)S(1)}, bf16[768,768]{1,0:T(8,128)(2,1)S(1)}, u32[]{:S(2)}, u32[]{:S(2)}) collective-permute-start(bf16[768,768]{1,0:T(8,128)(2,1)S(1)} %convolution_convert_fusion.1), channel_id=1, source_target_pairs={{0,4},{4,0},{1,5},{5,1},{2,6},{6,2},{3,7},{7,3},{8,12},{12,8},{9,1... | collective-permute-start | bytes 3538952 | tf_op jit(solution)/shard_map/ppermute | solution.py:58
  128.4 2.9 %collective-permute-start.4 = (bf16[768,768]{1,0:T(8,128)(2,1)S(1)}, bf16[768,768]{1,0:T(8,128)(2,1)S(1)}, u32[]{:S(2)}, u32[]{:S(2)}) collective-permute-start(bf16[768,768]{1,0:T(8,128)(2,1)S(1)} %convolution_convert_fusion), channel_id=1, source_target_pairs={{0,4},{4,0},{1,5},{5,1},{2,6},{6,2},{3,7},{7,3},{8,12},{12,8},{9,1... | collective-permute-start | bytes 3538952 | tf_op jit(solution)/shard_map/ppermute | solution.py:58
Sparse Core Ops, SparseCore 0:
  11.5 92.5 all-gather.2

commit v11 on v9

--- a/solution.py
+++ b/solution.py
@@ -40,12 +40,19 @@
     return jnp.stack(parts)
 
 
+def pick(parts, index):
+    chosen = parts[0]
+    for place in range(1, len(parts)):
+        chosen = jnp.where(index == place, parts[place], chosen)
+    return chosen
+
+
 def group_exchange(parts, axes, count):
     member = lax.axis_index(axes)
-    got = [lax.dynamic_index_in_dim(parts, member, 0, keepdims=False)]
+    got = [pick(parts, member)]
     for shift in range(1, count):
         route = [(source, (source + shift) % count) for source in range(count)]
-        send = lax.dynamic_index_in_dim(parts, (member + shift) % count, 0, keepdims=False)
+        send = pick(parts, (member + shift) % count)
         got.append(lax.ppermute(send, axes, route))
     return jnp.stack(got)
 
@@ -71,7 +78,7 @@
     group_size = zlo_count * 2
     group = ("zlo", "core")
 
-    grad_parts = out_grad.reshape(tokens_here, group_size, own_rows).transpose(1, 0, 2)
+    grad_parts = [out_grad[:, part * own_rows:(part + 1) * own_rows] for part in range(group_size)]
     grad_mine = group_exchange(grad_parts, group, group_size)
     grad_mine, activations = lax.optimization_barrier((grad_mine, activations))
     grad_all = lax.all_gather(grad_mine, ("zhi", "expert"), axis=1, tiled=False)

time: 142 us -> 142 us (level)
  other arithmetic: 9.9 us -> 12.3 us
  local copies, waits for them, and re-layouts: 4.46 us -> 2.62 us
  transfers between devices with their start and end apart: 6 -> 6, of which waited for: 6 -> 6; matrix products, arithmetic and copies ran while one was open for 4% -> 5% of each run, Pallas kernels for 0% -> 0%
where the time goes in v11:
time: 142 us
  blocking collectives  61 us (43%)
  waiting for transfers between devices  32.6 us (23%)
  matrix products  17 us (12%)
  between operations  15.4 us (11%)
  other arithmetic  12.3 us (9%)
  local copies, waits for them, and re-layouts  2.62 us (2%)
    all_to_all x1, blocking collectives, body(): lax.all_to_all(scaled_hidden, ('zhi', 'expert'), split_axis=0, concat_axi...  61 us
    all_gather x1, waiting for transfers between devices, body(): grad_all = lax.all_gather(grad_mine, ('zhi', 'expert'), axis=1, tiled=False)  21.4 us
    ppermute x3, waiting for transfers between devices, group_sum(): total = total + lax.ppermute(sent, axes, route).astype(value.dtype)  6.78 us
    dot_general x1, matrix products, body(): lax.dot_general(grad_all, got_hidden, (((0,), (0,)), ((), ())), preferred...  6.39 us
    dot_general x2, matrix products, newton_update(): product = jnp.dot(scaled, poly, preferred_element_type=jnp.float32)  3.96 us
    ppermute x1, waiting for transfers between devices, group_gather(): parts.append(lax.ppermute(block, axes, route))  3.41 us
    convert_element_type x1, other arithmetic, body(): scaled = (ahead / (norm_value + EPSILON)).astype(jnp.bfloat16)  3.29 us
    reduce_sum x1, other arithmetic, body(): square_sum = group_sum(jnp.sum(ahead * ahead), group, group_size)  3.29 us
  transfers between devices with their start and end apart: 6, of which 6 were waited for; matrix products, arithmetic and copies ran while one was open for 5% of the time, Pallas kernels for 0%

profile of v11, /device:TPU:0, one launch (start us, length us, event | category | flops | bytes accessed | tf_op | source)
XLA Modules:
  0.0 142.2 jit_solution(4700907146908961655)
XLA Ops:
  7.2 0.0 copy-start
  7.2 0.0 all-gather.3.cloned.1.call-start
  7.2 1.1 select_bitcast_fusion
  8.3 0.6 collective-permute-start
  8.9 1.0 collective-permute-done
  9.8 0.7 pad_maximum_fusion.1
  10.6 0.0 all-gather.3.cloned.1.call-update
  10.6 0.7 select_reduce_fusion
  11.3 0.1 mul.44
  11.4 0.7 iota_compare_fusion
  12.1 0.6 broadcast_and_fusion
  12.7 2.4 %and.34 = pred[1024,512]{0,1:T(32,128)(4,1)S(1)} reshape(pred[16,64,64,8]{1,0,3,2:T(8,128)(4,1)S(1)} %broadcast_and_fusion) | data formatting | bytes 1048576 | tf_op jit(solution)/shard_map/and | solution.py:94
  15.1 0.0 copy-done
  15.1 1.0 multiply_convert_fusion.1
  16.2 0.1 copy.13
  16.3 61.0 %all_to_all.5 = bf16[16,64,768]{2,1,0:T(8,128)(2,1)S(1)} all-to-all(bf16[16,64,768]{2,1,0:T(8,128)(2,1)S(1)} %bitcast.30), channel_id=1, replica_groups=mesh['zhi'=4,'zlo'=1,'core'=2,'expert'=4] {'zhi','expert'}, dimensions={0} | all-to-all | bytes 3145728 | tf_op jit(solution)/shard_map/all_to_all | solution.py:102
  77.4 0.0 collective-permute-start.1
  77.4 3.4 %collective-permute-done.1 = bf16[16,64,768]{2,1,0:T(8,128)(2,1)S(1)} collective-permute-done((bf16[16,64,768]{2,1,0:T(8,128)(2,1)S(1)}, bf16[16,64,768]{2,1,0:T(8,128)(2,1)S(1)}, u32[]{:S(2)}, u32[]{:S(2)}) %collective-permute-start.1) | collective-permute-done | bytes 1572896 | tf_op jit(solution)/shard_map/ppermute | solution.py:39
  80.8 1.9 %pad_maximum_fusion = bf16[2,16,64,768]{3,2,1,0:T(8,128)(2,1)} fusion(bf16[1,16,64,768]{3,2,1,0:T(8,128)(2,1)S(1)} %bitcast.34, bf16[1,16,64,768]{3,2,1,0:T(8,128)(2,1)S(1)} %bitcast.31), kind=kLoop, calls=%fused_computation | loop fusion | flops 1572864 | bytes 6291456 | tf_op jit(solution)/shard_map/stack | solution.py:40
  82.7 21.4 %all-gather.3.cloned.1.call-done = bf16[2,1024,1024]{2,1,0:T(8,128)(2,1)} async-done(((bf16[2,64,1024]{2,1,0:T(8,128)(2,1)}), bf16[2,1024,1024]{2,1,0:T(8,128)(2,1)}) %all-gather.3.cloned.1.call-update) | async-done | bytes 4194320 | tf_op jit(solution)/shard_map/all_gather | solution.py:84
  104.2 0.0 copy-start.2
  104.2 6.4 %fusion.1 = f32[1024,768]{1,0:T(8,128)S(1)} fusion(bf16[2048,1024]{1,0:T(8,128)(2,1)} %bitcast.37, bf16[2048,768]{1,0:T(8,128)(2,1)} %bitcast.32), kind=kOutput, calls=%fused_computation.24 | convolution fusion | flops 3221225472 | bytes 10485760 | tf_op jit(solution)/shard_map/dot_general | solution.py:109
  110.5 0.0 copy-done.2
  110.6 0.0 copy-start.1
  110.6 3.3 %multiply_reduce_fusion = (f32[]{:T(128)}, f32[1024,768]{1,0:T(8,128)}) fusion(f32[1024,768]{1,0:T(8,128)S(1)} %fusion.1, f32[1024,768]{1,0:T(8,128)S(1)} %copy-done.2), kind=kLoop, calls=%fused_computation.5 | loop fusion | flops 4718591 | bytes 9437188 | tf_op jit(solution)/shard_map/reduce_sum | solution.py:116
  113.9 0.0 copy-done.1
  113.9 0.0 collective-permute-start.2
  113.9 1.4 %collective-permute-done.2 = f32[]{:T(128)} collective-permute-done((f32[]{:T(128)}, f32[]{:T(128)}, u32[]{:S(2)}, u32[]{:S(2)}) %collective-permute-start.2) | collective-permute-done | bytes 36 | tf_op jit(solution)/shard_map/ppermute | solution.py:65
  116.5 3.3 %divide_convert_fusion = bf16[1024,768]{1,0:T(8,128)(2,1)S(1)} fusion(f32[]{:T(128)S(6)} %add.43, f32[1024,768]{1,0:T(8,128)} %copy-done.1, f32[1024,768]{1,0:T(8,128)} %get-tuple-element.11), kind=kLoop, calls=%fused_computation.4 | loop fusion | flops 3145728 | bytes 7864324 | tf_op jit(solution)/shard_map/convert_element_type | solution.py:118
  119.8 1.4 %convolution_convert_fusion.1 = bf16[768,768]{1,0:T(8,128)(2,1)S(1)} fusion(bf16[1024,768]{1,0:T(8,128)(2,1)S(1)} %divide_convert_fusion), kind=kOutput, calls=%fused_computation.15 | convolution fusion | flops 1208549376 | bytes 2752512 | tf_op jit(solution)/shard_map/dot_general | solution.py:30
  121.3 0.2 collective-permute-start.3
  121.5 2.7 %collective-permute-done.3 = bf16[768,768]{1,0:T(8,128)(2,1)S(1)} collective-permute-done((bf16[768,768]{1,0:T(8,128)(2,1)S(1)}, bf16[768,768]{1,0:T(8,128)(2,1)S(1)}, u32[]{:S(2)}, u32[]{:S(2)}) %collective-permute-start.3) | collective-permute-done | bytes 1179680 | tf_op jit(solution)/shard_map/ppermute | solution.py:65
  124.2 1.4 add_convert_fusion.4
  125.6 1.4 add_convert_fusion.1
  127.0 1.4 %convolution_convert_fusion = bf16[768,768]{1,0:T(8,128)(2,1)S(1)} fusion(bf16[1024,768]{1,0:T(8,128)(2,1)S(1)} %add_convert_fusion.1), kind=kOutput, calls=%fused_computation.14 | convolution fusion | flops 1208549376 | bytes 2752512 | tf_op jit(solution)/shard_map/dot_general | solution.py:30
  128.4 0.2 collective-permute-start.4
  128.7 2.7 %collective-permute-done.4 = bf16[768,768]{1,0:T(8,128)(2,1)S(1)} collective-permute-done((bf16[768,768]{1,0:T(8,128)(2,1)S(1)}, bf16[768,768]{1,0:T(8,128)(2,1)S(1)}, u32[]{:S(2)}, u32[]{:S(2)}) %collective-permute-start.4) | collective-permute-done | bytes 1179680 | tf_op jit(solution)/shard_map/ppermute | solution.py:65
  131.3 1.4 add_convert_fusion.2
  132.7 2.6 %multiply_convert_fusion = bf16[1024,768]{1,0:T(8,128)(2,1)} fusion(bf16[1024,768]{1,0:T(8,128)(2,1)S(1)} %add_convert_fusion.1, bf16[768,768]{1,0:T(8,128)(2,1)S(1)} %add_convert_fusion.2), kind=kOutput, calls=%fused_computation.1 | convolution fusion | flops 1213464576 | bytes 4325376 | tf_op jit(solution)/shard_map/dot_general | solution.py:25
  (1 shorter events, 0.0 us)
Async XLA Ops:
  7.2 8.0 %copy-start = (bf16[64,8,768]{2,1,0:T(8,128)(2,1)S(1)}, bf16[64,8,768]{2,1,0:T(8,128)(2,1)}, u32[]{:S(2)}) copy-start(bf16[64,8,768]{2,1,0:T(8,128)(2,1)} %param.5) | copy-start | bytes 2359300
  7.2 97.0 %all-gather.3.cloned.1.call-start = ((), (), s32[]{:S(2)}) async-start(), calls=%async_computation.1 | async-start | bytes 4456448 | tf_op jit(solution)/shard_map/all_gather | solution.py:84
  8.3 1.5 %collective-permute-start = (bf16[64,1024]{1,0:T(8,128)(2,1)S(1)}, bf16[64,1024]{1,0:T(8,128)(2,1)S(1)}, u32[]{:S(2)}, u32[]{:S(2)}) collective-permute-start(bf16[64,1024]{1,0:T(8,128)(2,1)S(1)} %get-tuple-element.13), channel_id=1, source_target_pairs={{0,4},{4,0},{1,5},{5,1},{2,6},{6,2},{3,7},{7,3},{8,12},{12,8},{9,1... | collective-permute-start | bytes 393224 | tf_op jit(solution)/shard_map/ppermute | solution.py:56
  77.4 3.4 %collective-permute-start.1 = (bf16[16,64,768]{2,1,0:T(8,128)(2,1)S(1)}, bf16[16,64,768]{2,1,0:T(8,128)(2,1)S(1)}, u32[]{:S(2)}, u32[]{:S(2)}) collective-permute-start(bf16[16,64,768]{2,1,0:T(8,128)(2,1)S(1)} %all_to_all.5), channel_id=1, source_target_pairs={{0,4},{4,0},{1,5},{5,1},{2,6},{6,2},{3,7},{7,3},{8,12},{12,8},{9,1... | collective-permute-start | bytes 4718600 | tf_op jit(solution)/shard_map/ppermute | solution.py:39
  104.2 6.4 %copy-start.2 = (f32[1024,768]{1,0:T(8,128)S(1)}, f32[1024,768]{1,0:T(8,128)}, u32[]{:S(2)}) copy-start(f32[1024,768]{1,0:T(8,128)} %param.9) | copy-start | bytes 9437188
  110.6 3.3 %copy-start.1 = (f32[1024,768]{1,0:T(8,128)}, f32[1024,768]{1,0:T(8,128)S(1)}, u32[]{:S(2)}) copy-start(f32[1024,768]{1,0:T(8,128)S(1)} %fusion.1) | copy-start | bytes 9437188
  113.9 1.4 %collective-permute-start.2 = (f32[]{:T(128)}, f32[]{:T(128)}, u32[]{:S(2)}, u32[]{:S(2)}) collective-permute-start(f32[]{:T(128)} %get-tuple-element.10), channel_id=1, source_target_pairs={{0,4},{4,0},{1,5},{5,1},{2,6},{6,2},{3,7},{7,3},{8,12},{12,8},{9,1... | collective-permute-start | bytes 20 | tf_op jit(solution)/shard_map/ppermute | solution.py:65
  121.3 2.9 %collective-permute-start.3 = (bf16[768,768]{1,0:T(8,128)(2,1)S(1)}, bf16[768,768]{1,0:T(8,128)(2,1)S(1)}, u32[]{:S(2)}, u32[]{:S(2)}) collective-permute-start(bf16[768,768]{1,0:T(8,128)(2,1)S(1)} %convolution_convert_fusion.1), channel_id=1, source_target_pairs={{0,4},{4,0},{1,5},{5,1},{2,6},{6,2},{3,7},{7,3},{8,12},{12,8},{9,1... | collective-permute-start | bytes 3538952 | tf_op jit(solution)/shard_map/ppermute | solution.py:65
  128.4 2.9 %collective-permute-start.4 = (bf16[768,768]{1,0:T(8,128)(2,1)S(1)}, bf16[768,768]{1,0:T(8,128)(2,1)S(1)}, u32[]{:S(2)}, u32[]{:S(2)}) collective-permute-start(bf16[768,768]{1,0:T(8,128)(2,1)S(1)} %convolution_convert_fusion), channel_id=1, source_target_pairs={{0,4},{4,0},{1,5},{5,1},{2,6},{6,2},{3,7},{7,3},{8,12},{12,8},{9,1... | collective-permute-start | bytes 3538952 | tf_op jit(solution)/shard_map/ppermute | solution.py:65
Sparse Core Ops, SparseCore 0:
  11.3 92.7 all-gather.2

commit v12 on v9

--- a/solution.py
+++ b/solution.py
@@ -106,7 +106,8 @@
 
     new_momentum = MOMENT * momentum + gradient
     ahead = gradient + MOMENT * new_momentum
-    square_sum = group_sum(jnp.sum(ahead * ahead), group, group_size)
+    ahead, own_square_sum = lax.optimization_barrier((ahead, jnp.sum(ahead * ahead)))
+    square_sum = group_sum(own_square_sum, group, group_size)
     norm_value = jnp.sqrt(square_sum)
     scaled = (ahead / (norm_value + EPSILON)).astype(jnp.bfloat16)
     for turn_index in range(NS_ITERS):

time: 142 us -> 143 us (level)
  matrix products: 17.1 us -> 20 us
  other arithmetic: 9.9 us -> 7.39 us
    convert_element_type x1 -> x0, other arithmetic: 3.29 us -> none  [body(): scaled = (ahead / (norm_value + EPSILON)).astype(jnp.bfloat16)]
    dot_general x2, matrix products: 2.91 us -> 5.76 us  [gram_of(): lax.dot_general(scaled, scaled, (((0,), (0,)), ((), ())), preferred_eleme...]
where the time goes in v12:
time: 143 us; the launch traced here: 142 us
  blocking collectives  61.5 us (43%)
  waiting for transfers between devices  32.5 us (23%)
  matrix products  20 us (14%)
  between operations  15.6 us (11%)
  other arithmetic  7.39 us (5%)
  local copies, waits for them, and re-layouts  4.46 us (3%)
    all_to_all x1, blocking collectives, body(): lax.all_to_all(scaled_hidden, ('zhi', 'expert'), split_axis=0, concat_axi...  61.5 us
    all_gather x1, waiting for transfers between devices, body(): grad_all = lax.all_gather(grad_mine, ('zhi', 'expert'), axis=1, tiled=False)  21.6 us
    ppermute x3, waiting for transfers between devices, group_sum(): total = total + lax.ppermute(sent, axes, route).astype(value.dtype)  6.59 us
    dot_general x1, matrix products, body(): lax.dot_general(grad_all, got_hidden, (((0,), (0,)), ((), ())), preferred...  6.4 us
    dot_general x2, matrix products, gram_of(): lax.dot_general(scaled, scaled, (((0,), (0,)), ((), ())), preferred_eleme...  5.76 us
    reduce_sum x1, other arithmetic, body(): jnp.sum(ahead * ahead)  4.07 us
    dot_general x2, matrix products, newton_update(): product = jnp.dot(scaled, poly, preferred_element_type=jnp.float32)  4 us
    ppermute x1, waiting for transfers between devices, group_gather(): parts.append(lax.ppermute(block, axes, route))  3.41 us
  transfers between devices with their start and end apart: 6, of which 6 were waited for; matrix products, arithmetic and copies ran while one was open for 4% of the time, Pallas kernels for 0%

profile of v12, /device:TPU:0, one launch (start us, length us, event | category | flops | bytes accessed | tf_op | source)
XLA Modules:
  0.0 142.5 jit_solution(14687724476750653635)
XLA Ops:
  7.2 0.0 copy-start
  7.2 0.0 copy-start.3
  7.2 0.0 copy-start.4
  7.2 0.0 all-gather.3.cloned.1.call-start
  7.3 1.2 reshape.64
  8.5 0.6 constant_dynamic-slice_fusion.1
  9.1 0.6 collective-permute-start
  9.7 0.9 collective-permute-done
  10.6 0.7 pad_maximum_fusion.1
  11.4 0.0 all-gather.3.cloned.1.call-update
  11.4 0.0 copy-done.3
  11.4 0.0 copy-done.4
  11.4 0.1 mul.44
  11.5 0.6 broadcast_and_fusion
  12.2 2.4 %and.34 = pred[1024,512]{0,1:T(32,128)(4,1)S(1)} reshape(pred[16,64,64,8]{1,0,3,2:T(8,128)(4,1)S(1)} %broadcast_and_fusion) | data formatting | bytes 1048576 | tf_op jit(solution)/shard_map/and | solution.py:87
  14.5 0.0 copy-done
  14.6 1.0 multiply_convert_fusion.1
  15.6 0.1 copy.16
  15.7 61.5 %all_to_all.5 = bf16[16,64,768]{2,1,0:T(8,128)(2,1)S(1)} all-to-all(bf16[16,64,768]{2,1,0:T(8,128)(2,1)S(1)} %bitcast.31), channel_id=1, replica_groups=mesh['zhi'=4,'zlo'=1,'core'=2,'expert'=4] {'zhi','expert'}, dimensions={0} | all-to-all | bytes 3145728 | tf_op jit(solution)/shard_map/all_to_all | solution.py:95
  77.2 0.0 collective-permute-start.1
  77.2 3.4 %collective-permute-done.1 = bf16[16,64,768]{2,1,0:T(8,128)(2,1)S(1)} collective-permute-done((bf16[16,64,768]{2,1,0:T(8,128)(2,1)S(1)}, bf16[16,64,768]{2,1,0:T(8,128)(2,1)S(1)}, u32[]{:S(2)}, u32[]{:S(2)}) %collective-permute-start.1) | collective-permute-done | bytes 1572896 | tf_op jit(solution)/shard_map/ppermute | solution.py:39
  80.6 1.9 %pad_maximum_fusion = bf16[2,16,64,768]{3,2,1,0:T(8,128)(2,1)} fusion(bf16[1,16,64,768]{3,2,1,0:T(8,128)(2,1)S(1)} %bitcast.35, bf16[1,16,64,768]{3,2,1,0:T(8,128)(2,1)S(1)} %bitcast.32), kind=kLoop, calls=%fused_computation | loop fusion | flops 1572864 | bytes 6291456 | tf_op jit(solution)/shard_map/stack | solution.py:40
  82.6 21.6 %all-gather.3.cloned.1.call-done = bf16[2,1024,1024]{2,1,0:T(8,128)(2,1)} async-done(((bf16[2,64,1024]{2,1,0:T(8,128)(2,1)}), bf16[2,1024,1024]{2,1,0:T(8,128)(2,1)}) %all-gather.3.cloned.1.call-update) | async-done | bytes 4194320 | tf_op jit(solution)/shard_map/all_gather | solution.py:77
  104.1 0.0 copy-start.1
  104.1 6.4 %fusion.1 = f32[1024,768]{1,0:T(8,128)S(1)} fusion(bf16[2048,1024]{1,0:T(8,128)(2,1)} %bitcast.40, bf16[2048,768]{1,0:T(8,128)(2,1)} %bitcast.33), kind=kOutput, calls=%fused_computation.26 | convolution fusion | flops 3221225472 | bytes 10485760 | tf_op jit(solution)/shard_map/dot_general | solution.py:102
  110.5 0.0 copy-done.1
  110.6 4.1 %multiply_reduce_fusion = (f32[]{:T(128)}, f32[1024,768]{1,0:T(8,128)}, f32[1024,768]{1,0:T(8,128)}) fusion(f32[1024,768]{1,0:T(8,128)S(1)} %fusion.1, f32[1024,768]{1,0:T(8,128)S(1)} %copy-done.1), kind=kLoop, calls=%fused_computation.5 | loop fusion | flops 4718591 | bytes 12582916 | tf_op jit(solution)/shard_map/reduce_sum | solution.py:109
  114.6 0.0 collective-permute-start.2
  114.6 1.3 collective-permute-done.2
  117.2 4.3 %convolution_convert_fusion.1 = bf16[768,768]{1,0:T(8,128)(2,1)S(1)} fusion(f32[1024,768]{1,0:T(8,128)} %get-tuple-element.12, f32[]{:T(128)S(6)} %add.52), kind=kOutput, calls=%fused_computation.15 | convolution fusion | flops 1210122240 | bytes 4325380 | tf_op jit(solution)/shard_map/dot_general | solution.py:30
  121.5 0.0 copy-start.2
  121.5 0.3 collective-permute-start.3
  121.8 2.7 %collective-permute-done.3 = bf16[768,768]{1,0:T(8,128)(2,1)S(1)} collective-permute-done((bf16[768,768]{1,0:T(8,128)(2,1)S(1)}, bf16[768,768]{1,0:T(8,128)(2,1)S(1)}, u32[]{:S(2)}, u32[]{:S(2)}) %collective-permute-start.3) | collective-permute-done | bytes 1179680 | tf_op jit(solution)/shard_map/ppermute | solution.py:58
  124.5 1.4 add_convert_fusion.4
  125.8 0.0 copy-done.2
  125.9 1.4 add_convert_fusion.1
  127.3 1.5 %convolution_convert_fusion = bf16[768,768]{1,0:T(8,128)(2,1)S(1)} fusion(bf16[1024,768]{1,0:T(8,128)(2,1)S(1)} %add_convert_fusion.1), kind=kOutput, calls=%fused_computation.14 | convolution fusion | flops 1208549376 | bytes 2752512 | tf_op jit(solution)/shard_map/dot_general | solution.py:30
  128.8 0.3 collective-permute-start.4
  129.0 2.7 %collective-permute-done.4 = bf16[768,768]{1,0:T(8,128)(2,1)S(1)} collective-permute-done((bf16[768,768]{1,0:T(8,128)(2,1)S(1)}, bf16[768,768]{1,0:T(8,128)(2,1)S(1)}, u32[]{:S(2)}, u32[]{:S(2)}) %collective-permute-start.4) | collective-permute-done | bytes 1179680 | tf_op jit(solution)/shard_map/ppermute | solution.py:58
  131.7 1.4 add_convert_fusion.2
  133.1 2.6 %multiply_convert_fusion = bf16[1024,768]{1,0:T(8,128)(2,1)} fusion(bf16[1024,768]{1,0:T(8,128)(2,1)S(1)} %add_convert_fusion.1, bf16[768,768]{1,0:T(8,128)(2,1)S(1)} %add_convert_fusion.2), kind=kOutput, calls=%fused_computation.1 | convolution fusion | flops 1213464576 | bytes 4325376 | tf_op jit(solution)/shard_map/dot_general | solution.py:25
  (5 shorter events, 0.1 us)
Async XLA Ops:
  7.2 7.4 %copy-start = (bf16[64,8,768]{2,1,0:T(8,128)(2,1)S(1)}, bf16[64,8,768]{2,1,0:T(8,128)(2,1)}, u32[]{:S(2)}) copy-start(bf16[64,8,768]{2,1,0:T(8,128)(2,1)} %param.5) | copy-start | bytes 2359300
  7.2 4.2 %copy-start.3 = (s32[64,8]{0,1:T(8,128)S(1)}, s32[64,8]{0,1:T(8,128)}, u32[]{:S(2)}) copy-start(s32[64,8]{0,1:T(8,128)} %param.8) | copy-start | bytes 6148
  7.2 4.2 %copy-start.4 = (f32[64,8]{0,1:T(8,128)S(1)}, f32[64,8]{0,1:T(8,128)}, u32[]{:S(2)}) copy-start(f32[64,8]{0,1:T(8,128)} %param.7) | copy-start | bytes 6148
  7.2 96.9 %all-gather.3.cloned.1.call-start = ((), (), s32[]{:S(2)}) async-start(), calls=%async_computation.1 | async-start | bytes 4456448 | tf_op jit(solution)/shard_map/all_gather | solution.py:77
  9.1 1.5 %collective-permute-start = (bf16[64,1024]{1,0:T(8,128)(2,1)S(1)}, bf16[64,1024]{1,0:T(8,128)(2,1)S(1)}, u32[]{:S(2)}, u32[]{:S(2)}) collective-permute-start(bf16[64,1024]{1,0:T(8,128)(2,1)S(1)} %bitcast.37), channel_id=1, source_target_pairs={{0,4},{4,0},{1,5},{5,1},{2,6},{6,2},{3,7},{7,3},{8,12},{12,8},{9,1... | collective-permute-start | bytes 393224 | tf_op jit(solution)/shard_map/ppermute | solution.py:49
  77.2 3.4 %collective-permute-start.1 = (bf16[16,64,768]{2,1,0:T(8,128)(2,1)S(1)}, bf16[16,64,768]{2,1,0:T(8,128)(2,1)S(1)}, u32[]{:S(2)}, u32[]{:S(2)}) collective-permute-start(bf16[16,64,768]{2,1,0:T(8,128)(2,1)S(1)} %all_to_all.5), channel_id=1, source_target_pairs={{0,4},{4,0},{1,5},{5,1},{2,6},{6,2},{3,7},{7,3},{8,12},{12,8},{9,1... | collective-permute-start | bytes 4718600 | tf_op jit(solution)/shard_map/ppermute | solution.py:39
  104.1 6.4 %copy-start.1 = (f32[1024,768]{1,0:T(8,128)S(1)}, f32[1024,768]{1,0:T(8,128)}, u32[]{:S(2)}) copy-start(f32[1024,768]{1,0:T(8,128)} %param.9) | copy-start | bytes 9437188
  114.6 1.3 collective-permute-start.2
  121.5 4.3 %copy-start.2 = (f32[1024,768]{1,0:T(8,128)S(1)}, f32[1024,768]{1,0:T(8,128)}, u32[]{:S(2)}) copy-start(f32[1024,768]{1,0:T(8,128)} %get-tuple-element.12) | copy-start | bytes 9437188
  121.5 2.9 %collective-permute-start.3 = (bf16[768,768]{1,0:T(8,128)(2,1)S(1)}, bf16[768,768]{1,0:T(8,128)(2,1)S(1)}, u32[]{:S(2)}, u32[]{:S(2)}) collective-permute-start(bf16[768,768]{1,0:T(8,128)(2,1)S(1)} %convolution_convert_fusion.1), channel_id=1, source_target_pairs={{0,4},{4,0},{1,5},{5,1},{2,6},{6,2},{3,7},{7,3},{8,12},{12,8},{9,1... | collective-permute-start | bytes 3538952 | tf_op jit(solution)/shard_map/ppermute | solution.py:58
  128.8 2.9 %collective-permute-start.4 = (bf16[768,768]{1,0:T(8,128)(2,1)S(1)}, bf16[768,768]{1,0:T(8,128)(2,1)S(1)}, u32[]{:S(2)}, u32[]{:S(2)}) collective-permute-start(bf16[768,768]{1,0:T(8,128)(2,1)S(1)} %convolution_convert_fusion), channel_id=1, source_target_pairs={{0,4},{4,0},{1,5},{5,1},{2,6},{6,2},{3,7},{7,3},{8,12},{12,8},{9,1... | collective-permute-start | bytes 3538952 | tf_op jit(solution)/shard_map/ppermute | solution.py:58
Sparse Core Ops, SparseCore 0:
  11.5 92.5 all-gather.2

commit v13 on v9

--- a/solution.py
+++ b/solution.py
@@ -100,8 +100,8 @@
 
     grad_all, got_hidden = lax.optimization_barrier((grad_all, got_hidden))
     gradient = lax.dot_general(
-        grad_all, got_hidden, (((0,), (0,)), ((), ())), preferred_element_type=jnp.float32
-    )
+        got_hidden, grad_all, (((0,), (0,)), ((), ())), preferred_element_type=jnp.float32
+    ).T
     gradient = lax.optimization_barrier(gradient)
 
     new_momentum = MOMENT * momentum + gradient

time: 142 us -> 142 us (level)
  no operation moved by 1% of the time
where the time goes in v13:
time: 142 us
  blocking collectives  61.5 us (43%)
  waiting for transfers between devices  32.5 us (23%)
  matrix products  17.1 us (12%)
  between operations  15.6 us (11%)
  other arithmetic  9.9 us (7%)
  local copies, waits for them, and re-layouts  4.46 us (3%)
    all_to_all x1, blocking collectives, body(): lax.all_to_all(scaled_hidden, ('zhi', 'expert'), split_axis=0, concat_axi...  61.5 us
    all_gather x1, waiting for transfers between devices, body(): grad_all = lax.all_gather(grad_mine, ('zhi', 'expert'), axis=1, tiled=False)  21.6 us
    ppermute x3, waiting for transfers between devices, group_sum(): total = total + lax.ppermute(sent, axes, route).astype(value.dtype)  6.58 us
    dot_general x1, matrix products, body(): lax.dot_general(got_hidden, grad_all, (((0,), (0,)), ((), ())), preferred...  6.4 us
    dot_general x2, matrix products, newton_update(): product = jnp.dot(scaled, poly, preferred_element_type=jnp.float32)  3.97 us
    ppermute x1, waiting for transfers between devices, group_gather(): parts.append(lax.ppermute(block, axes, route))  3.41 us
    convert_element_type x1, other arithmetic, body(): scaled = (ahead / (norm_value + EPSILON)).astype(jnp.bfloat16)  3.29 us
    reduce_sum x1, other arithmetic, body(): square_sum = group_sum(jnp.sum(ahead * ahead), group, group_size)  3.29 us
  transfers between devices with their start and end apart: 6, of which 6 were waited for; matrix products, arithmetic and copies ran while one was open for 4% of the time, Pallas kernels for 0%

profile of v13, /device:TPU:0, one launch (start us, length us, event | category | flops | bytes accessed | tf_op | source)
XLA Modules:
  0.0 142.1 jit_solution(4336360466863545494)
XLA Ops:
  7.2 0.0 copy-start
  7.2 0.0 copy-start.3
  7.2 0.0 copy-start.4
  7.2 0.0 all-gather.3.cloned.1.call-start
  7.3 1.2 reshape.64
  8.5 0.6 constant_dynamic-slice_fusion.1
  9.1 0.6 collective-permute-start
  9.7 0.9 collective-permute-done
  10.6 0.7 pad_maximum_fusion.1
  11.4 0.0 all-gather.3.cloned.1.call-update
  11.4 0.0 copy-done.3
  11.4 0.0 copy-done.4
  11.4 0.1 mul.44
  11.5 0.6 broadcast_and_fusion
  12.2 2.4 %and.34 = pred[1024,512]{0,1:T(32,128)(4,1)S(1)} reshape(pred[16,64,64,8]{1,0,3,2:T(8,128)(4,1)S(1)} %broadcast_and_fusion) | data formatting | bytes 1048576 | tf_op jit(solution)/shard_map/and | solution.py:87
  14.5 0.0 copy-done
  14.6 1.0 multiply_convert_fusion.1
  15.6 0.1 copy.16
  15.7 61.5 %all_to_all.5 = bf16[16,64,768]{2,1,0:T(8,128)(2,1)S(1)} all-to-all(bf16[16,64,768]{2,1,0:T(8,128)(2,1)S(1)} %bitcast.34), channel_id=1, replica_groups=mesh['zhi'=4,'zlo'=1,'core'=2,'expert'=4] {'zhi','expert'}, dimensions={0} | all-to-all | bytes 3145728 | tf_op jit(solution)/shard_map/all_to_all | solution.py:95
  77.2 0.0 collective-permute-start.1
  77.2 3.4 %collective-permute-done.1 = bf16[16,64,768]{2,1,0:T(8,128)(2,1)S(1)} collective-permute-done((bf16[16,64,768]{2,1,0:T(8,128)(2,1)S(1)}, bf16[16,64,768]{2,1,0:T(8,128)(2,1)S(1)}, u32[]{:S(2)}, u32[]{:S(2)}) %collective-permute-start.1) | collective-permute-done | bytes 1572896 | tf_op jit(solution)/shard_map/ppermute | solution.py:39
  80.6 1.9 %pad_maximum_fusion = bf16[2,16,64,768]{3,2,1,0:T(8,128)(2,1)} fusion(bf16[1,16,64,768]{3,2,1,0:T(8,128)(2,1)S(1)} %bitcast.38, bf16[1,16,64,768]{3,2,1,0:T(8,128)(2,1)S(1)} %bitcast.35), kind=kLoop, calls=%fused_computation | loop fusion | flops 1572864 | bytes 6291456 | tf_op jit(solution)/shard_map/stack | solution.py:40
  82.6 21.6 %all-gather.3.cloned.1.call-done = bf16[2,1024,1024]{2,1,0:T(8,128)(2,1)} async-done(((bf16[2,64,1024]{2,1,0:T(8,128)(2,1)}), bf16[2,1024,1024]{2,1,0:T(8,128)(2,1)}) %all-gather.3.cloned.1.call-update) | async-done | bytes 4194320 | tf_op jit(solution)/shard_map/all_gather | solution.py:77
  104.1 0.0 copy-start.2
  104.1 6.4 %fusion.1 = f32[1024,768]{1,0:T(8,128)S(1)} fusion(bf16[2048,1024]{1,0:T(8,128)(2,1)} %bitcast.43, bf16[2048,768]{1,0:T(8,128)(2,1)} %bitcast.36), kind=kOutput, calls=%fused_computation.26 | convolution fusion | flops 3221225472 | bytes 10485760 | tf_op jit(solution)/shard_map/dot_general | solution.py:102
  110.6 0.0 copy-done.2
  110.6 0.0 copy-start.1
  110.6 3.3 %multiply_reduce_fusion = (f32[]{:T(128)}, f32[1024,768]{1,0:T(8,128)}) fusion(f32[1024,768]{1,0:T(8,128)S(1)} %fusion.1, f32[1024,768]{1,0:T(8,128)S(1)} %copy-done.2), kind=kLoop, calls=%fused_computation.5 | loop fusion | flops 4718591 | bytes 9437188 | tf_op jit(solution)/shard_map/reduce_sum | solution.py:109
  113.9 0.0 copy-done.1
  113.9 0.0 collective-permute-start.2
  113.9 1.3 collective-permute-done.2
  116.5 3.3 %divide_convert_fusion = bf16[1024,768]{1,0:T(8,128)(2,1)S(1)} fusion(f32[]{:T(128)S(6)} %add.52, f32[1024,768]{1,0:T(8,128)} %copy-done.1, f32[1024,768]{1,0:T(8,128)} %get-tuple-element.11), kind=kLoop, calls=%fused_computation.4 | loop fusion | flops 3145728 | bytes 7864324 | tf_op jit(solution)/shard_map/convert_element_type | solution.py:111
  119.8 1.4 %convolution_convert_fusion.1 = bf16[768,768]{1,0:T(8,128)(2,1)S(1)} fusion(bf16[1024,768]{1,0:T(8,128)(2,1)S(1)} %divide_convert_fusion), kind=kOutput, calls=%fused_computation.15 | convolution fusion | flops 1208549376 | bytes 2752512 | tf_op jit(solution)/shard_map/dot_general | solution.py:30
  121.2 0.3 collective-permute-start.3
  121.5 2.7 %collective-permute-done.3 = bf16[768,768]{1,0:T(8,128)(2,1)S(1)} collective-permute-done((bf16[768,768]{1,0:T(8,128)(2,1)S(1)}, bf16[768,768]{1,0:T(8,128)(2,1)S(1)}, u32[]{:S(2)}, u32[]{:S(2)}) %collective-permute-start.3) | collective-permute-done | bytes 1179680 | tf_op jit(solution)/shard_map/ppermute | solution.py:58
  124.1 1.4 add_convert_fusion.4
  125.5 1.4 add_convert_fusion.1
  126.9 1.5 %convolution_convert_fusion = bf16[768,768]{1,0:T(8,128)(2,1)S(1)} fusion(bf16[1024,768]{1,0:T(8,128)(2,1)S(1)} %add_convert_fusion.1), kind=kOutput, calls=%fused_computation.14 | convolution fusion | flops 1208549376 | bytes 2752512 | tf_op jit(solution)/shard_map/dot_general | solution.py:30
  128.4 0.3 collective-permute-start.4
  128.6 2.7 %collective-permute-done.4 = bf16[768,768]{1,0:T(8,128)(2,1)S(1)} collective-permute-done((bf16[768,768]{1,0:T(8,128)(2,1)S(1)}, bf16[768,768]{1,0:T(8,128)(2,1)S(1)}, u32[]{:S(2)}, u32[]{:S(2)}) %collective-permute-start.4) | collective-permute-done | bytes 1179680 | tf_op jit(solution)/shard_map/ppermute | solution.py:58
  131.3 1.4 add_convert_fusion.2
  132.7 2.6 %multiply_convert_fusion = bf16[1024,768]{1,0:T(8,128)(2,1)} fusion(bf16[1024,768]{1,0:T(8,128)(2,1)S(1)} %add_convert_fusion.1, bf16[768,768]{1,0:T(8,128)(2,1)S(1)} %add_convert_fusion.2), kind=kOutput, calls=%fused_computation.1 | convolution fusion | flops 1213464576 | bytes 4325376 | tf_op jit(solution)/shard_map/dot_general | solution.py:25
  (5 shorter events, 0.1 us)
Async XLA Ops:
  7.2 7.4 %copy-start = (bf16[64,8,768]{2,1,0:T(8,128)(2,1)S(1)}, bf16[64,8,768]{2,1,0:T(8,128)(2,1)}, u32[]{:S(2)}) copy-start(bf16[64,8,768]{2,1,0:T(8,128)(2,1)} %param.5) | copy-start | bytes 2359300
  7.2 4.2 %copy-start.3 = (s32[64,8]{0,1:T(8,128)S(1)}, s32[64,8]{0,1:T(8,128)}, u32[]{:S(2)}) copy-start(s32[64,8]{0,1:T(8,128)} %param.8) | copy-start | bytes 6148
  7.2 4.2 %copy-start.4 = (f32[64,8]{0,1:T(8,128)S(1)}, f32[64,8]{0,1:T(8,128)}, u32[]{:S(2)}) copy-start(f32[64,8]{0,1:T(8,128)} %param.7) | copy-start | bytes 6148
  7.2 96.9 %all-gather.3.cloned.1.call-start = ((), (), s32[]{:S(2)}) async-start(), calls=%async_computation.1 | async-start | bytes 4456448 | tf_op jit(solution)/shard_map/all_gather | solution.py:77
  9.1 1.5 %collective-permute-start = (bf16[64,1024]{1,0:T(8,128)(2,1)S(1)}, bf16[64,1024]{1,0:T(8,128)(2,1)S(1)}, u32[]{:S(2)}, u32[]{:S(2)}) collective-permute-start(bf16[64,1024]{1,0:T(8,128)(2,1)S(1)} %bitcast.40), channel_id=1, source_target_pairs={{0,4},{4,0},{1,5},{5,1},{2,6},{6,2},{3,7},{7,3},{8,12},{12,8},{9,1... | collective-permute-start | bytes 393224 | tf_op jit(solution)/shard_map/ppermute | solution.py:49
  77.2 3.4 %collective-permute-start.1 = (bf16[16,64,768]{2,1,0:T(8,128)(2,1)S(1)}, bf16[16,64,768]{2,1,0:T(8,128)(2,1)S(1)}, u32[]{:S(2)}, u32[]{:S(2)}) collective-permute-start(bf16[16,64,768]{2,1,0:T(8,128)(2,1)S(1)} %all_to_all.5), channel_id=1, source_target_pairs={{0,4},{4,0},{1,5},{5,1},{2,6},{6,2},{3,7},{7,3},{8,12},{12,8},{9,1... | collective-permute-start | bytes 4718600 | tf_op jit(solution)/shard_map/ppermute | solution.py:39
  104.1 6.4 %copy-start.2 = (f32[1024,768]{1,0:T(8,128)S(1)}, f32[1024,768]{1,0:T(8,128)}, u32[]{:S(2)}) copy-start(f32[1024,768]{1,0:T(8,128)} %param.9) | copy-start | bytes 9437188
  110.6 3.3 %copy-start.1 = (f32[1024,768]{1,0:T(8,128)}, f32[1024,768]{1,0:T(8,128)S(1)}, u32[]{:S(2)}) copy-start(f32[1024,768]{1,0:T(8,128)S(1)} %fusion.1) | copy-start | bytes 9437188
  113.9 1.3 collective-permute-start.2
  121.2 2.9 %collective-permute-start.3 = (bf16[768,768]{1,0:T(8,128)(2,1)S(1)}, bf16[768,768]{1,0:T(8,128)(2,1)S(1)}, u32[]{:S(2)}, u32[]{:S(2)}) collective-permute-start(bf16[768,768]{1,0:T(8,128)(2,1)S(1)} %convolution_convert_fusion.1), channel_id=1, source_target_pairs={{0,4},{4,0},{1,5},{5,1},{2,6},{6,2},{3,7},{7,3},{8,12},{12,8},{9,1... | collective-permute-start | bytes 3538952 | tf_op jit(solution)/shard_map/ppermute | solution.py:58
  128.4 2.9 %collective-permute-start.4 = (bf16[768,768]{1,0:T(8,128)(2,1)S(1)}, bf16[768,768]{1,0:T(8,128)(2,1)S(1)}, u32[]{:S(2)}, u32[]{:S(2)}) collective-permute-start(bf16[768,768]{1,0:T(8,128)(2,1)S(1)} %convolution_convert_fusion), channel_id=1, source_target_pairs={{0,4},{4,0},{1,5},{5,1},{2,6},{6,2},{3,7},{7,3},{8,12},{12,8},{9,1... | collective-permute-start | bytes 3538952 | tf_op jit(solution)/shard_map/ppermute | solution.py:58
Sparse Core Ops, SparseCore 0:
  11.5 92.5 all-gather.2

commit v14 on v9

--- a/solution.py
+++ b/solution.py
@@ -107,10 +107,15 @@
     new_momentum = MOMENT * momentum + gradient
     ahead = gradient + MOMENT * new_momentum
     square_sum = group_sum(jnp.sum(ahead * ahead), group, group_size)
+    raw_gram = group_sum(gram_of(ahead.astype(jnp.bfloat16)), group, group_size, jnp.bfloat16)
     norm_value = jnp.sqrt(square_sum)
     scaled = (ahead / (norm_value + EPSILON)).astype(jnp.bfloat16)
+    inverse = 1.0 / (norm_value + EPSILON)
     for turn_index in range(NS_ITERS):
-        gram = group_sum(gram_of(scaled), group, group_size, jnp.bfloat16).astype(jnp.bfloat16)
+        if turn_index == 0:
+            gram = (raw_gram * (inverse * inverse)).astype(jnp.bfloat16)
+        else:
+            gram = group_sum(gram_of(scaled), group, group_size, jnp.bfloat16).astype(jnp.bfloat16)
         scaled = newton_update(scaled, gram)
     update = (math.sqrt(model_width) * scaled.astype(jnp.float32)).astype(jnp.bfloat16)
     return (update, new_momentum)

time: 142 us -> 138 us (0.972)
  other arithmetic: 9.9 us -> 4.86 us
    convert_element_type x1 -> x0, other arithmetic: 3.29 us -> none  [body(): scaled = (ahead / (norm_value + EPSILON)).astype(jnp.bfloat16)]
    reduce_sum x1, other arithmetic: 3.29 us -> 1.54 us  [body(): square_sum = group_sum(jnp.sum(ahead * ahead), group, group_size)]
  transfers between devices with their start and end apart: 6 -> 6, of which waited for: 6 -> 5; matrix products, arithmetic and copies ran while one was open for 4% -> 5% of each run, Pallas kernels for 0% -> 0%
where the time goes in v14:
time: 138 us
  blocking collectives  61.5 us (45%)
  waiting for transfers between devices  31.1 us (23%)
  matrix products  17.5 us (13%)
  between operations  15.6 us (11%)
  local copies, waits for them, and re-layouts  5.87 us (4%)
  other arithmetic  4.86 us (4%)
    all_to_all x1, blocking collectives, body(): lax.all_to_all(scaled_hidden, ('zhi', 'expert'), split_axis=0, concat_axi...  61.5 us
    all_gather x1, waiting for transfers between devices, body(): grad_all = lax.all_gather(grad_mine, ('zhi', 'expert'), axis=1, tiled=False)  21.6 us
    dot_general x1, matrix products, body(): lax.dot_general(grad_all, got_hidden, (((0,), (0,)), ((), ())), preferred...  6.39 us
    ppermute x3, waiting for transfers between devices, group_sum(): total = total + lax.ppermute(sent, axes, route).astype(value.dtype)  5.18 us
    dot_general x2, matrix products, newton_update(): product = jnp.dot(scaled, poly, preferred_element_type=jnp.float32)  4.15 us
    ppermute x1, waiting for transfers between devices, group_gather(): parts.append(lax.ppermute(block, axes, route))  3.41 us
    dot_general x2, matrix products, gram_of(): lax.dot_general(scaled, scaled, (((0,), (0,)), ((), ())), preferred_eleme...  2.94 us
    dot_general x2, matrix products, newton_update(): square = jnp.dot(gram, gram, preferred_element_type=jnp.float32)  2.94 us
  transfers between devices with their start and end apart: 6, of which 5 were waited for; matrix products, arithmetic and copies ran while one was open for 5% of the time, Pallas kernels for 0%

profile of v14, /device:TPU:0, one launch (start us, length us, event | category | flops | bytes accessed | tf_op | source)
XLA Modules:
  0.0 137.7 jit_solution(9209909190889194968)
XLA Ops:
  7.2 0.0 copy-start
  7.2 0.0 copy-start.6
  7.2 0.0 copy-start.7
  7.2 0.0 all-gather.3.cloned.1.call-start
  7.3 1.2 reshape.64
  8.5 0.6 constant_dynamic-slice_fusion.1
  9.1 0.6 collective-permute-start
  9.7 0.9 collective-permute-done
  10.6 0.7 pad_maximum_fusion.1
  11.4 0.0 all-gather.3.cloned.1.call-update
  11.4 0.0 copy-done.6
  11.4 0.0 copy-done.7
  11.4 0.1 mul.53
  11.5 0.6 broadcast_and_fusion
  12.2 2.4 %and.34 = pred[1024,512]{0,1:T(32,128)(4,1)S(1)} reshape(pred[16,64,64,8]{1,0,3,2:T(8,128)(4,1)S(1)} %broadcast_and_fusion) | data formatting | bytes 1048576 | tf_op jit(solution)/shard_map/and | solution.py:87
  14.5 0.0 copy-done
  14.6 1.0 multiply_convert_fusion.1
  15.6 0.1 copy.16
  15.7 61.5 %all_to_all.5 = bf16[16,64,768]{2,1,0:T(8,128)(2,1)S(1)} all-to-all(bf16[16,64,768]{2,1,0:T(8,128)(2,1)S(1)} %bitcast.31), channel_id=1, replica_groups=mesh['zhi'=4,'zlo'=1,'core'=2,'expert'=4] {'zhi','expert'}, dimensions={0} | all-to-all | bytes 3145728 | tf_op jit(solution)/shard_map/all_to_all | solution.py:95
  77.2 0.0 collective-permute-start.1
  77.2 3.4 %collective-permute-done.1 = bf16[16,64,768]{2,1,0:T(8,128)(2,1)S(1)} collective-permute-done((bf16[16,64,768]{2,1,0:T(8,128)(2,1)S(1)}, bf16[16,64,768]{2,1,0:T(8,128)(2,1)S(1)}, u32[]{:S(2)}, u32[]{:S(2)}) %collective-permute-start.1) | collective-permute-done | bytes 1572896 | tf_op jit(solution)/shard_map/ppermute | solution.py:39
  80.6 1.9 %pad_maximum_fusion = bf16[2,16,64,768]{3,2,1,0:T(8,128)(2,1)} fusion(bf16[1,16,64,768]{3,2,1,0:T(8,128)(2,1)S(1)} %bitcast.35, bf16[1,16,64,768]{3,2,1,0:T(8,128)(2,1)S(1)} %bitcast.32), kind=kLoop, calls=%fused_computation | loop fusion | flops 1572864 | bytes 6291456 | tf_op jit(solution)/shard_map/stack | solution.py:40
  82.6 21.6 %all-gather.3.cloned.1.call-done = bf16[2,1024,1024]{2,1,0:T(8,128)(2,1)} async-done(((bf16[2,64,1024]{2,1,0:T(8,128)(2,1)}), bf16[2,1024,1024]{2,1,0:T(8,128)(2,1)}) %all-gather.3.cloned.1.call-update) | async-done | bytes 4194320 | tf_op jit(solution)/shard_map/all_gather | solution.py:77
  104.1 0.0 copy-start.1
  104.1 6.4 %fusion.8 = f32[1024,768]{1,0:T(8,128)S(1)} fusion(bf16[2048,1024]{1,0:T(8,128)(2,1)} %bitcast.40, bf16[2048,768]{1,0:T(8,128)(2,1)} %bitcast.33), kind=kOutput, calls=%fused_computation.30 | convolution fusion | flops 3221225472 | bytes 10485760 | tf_op jit(solution)/shard_map/dot_general | solution.py:102
  110.5 0.0 copy-done.1
  110.6 0.0 copy-start.4
  110.6 1.5 %multiply_reduce_fusion = (f32[]{:T(128)}, f32[1024,768]{1,0:T(8,128)S(1)}) fusion(f32[1024,768]{1,0:T(8,128)S(1)} %fusion.8, f32[1024,768]{1,0:T(8,128)S(1)} %copy-done.1), kind=kLoop, calls=%fused_computation.5 | loop fusion | flops 4718591 | bytes 9437188 | tf_op jit(solution)/shard_map/reduce_sum | solution.py:109
  112.1 0.0 copy-start.2
  112.1 0.1 copy-done.4
  112.2 1.5 %fusion.3 = bf16[768,768]{1,0:T(8,128)(2,1)S(1)} fusion(f32[1024,768]{1,0:T(8,128)S(1)} %fusion.8, f32[1024,768]{1,0:T(8,128)S(1)} %get-tuple-element.11), kind=kOutput, calls=%fused_computation.17 | convolution fusion | flops 1210908672 | bytes 7471104 | tf_op jit(solution)/shard_map/dot_general | solution.py:30
  113.7 0.1 copy-done.2
  113.8 0.0 collective-permute-start.3
  113.8 0.5 collective-permute-start.2
  114.3 2.5 %collective-permute-done.2 = f32[]{:T(128)} collective-permute-done((f32[]{:T(128)}, f32[]{:T(128)}, u32[]{:S(2)}, u32[]{:S(2)}) %collective-permute-start.2) | collective-permute-done | bytes 36 | tf_op jit(solution)/shard_map/ppermute | solution.py:58
  118.1 0.0 copy-start.3
  118.1 0.0 copy-start.5
  118.1 0.0 collective-permute-done.3
  118.1 1.6 %add_convert_fusion.4 = bf16[768,768]{1,0:T(8,128)(2,1)S(1)} fusion(bf16[768,768]{1,0:T(8,128)(2,1)S(1)} %collective-permute-done.3, bf16[768,768]{1,0:T(8,128)(2,1)S(1)} %fusion.3, f32[]{:T(128)S(6)} %mul.60), kind=kOutput, calls=%fused_computation.11 | convolution fusion | flops 914817024 | bytes 3538948 | tf_op jit(solution)/shard_map/dot_general | solution.py:22
  119.7 0.3 copy-done.3
  120.0 1.0 copy-done.5
  121.0 1.6 %add_convert_fusion.1 = bf16[1024,768]{1,0:T(8,128)(2,1)S(1)} fusion(bf16[768,768]{1,0:T(8,128)(2,1)S(1)} %add_convert_fusion.4, f32[]{:T(128)S(6)} %add.53, f32[1024,768]{1,0:T(8,128)S(1)} %copy-done.5, f32[1024,768]{1,0:T(8,128)S(1)} %copy-done.3), kind=kOutput, calls=%fused_computation.3 | convolution fusion | flops 1217396736 | bytes 9043972 | tf_op jit(solution)/shard_map/dot_general | solution.py:25
  122.6 1.4 %convolution_convert_fusion = bf16[768,768]{1,0:T(8,128)(2,1)S(1)} fusion(bf16[1024,768]{1,0:T(8,128)(2,1)S(1)} %add_convert_fusion.1), kind=kOutput, calls=%fused_computation.18 | convolution fusion | flops 1208549376 | bytes 2752512 | tf_op jit(solution)/shard_map/dot_general | solution.py:30
  124.0 0.2 collective-permute-start.4
  124.2 2.7 %collective-permute-done.4 = bf16[768,768]{1,0:T(8,128)(2,1)S(1)} collective-permute-done((bf16[768,768]{1,0:T(8,128)(2,1)S(1)}, bf16[768,768]{1,0:T(8,128)(2,1)S(1)}, u32[]{:S(2)}, u32[]{:S(2)}) %collective-permute-start.4) | collective-permute-done | bytes 1179680 | tf_op jit(solution)/shard_map/ppermute | solution.py:58
  126.9 1.4 %add_convert_fusion.2 = bf16[768,768]{1,0:T(8,128)(2,1)S(1)} fusion(bf16[768,768]{1,0:T(8,128)(2,1)S(1)} %collective-permute-done.4, bf16[768,768]{1,0:T(8,128)(2,1)S(1)} %convolution_convert_fusion), kind=kOutput, calls=%fused_computation.9 | convolution fusion | flops 913637376 | bytes 3538944 | tf_op jit(solution)/shard_map/dot_general | solution.py:22
  128.3 2.6 %multiply_convert_fusion = bf16[1024,768]{1,0:T(8,128)(2,1)} fusion(bf16[1024,768]{1,0:T(8,128)(2,1)S(1)} %add_convert_fusion.1, bf16[768,768]{1,0:T(8,128)(2,1)S(1)} %add_convert_fusion.2), kind=kOutput, calls=%fused_computation.1 | convolution fusion | flops 1213464576 | bytes 4325376 | tf_op jit(solution)/shard_map/dot_general | solution.py:25
  (5 shorter events, 0.1 us)
Async XLA Ops:
  7.2 7.4 %copy-start = (bf16[64,8,768]{2,1,0:T(8,128)(2,1)S(1)}, bf16[64,8,768]{2,1,0:T(8,128)(2,1)}, u32[]{:S(2)}) copy-start(bf16[64,8,768]{2,1,0:T(8,128)(2,1)} %param.5) | copy-start | bytes 2359300
  7.2 4.2 %copy-start.6 = (s32[64,8]{0,1:T(8,128)S(1)}, s32[64,8]{0,1:T(8,128)}, u32[]{:S(2)}) copy-start(s32[64,8]{0,1:T(8,128)} %param.8) | copy-start | bytes 6148
  7.2 4.2 %copy-start.7 = (f32[64,8]{0,1:T(8,128)S(1)}, f32[64,8]{0,1:T(8,128)}, u32[]{:S(2)}) copy-start(f32[64,8]{0,1:T(8,128)} %param.7) | copy-start | bytes 6148
  7.2 96.9 %all-gather.3.cloned.1.call-start = ((), (), s32[]{:S(2)}) async-start(), calls=%async_computation.1 | async-start | bytes 4456448 | tf_op jit(solution)/shard_map/all_gather | solution.py:77
  9.1 1.5 %collective-permute-start = (bf16[64,1024]{1,0:T(8,128)(2,1)S(1)}, bf16[64,1024]{1,0:T(8,128)(2,1)S(1)}, u32[]{:S(2)}, u32[]{:S(2)}) collective-permute-start(bf16[64,1024]{1,0:T(8,128)(2,1)S(1)} %bitcast.37), channel_id=1, source_target_pairs={{0,4},{4,0},{1,5},{5,1},{2,6},{6,2},{3,7},{7,3},{8,12},{12,8},{9,1... | collective-permute-start | bytes 393224 | tf_op jit(solution)/shard_map/ppermute | solution.py:49
  77.2 3.4 %collective-permute-start.1 = (bf16[16,64,768]{2,1,0:T(8,128)(2,1)S(1)}, bf16[16,64,768]{2,1,0:T(8,128)(2,1)S(1)}, u32[]{:S(2)}, u32[]{:S(2)}) collective-permute-start(bf16[16,64,768]{2,1,0:T(8,128)(2,1)S(1)} %all_to_all.5), channel_id=1, source_target_pairs={{0,4},{4,0},{1,5},{5,1},{2,6},{6,2},{3,7},{7,3},{8,12},{12,8},{9,1... | collective-permute-start | bytes 4718600 | tf_op jit(solution)/shard_map/ppermute | solution.py:39
  104.1 6.4 %copy-start.1 = (f32[1024,768]{1,0:T(8,128)S(1)}, f32[1024,768]{1,0:T(8,128)}, u32[]{:S(2)}) copy-start(f32[1024,768]{1,0:T(8,128)} %param.9) | copy-start | bytes 9437188
  110.6 1.6 %copy-start.4 = (f32[1024,768]{1,0:T(8,128)}, f32[1024,768]{1,0:T(8,128)S(1)}, u32[]{:S(2)}) copy-start(f32[1024,768]{1,0:T(8,128)S(1)} %fusion.8) | copy-start | bytes 9437188
  112.1 1.7 %copy-start.2 = (f32[1024,768]{1,0:T(8,128)}, f32[1024,768]{1,0:T(8,128)S(1)}, u32[]{:S(2)}) copy-start(f32[1024,768]{1,0:T(8,128)S(1)} %get-tuple-element.11) | copy-start | bytes 9437188
  113.8 4.4 %collective-permute-start.3 = (bf16[768,768]{1,0:T(8,128)(2,1)S(1)}, bf16[768,768]{1,0:T(8,128)(2,1)S(1)}, u32[]{:S(2)}, u32[]{:S(2)}) collective-permute-start(bf16[768,768]{1,0:T(8,128)(2,1)S(1)} %fusion.3), channel_id=1, source_target_pairs={{0,4},{4,0},{1,5},{5,1},{2,6},{6,2},{3,7},{7,3},{8,12},{12,8},{9,1... | collective-permute-start | bytes 3538952 | tf_op jit(solution)/shard_map/ppermute | solution.py:58
  113.8 3.0 %collective-permute-start.2 = (f32[]{:T(128)}, f32[]{:T(128)}, u32[]{:S(2)}, u32[]{:S(2)}) collective-permute-start(f32[]{:T(128)} %get-tuple-element.10), channel_id=1, source_target_pairs={{0,4},{4,0},{1,5},{5,1},{2,6},{6,2},{3,7},{7,3},{8,12},{12,8},{9,1... | collective-permute-start | bytes 20 | tf_op jit(solution)/shard_map/ppermute | solution.py:58
  118.1 1.9 %copy-start.3 = (f32[1024,768]{1,0:T(8,128)S(1)}, f32[1024,768]{1,0:T(8,128)}, u32[]{:S(2)}) copy-start(f32[1024,768]{1,0:T(8,128)} %copy-done.2) | copy-start | bytes 9437188
  118.1 2.8 %copy-start.5 = (f32[1024,768]{1,0:T(8,128)S(1)}, f32[1024,768]{1,0:T(8,128)}, u32[]{:S(2)}) copy-start(f32[1024,768]{1,0:T(8,128)} %copy-done.4) | copy-start | bytes 9437188
  124.0 2.9 %collective-permute-start.4 = (bf16[768,768]{1,0:T(8,128)(2,1)S(1)}, bf16[768,768]{1,0:T(8,128)(2,1)S(1)}, u32[]{:S(2)}, u32[]{:S(2)}) collective-permute-start(bf16[768,768]{1,0:T(8,128)(2,1)S(1)} %convolution_convert_fusion), channel_id=1, source_target_pairs={{0,4},{4,0},{1,5},{5,1},{2,6},{6,2},{3,7},{7,3},{8,12},{12,8},{9,1... | collective-permute-start | bytes 3538952 | tf_op jit(solution)/shard_map/ppermute | solution.py:58
Sparse Core Ops, SparseCore 0:
  11.5 92.5 all-gather.2

commit v15 on v14

--- a/solution.py
+++ b/solution.py
@@ -30,6 +30,18 @@
     return lax.dot_general(
         scaled, scaled, (((0,), (0,)), ((), ())), preferred_element_type=jnp.float32
     )
+
+
+def gram_sum(scaled, axes, count):
+    width = scaled.shape[1]
+    halves = []
+    for begin in (0, width // 2):
+        part = lax.dot_general(
+            scaled, scaled[:, begin:begin + width // 2], (((0,), (0,)), ((), ())),
+            preferred_element_type=jnp.float32,
+        )
+        halves.append(group_sum(part, axes, count, jnp.bfloat16))
+    return jnp.concatenate(halves, axis=1)
 
 
 def group_gather(block, axes, count):
@@ -107,7 +119,7 @@
     new_momentum = MOMENT * momentum + gradient
     ahead = gradient + MOMENT * new_momentum
     square_sum = group_sum(jnp.sum(ahead * ahead), group, group_size)
-    raw_gram = group_sum(gram_of(ahead.astype(jnp.bfloat16)), group, group_size, jnp.bfloat16)
+    raw_gram = gram_sum(ahead.astype(jnp.bfloat16), group, group_size)
     norm_value = jnp.sqrt(square_sum)
     scaled = (ahead / (norm_value + EPSILON)).astype(jnp.bfloat16)
     inverse = 1.0 / (norm_value + EPSILON)
@@ -115,7 +127,7 @@
         if turn_index == 0:
             gram = (raw_gram * (inverse * inverse)).astype(jnp.bfloat16)
         else:
-            gram = group_sum(gram_of(scaled), group, group_size, jnp.bfloat16).astype(jnp.bfloat16)
+            gram = gram_sum(scaled, group, group_size).astype(jnp.bfloat16)
         scaled = newton_update(scaled, gram)
     update = (math.sqrt(model_width) * scaled.astype(jnp.float32)).astype(jnp.bfloat16)
     return (update, new_momentum)

time: 138 us -> 139 us (level)
  waiting for transfers between devices: 31.1 us -> 29.2 us
  local copies, waits for them, and re-layouts: 5.87 us -> 7.31 us
    ppermute x3 -> x5, waiting for transfers between devices: 5.18 us -> 3.28 us  [group_sum(): total = total + lax.ppermute(sent, axes, route).astype(value.dtype)]
    unnamed x18, local copies, waits for them, and re-layouts: 1.53 us -> 2.97 us
    dot_general x2 -> x4, matrix products: 2.94 us -> 3.34 us  [gram_sum(): lax.dot_general(scaled, scaled[:, begin:begin + width // 2], (((0,), (0,)...]
  transfers between devices with their start and end apart: 6 -> 8, of which waited for: 5 -> 6; matrix products, arithmetic and copies ran while one was open for 5% -> 6% of each run, Pallas kernels for 0% -> 0%
where the time goes in v15:
time: 139 us
  blocking collectives  61.5 us (44%)
  waiting for transfers between devices  29.2 us (21%)
  matrix products  17.4 us (13%)
  between operations  15.7 us (11%)
  local copies, waits for them, and re-layouts  7.31 us (5%)
  other arithmetic  5.83 us (4%)
  starting transfers between devices  1.95 us (1%)
    all_to_all x1, blocking collectives, body(): lax.all_to_all(scaled_hidden, ('zhi', 'expert'), split_axis=0, concat_axi...  61.5 us
    all_gather x1, waiting for transfers between devices, body(): grad_all = lax.all_gather(grad_mine, ('zhi', 'expert'), axis=1, tiled=False)  21.6 us
    dot_general x1, matrix products, body(): lax.dot_general(grad_all, got_hidden, (((0,), (0,)), ((), ())), preferred...  6.39 us
    dot_general x2, matrix products, newton_update(): product = jnp.dot(scaled, poly, preferred_element_type=jnp.float32)  4.35 us
    ppermute x1, waiting for transfers between devices, group_gather(): parts.append(lax.ppermute(block, axes, route))  3.41 us
    dot_general x4, matrix products, gram_sum(): lax.dot_general(scaled, scaled[:, begin:begin + width // 2], (((0,), (0,)...  3.34 us
    ppermute x5, waiting for transfers between devices, group_sum(): total = total + lax.ppermute(sent, axes, route).astype(value.dtype)  3.28 us
    unnamed x18, local copies, waits for them, and re-layouts  2.97 us
  transfers between devices with their start and end apart: 8, of which 6 were waited for; matrix products, arithmetic and copies ran while one was open for 6% of the time, Pallas kernels for 0%

profile of v15, /device:TPU:0, one launch (start us, length us, event | category | flops | bytes accessed | tf_op | source)
XLA Modules:
  0.0 138.9 jit_solution(3259913792936354105)
XLA Ops:
  7.2 0.0 copy-start
  7.2 0.0 all-gather.3.cloned.1.call-start
  7.3 1.2 reshape.64
  8.5 0.6 constant_dynamic-slice_fusion.1
  9.1 0.6 collective-permute-start
  9.7 0.9 collective-permute-done
  10.6 0.7 pad_maximum_fusion.1
  11.4 0.0 all-gather.3.cloned.1.call-update
  11.4 0.1 mul.53
  11.5 0.6 broadcast_and_fusion
  12.2 2.4 %and.34 = pred[1024,512]{0,1:T(32,128)(4,1)S(1)} reshape(pred[16,64,64,8]{1,0,3,2:T(8,128)(4,1)S(1)} %broadcast_and_fusion) | data formatting | bytes 1048576 | tf_op jit(solution)/shard_map/and | solution.py:99
  14.5 1.0 multiply_convert_fusion.1
  15.6 0.1 copy.18
  15.7 61.5 %all_to_all.5 = bf16[16,64,768]{2,1,0:T(8,128)(2,1)S(1)} all-to-all(bf16[16,64,768]{2,1,0:T(8,128)(2,1)S(1)} %bitcast.33), channel_id=1, replica_groups=mesh['zhi'=4,'zlo'=1,'core'=2,'expert'=4] {'zhi','expert'}, dimensions={0} | all-to-all | bytes 3145728 | tf_op jit(solution)/shard_map/all_to_all | solution.py:107
  77.2 0.0 collective-permute-start.1
  77.2 3.4 %collective-permute-done.1 = bf16[16,64,768]{2,1,0:T(8,128)(2,1)S(1)} collective-permute-done((bf16[16,64,768]{2,1,0:T(8,128)(2,1)S(1)}, bf16[16,64,768]{2,1,0:T(8,128)(2,1)S(1)}, u32[]{:S(2)}, u32[]{:S(2)}) %collective-permute-start.1) | collective-permute-done | bytes 1572896 | tf_op jit(solution)/shard_map/ppermute | solution.py:51
  80.6 1.9 %pad_maximum_fusion = bf16[2,16,64,768]{3,2,1,0:T(8,128)(2,1)} fusion(bf16[1,16,64,768]{3,2,1,0:T(8,128)(2,1)S(1)} %bitcast.37, bf16[1,16,64,768]{3,2,1,0:T(8,128)(2,1)S(1)} %bitcast.34), kind=kLoop, calls=%fused_computation | loop fusion | flops 1572864 | bytes 6291456 | tf_op jit(solution)/shard_map/stack | solution.py:52
  82.6 21.6 %all-gather.3.cloned.1.call-done = bf16[2,1024,1024]{2,1,0:T(8,128)(2,1)} async-done(((bf16[2,64,1024]{2,1,0:T(8,128)(2,1)}), bf16[2,1024,1024]{2,1,0:T(8,128)(2,1)}) %all-gather.3.cloned.1.call-update) | async-done | bytes 4194320 | tf_op jit(solution)/shard_map/all_gather | solution.py:89
  104.1 6.4 %fusion.15 = f32[1024,768]{1,0:T(8,128)S(1)} fusion(bf16[2048,1024]{1,0:T(8,128)(2,1)} %bitcast.42, bf16[2048,768]{1,0:T(8,128)(2,1)} %bitcast.35), kind=kOutput, calls=%fused_computation.44 | convolution fusion | flops 3221225472 | bytes 10485760 | tf_op jit(solution)/shard_map/dot_general | solution.py:114
  110.6 1.5 %multiply_reduce_fusion = (f32[]{:T(128)}, f32[1024,768]{1,0:T(8,128)S(1)}) fusion(f32[1024,768]{1,0:T(8,128)S(1)} %fusion.15, f32[1024,768]{1,0:T(8,128)S(1)} %copy-done.5), kind=kLoop, calls=%fused_computation.5 | loop fusion | flops 4718591 | bytes 9437188 | tf_op jit(solution)/shard_map/reduce_sum | solution.py:121
  112.1 0.1 copy-done.3
  112.2 0.5 fusion.14
  112.7 1.1 copy-done.1
  113.8 0.8 convolution_convert_fusion.2
  114.6 0.1 collective-permute-start.4
  114.7 0.8 convolution_convert_fusion.3
  115.5 0.6 collective-permute-start.3
  116.0 0.1 collective-permute-start.2
  116.1 1.6 %collective-permute-done.2 = f32[]{:T(128)} collective-permute-done((f32[]{:T(128)}, f32[]{:T(128)}, u32[]{:S(2)}, u32[]{:S(2)}) %collective-permute-start.2) | collective-permute-done | bytes 36 | tf_op jit(solution)/shard_map/ppermute | solution.py:70
  119.0 0.0 collective-permute-done.4
  119.0 0.1 convert_add_fusion
  119.2 0.0 collective-permute-done.3
  119.2 0.1 convert_add_fusion.1
  119.3 0.0 copy-start.2
  119.3 1.2 add_convert_fusion.3
  120.5 0.7 copy-done.2
  121.2 1.0 copy-done.4
  122.2 1.7 %add_convert_fusion.1 = bf16[1024,768]{1,0:T(8,128)(2,1)S(1)} fusion(bf16[768,768]{0,1:T(8,128)(2,1)S(1)} %add_convert_fusion.3, f32[]{:T(128)S(6)} %add.59, f32[1024,768]{1,0:T(8,128)S(1)} %copy-done.4, f32[1024,768]{1,0:T(8,128)S(1)} %copy-done.2), kind=kOutput, calls=%fused_computation.3 | convolution fusion | flops 1217396736 | bytes 9043972 | tf_op jit(solution)/shard_map/dot_general | solution.py:25
  123.9 0.9 convolution_convert_fusion
  124.8 0.4 collective-permute-start.6
  125.2 0.8 convolution_convert_fusion.1
  126.1 0.2 collective-permute-start.5
  126.3 0.6 collective-permute-done.6
  126.8 0.1 add_convert_fusion.4
  127.0 1.1 collective-permute-done.5
  128.1 0.1 add_convert_fusion.5
  128.3 1.1 add_convert_fusion.2
  129.4 2.6 %multiply_convert_fusion = bf16[1024,768]{1,0:T(8,128)(2,1)} fusion(bf16[1024,768]{1,0:T(8,128)(2,1)S(1)} %add_convert_fusion.1, bf16[768,768]{0,1:T(8,128)(2,1)S(1)} %add_convert_fusion.2), kind=kOutput, calls=%fused_computation.1 | convolution fusion | flops 1213464576 | bytes 4325376 | tf_op jit(solution)/shard_map/dot_general | solution.py:25
  (15 shorter events, 0.2 us)
Async XLA Ops:
  7.2 7.4 %copy-start = (bf16[64,8,768]{2,1,0:T(8,128)(2,1)S(1)}, bf16[64,8,768]{2,1,0:T(8,128)(2,1)}, u32[]{:S(2)}) copy-start(bf16[64,8,768]{2,1,0:T(8,128)(2,1)} %param.5) | copy-start | bytes 2359300
  7.2 4.2 %copy-start.6 = (s32[64,8]{0,1:T(8,128)S(1)}, s32[64,8]{0,1:T(8,128)}, u32[]{:S(2)}) copy-start(s32[64,8]{0,1:T(8,128)} %param.8) | copy-start | bytes 6148
  7.2 4.2 %copy-start.7 = (f32[64,8]{0,1:T(8,128)S(1)}, f32[64,8]{0,1:T(8,128)}, u32[]{:S(2)}) copy-start(f32[64,8]{0,1:T(8,128)} %param.7) | copy-start | bytes 6148
  7.2 96.9 %all-gather.3.cloned.1.call-start = ((), (), s32[]{:S(2)}) async-start(), calls=%async_computation.1 | async-start | bytes 4456448 | tf_op jit(solution)/shard_map/all_gather | solution.py:89
  9.1 1.5 %collective-permute-start = (bf16[64,1024]{1,0:T(8,128)(2,1)S(1)}, bf16[64,1024]{1,0:T(8,128)(2,1)S(1)}, u32[]{:S(2)}, u32[]{:S(2)}) collective-permute-start(bf16[64,1024]{1,0:T(8,128)(2,1)S(1)} %bitcast.39), channel_id=1, source_target_pairs={{0,4},{4,0},{1,5},{5,1},{2,6},{6,2},{3,7},{7,3},{8,12},{12,8},{9,1... | collective-permute-start | bytes 393224 | tf_op jit(solution)/shard_map/ppermute | solution.py:61
  77.2 3.4 %collective-permute-start.1 = (bf16[16,64,768]{2,1,0:T(8,128)(2,1)S(1)}, bf16[16,64,768]{2,1,0:T(8,128)(2,1)S(1)}, u32[]{:S(2)}, u32[]{:S(2)}) collective-permute-start(bf16[16,64,768]{2,1,0:T(8,128)(2,1)S(1)} %all_to_all.5), channel_id=1, source_target_pairs={{0,4},{4,0},{1,5},{5,1},{2,6},{6,2},{3,7},{7,3},{8,12},{12,8},{9,1... | collective-permute-start | bytes 4718600 | tf_op jit(solution)/shard_map/ppermute | solution.py:51
  104.1 6.4 %copy-start.5 = (f32[1024,768]{1,0:T(8,128)S(1)}, f32[1024,768]{1,0:T(8,128)}, u32[]{:S(2)}) copy-start(f32[1024,768]{1,0:T(8,128)} %param.9) | copy-start | bytes 9437188
  110.5 1.6 %copy-start.3 = (f32[1024,768]{1,0:T(8,128)}, f32[1024,768]{1,0:T(8,128)S(1)}, u32[]{:S(2)}) copy-start(f32[1024,768]{1,0:T(8,128)S(1)} %fusion.15) | copy-start | bytes 9437188
  112.1 1.7 %copy-start.1 = (f32[1024,768]{1,0:T(8,128)}, f32[1024,768]{1,0:T(8,128)S(1)}, u32[]{:S(2)}) copy-start(f32[1024,768]{1,0:T(8,128)S(1)} %get-tuple-element.11) | copy-start | bytes 9437188
  114.6 4.5 %collective-permute-start.4 = (bf16[768,384]{0,1:T(8,128)(2,1)S(1)}, bf16[768,384]{0,1:T(8,128)(2,1)S(1)}, u32[]{:S(2)}, u32[]{:S(2)}) collective-permute-start(bf16[768,384]{0,1:T(8,128)(2,1)S(1)} %convolution_convert_fusion.2), channel_id=1, source_target_pairs={{0,4},{4,0},{1,5},{5,1},{2,6},{6,2},{3,7},{7,3},{8,12},{12,8},{9,1... | collective-permute-start | bytes 1769480 | tf_op jit(solution)/shard_map/ppermute | solution.py:70
  115.5 3.7 %collective-permute-start.3 = (bf16[768,384]{0,1:T(8,128)(2,1)S(1)}, bf16[768,384]{0,1:T(8,128)(2,1)S(1)}, u32[]{:S(2)}, u32[]{:S(2)}) collective-permute-start(bf16[768,384]{0,1:T(8,128)(2,1)S(1)} %convolution_convert_fusion.3), channel_id=1, source_target_pairs={{0,4},{4,0},{1,5},{5,1},{2,6},{6,2},{3,7},{7,3},{8,12},{12,8},{9,1... | collective-permute-start | bytes 1769480 | tf_op jit(solution)/shard_map/ppermute | solution.py:70
  116.0 1.6 %collective-permute-start.2 = (f32[]{:T(128)}, f32[]{:T(128)}, u32[]{:S(2)}, u32[]{:S(2)}) collective-permute-start(f32[]{:T(128)} %get-tuple-element.10), channel_id=1, source_target_pairs={{0,4},{4,0},{1,5},{5,1},{2,6},{6,2},{3,7},{7,3},{8,12},{12,8},{9,1... | collective-permute-start | bytes 20 | tf_op jit(solution)/shard_map/ppermute | solution.py:70
  119.3 1.9 %copy-start.2 = (f32[1024,768]{1,0:T(8,128)S(1)}, f32[1024,768]{1,0:T(8,128)}, u32[]{:S(2)}) copy-start(f32[1024,768]{1,0:T(8,128)} %copy-done.1) | copy-start | bytes 9437188
  119.3 2.8 %copy-start.4 = (f32[1024,768]{1,0:T(8,128)S(1)}, f32[1024,768]{1,0:T(8,128)}, u32[]{:S(2)}) copy-start(f32[1024,768]{1,0:T(8,128)} %copy-done.3) | copy-start | bytes 9437188
  124.8 2.1 %collective-permute-start.6 = (bf16[768,384]{0,1:T(8,128)(2,1)S(1)}, bf16[768,384]{0,1:T(8,128)(2,1)S(1)}, u32[]{:S(2)}, u32[]{:S(2)}) collective-permute-start(bf16[768,384]{0,1:T(8,128)(2,1)S(1)} %convolution_convert_fusion), channel_id=1, source_target_pairs={{0,4},{4,0},{1,5},{5,1},{2,6},{6,2},{3,7},{7,3},{8,12},{12,8},{9,1... | collective-permute-start | bytes 1769480 | tf_op jit(solution)/shard_map/ppermute | solution.py:70
  126.1 2.1 %collective-permute-start.5 = (bf16[768,384]{0,1:T(8,128)(2,1)S(1)}, bf16[768,384]{0,1:T(8,128)(2,1)S(1)}, u32[]{:S(2)}, u32[]{:S(2)}) collective-permute-start(bf16[768,384]{0,1:T(8,128)(2,1)S(1)} %convolution_convert_fusion.1), channel_id=1, source_target_pairs={{0,4},{4,0},{1,5},{5,1},{2,6},{6,2},{3,7},{7,3},{8,12},{12,8},{9,1... | collective-permute-start | bytes 1769480 | tf_op jit(solution)/shard_map/ppermute | solution.py:70
Sparse Core Ops, SparseCore 0:
  11.5 92.5 all-gather.2

commit v16 on v14

--- a/solution.py
+++ b/solution.py
@@ -110,6 +110,7 @@
     raw_gram = group_sum(gram_of(ahead.astype(jnp.bfloat16)), group, group_size, jnp.bfloat16)
     norm_value = jnp.sqrt(square_sum)
     scaled = (ahead / (norm_value + EPSILON)).astype(jnp.bfloat16)
+    scaled = lax.optimization_barrier(scaled)
     inverse = 1.0 / (norm_value + EPSILON)
     for turn_index in range(NS_ITERS):
         if turn_index == 0:

time: 138 us -> 140 us (1.014)
  other arithmetic: 4.86 us -> 8.15 us
    convert_element_type x0 -> x1, other arithmetic: none -> 3.29 us  [body(): scaled = (ahead / (norm_value + EPSILON)).astype(jnp.bfloat16)]
  transfers between devices with their start and end apart: 6 -> 6, of which waited for: 5 -> 5; matrix products, arithmetic and copies ran while one was open for 5% -> 7% of each run, Pallas kernels for 0% -> 0%
where the time goes in v16:
time: 140 us
  blocking collectives  61.5 us (44%)
  waiting for transfers between devices  31.1 us (22%)
  matrix products  17.3 us (12%)
  between operations  15.5 us (11%)
  other arithmetic  8.15 us (6%)
  local copies, waits for them, and re-layouts  4.61 us (3%)
    all_to_all x1, blocking collectives, body(): lax.all_to_all(scaled_hidden, ('zhi', 'expert'), split_axis=0, concat_axi...  61.5 us
    all_gather x1, waiting for transfers between devices, body(): grad_all = lax.all_gather(grad_mine, ('zhi', 'expert'), axis=1, tiled=False)  21.6 us
    dot_general x1, matrix products, body(): lax.dot_general(grad_all, got_hidden, (((0,), (0,)), ((), ())), preferred...  6.39 us
    ppermute x3, waiting for transfers between devices, group_sum(): total = total + lax.ppermute(sent, axes, route).astype(value.dtype)  5.18 us
    dot_general x2, matrix products, newton_update(): product = jnp.dot(scaled, poly, preferred_element_type=jnp.float32)  3.98 us
    ppermute x1, waiting for transfers between devices, group_gather(): parts.append(lax.ppermute(block, axes, route))  3.41 us
    convert_element_type x1, other arithmetic, body(): scaled = (ahead / (norm_value + EPSILON)).astype(jnp.bfloat16)  3.29 us
    dot_general x2, matrix products, gram_of(): lax.dot_general(scaled, scaled, (((0,), (0,)), ((), ())), preferred_eleme...  2.97 us
  transfers between devices with their start and end apart: 6, of which 5 were waited for; matrix products, arithmetic and copies ran while one was open for 7% of the time, Pallas kernels for 0%

profile of v16, /device:TPU:0, one launch (start us, length us, event | category | flops | bytes accessed | tf_op | source)
XLA Modules:
  0.0 139.5 jit_solution(16174869505456847505)
XLA Ops:
  7.2 0.0 copy-start
  7.2 0.0 copy-start.4
  7.2 0.0 copy-start.5
  7.2 0.0 all-gather.3.cloned.1.call-start
  7.3 1.2 reshape.64
  8.5 0.6 constant_dynamic-slice_fusion.1
  9.1 0.6 collective-permute-start
  9.7 0.9 collective-permute-done
  10.6 0.7 pad_maximum_fusion.1
  11.4 0.0 all-gather.3.cloned.1.call-update
  11.4 0.0 copy-done.4
  11.4 0.0 copy-done.5
  11.4 0.1 mul.53
  11.5 0.6 broadcast_and_fusion
  12.2 2.4 %and.34 = pred[1024,512]{0,1:T(32,128)(4,1)S(1)} reshape(pred[16,64,64,8]{1,0,3,2:T(8,128)(4,1)S(1)} %broadcast_and_fusion) | data formatting | bytes 1048576 | tf_op jit(solution)/shard_map/and | solution.py:87
  14.5 0.0 copy-done
  14.6 1.0 multiply_convert_fusion.1
  15.6 0.1 copy.16
  15.7 61.5 %all_to_all.5 = bf16[16,64,768]{2,1,0:T(8,128)(2,1)S(1)} all-to-all(bf16[16,64,768]{2,1,0:T(8,128)(2,1)S(1)} %bitcast.32), channel_id=1, replica_groups=mesh['zhi'=4,'zlo'=1,'core'=2,'expert'=4] {'zhi','expert'}, dimensions={0} | all-to-all | bytes 3145728 | tf_op jit(solution)/shard_map/all_to_all | solution.py:95
  77.2 0.0 collective-permute-start.1
  77.2 3.4 %collective-permute-done.1 = bf16[16,64,768]{2,1,0:T(8,128)(2,1)S(1)} collective-permute-done((bf16[16,64,768]{2,1,0:T(8,128)(2,1)S(1)}, bf16[16,64,768]{2,1,0:T(8,128)(2,1)S(1)}, u32[]{:S(2)}, u32[]{:S(2)}) %collective-permute-start.1) | collective-permute-done | bytes 1572896 | tf_op jit(solution)/shard_map/ppermute | solution.py:39
  80.6 1.9 %pad_maximum_fusion = bf16[2,16,64,768]{3,2,1,0:T(8,128)(2,1)} fusion(bf16[1,16,64,768]{3,2,1,0:T(8,128)(2,1)S(1)} %bitcast.36, bf16[1,16,64,768]{3,2,1,0:T(8,128)(2,1)S(1)} %bitcast.33), kind=kLoop, calls=%fused_computation | loop fusion | flops 1572864 | bytes 6291456 | tf_op jit(solution)/shard_map/stack | solution.py:40
  82.6 21.6 %all-gather.3.cloned.1.call-done = bf16[2,1024,1024]{2,1,0:T(8,128)(2,1)} async-done(((bf16[2,64,1024]{2,1,0:T(8,128)(2,1)}), bf16[2,1024,1024]{2,1,0:T(8,128)(2,1)}) %all-gather.3.cloned.1.call-update) | async-done | bytes 4194320 | tf_op jit(solution)/shard_map/all_gather | solution.py:77
  104.1 0.0 copy-start.3
  104.1 6.4 %fusion.7 = f32[1024,768]{1,0:T(8,128)S(1)} fusion(bf16[2048,1024]{1,0:T(8,128)(2,1)} %bitcast.41, bf16[2048,768]{1,0:T(8,128)(2,1)} %bitcast.34), kind=kOutput, calls=%fused_computation.29 | convolution fusion | flops 3221225472 | bytes 10485760 | tf_op jit(solution)/shard_map/dot_general | solution.py:102
  110.5 0.0 copy-done.3
  110.6 0.0 copy-start.2
  110.6 1.5 %multiply_reduce_fusion = (f32[]{:T(128)}, f32[1024,768]{1,0:T(8,128)S(1)}) fusion(f32[1024,768]{1,0:T(8,128)S(1)} %fusion.7, f32[1024,768]{1,0:T(8,128)S(1)} %copy-done.3), kind=kLoop, calls=%fused_computation.5 | loop fusion | flops 4718591 | bytes 9437188 | tf_op jit(solution)/shard_map/reduce_sum | solution.py:109
  112.1 0.0 copy-start.1
  112.1 0.1 copy-done.2
  112.2 1.5 %fusion.2 = bf16[768,768]{1,0:T(8,128)(2,1)S(1)} fusion(f32[1024,768]{1,0:T(8,128)S(1)} %fusion.7, f32[1024,768]{1,0:T(8,128)S(1)} %get-tuple-element.11), kind=kOutput, calls=%fused_computation.16 | convolution fusion | flops 1210908672 | bytes 7471104 | tf_op jit(solution)/shard_map/dot_general | solution.py:30
  113.7 0.1 copy-done.1
  113.8 0.0 collective-permute-start.3
  113.8 0.5 collective-permute-start.2
  114.3 2.5 %collective-permute-done.2 = f32[]{:T(128)} collective-permute-done((f32[]{:T(128)}, f32[]{:T(128)}, u32[]{:S(2)}, u32[]{:S(2)}) %collective-permute-start.2) | collective-permute-done | bytes 36 | tf_op jit(solution)/shard_map/ppermute | solution.py:58
  118.0 3.3 %divide_convert_fusion = bf16[1024,768]{1,0:T(8,128)(2,1)S(1)} fusion(f32[]{:T(128)S(6)} %add.53, f32[1024,768]{1,0:T(8,128)} %copy-done.2, f32[1024,768]{1,0:T(8,128)} %copy-done.1), kind=kLoop, calls=%fused_computation.4 | loop fusion | flops 3145728 | bytes 7864324 | tf_op jit(solution)/shard_map/convert_element_type | solution.py:112
  121.3 0.0 collective-permute-done.3
  121.3 1.6 %add_convert_fusion.4 = bf16[768,768]{1,0:T(8,128)(2,1)S(1)} fusion(bf16[768,768]{1,0:T(8,128)(2,1)S(1)} %collective-permute-done.3, bf16[768,768]{1,0:T(8,128)(2,1)S(1)} %fusion.2, f32[]{:T(128)S(6)} %mul.60), kind=kOutput, calls=%fused_computation.11 | convolution fusion | flops 914817024 | bytes 3538948 | tf_op jit(solution)/shard_map/dot_general | solution.py:22
  122.9 1.4 %add_convert_fusion.1 = bf16[1024,768]{1,0:T(8,128)(2,1)S(1)} fusion(bf16[1024,768]{1,0:T(8,128)(2,1)S(1)} %divide_convert_fusion, bf16[768,768]{1,0:T(8,128)(2,1)S(1)} %add_convert_fusion.4), kind=kOutput, calls=%fused_computation.3 | convolution fusion | flops 1211105280 | bytes 4325376 | tf_op jit(solution)/shard_map/dot_general | solution.py:25
  124.3 1.5 %convolution_convert_fusion = bf16[768,768]{1,0:T(8,128)(2,1)S(1)} fusion(bf16[1024,768]{1,0:T(8,128)(2,1)S(1)} %add_convert_fusion.1), kind=kOutput, calls=%fused_computation.17 | convolution fusion | flops 1208549376 | bytes 2752512 | tf_op jit(solution)/shard_map/dot_general | solution.py:30
  125.8 0.2 collective-permute-start.4
  126.0 2.7 %collective-permute-done.4 = bf16[768,768]{1,0:T(8,128)(2,1)S(1)} collective-permute-done((bf16[768,768]{1,0:T(8,128)(2,1)S(1)}, bf16[768,768]{1,0:T(8,128)(2,1)S(1)}, u32[]{:S(2)}, u32[]{:S(2)}) %collective-permute-start.4) | collective-permute-done | bytes 1179680 | tf_op jit(solution)/shard_map/ppermute | solution.py:58
  128.7 1.4 add_convert_fusion.2
  130.1 2.6 %multiply_convert_fusion = bf16[1024,768]{1,0:T(8,128)(2,1)} fusion(bf16[1024,768]{1,0:T(8,128)(2,1)S(1)} %add_convert_fusion.1, bf16[768,768]{1,0:T(8,128)(2,1)S(1)} %add_convert_fusion.2), kind=kOutput, calls=%fused_computation.1 | convolution fusion | flops 1213464576 | bytes 4325376 | tf_op jit(solution)/shard_map/dot_general | solution.py:25
  (5 shorter events, 0.1 us)
Async XLA Ops:
  7.2 7.4 %copy-start = (bf16[64,8,768]{2,1,0:T(8,128)(2,1)S(1)}, bf16[64,8,768]{2,1,0:T(8,128)(2,1)}, u32[]{:S(2)}) copy-start(bf16[64,8,768]{2,1,0:T(8,128)(2,1)} %param.5) | copy-start | bytes 2359300
  7.2 4.2 %copy-start.4 = (s32[64,8]{0,1:T(8,128)S(1)}, s32[64,8]{0,1:T(8,128)}, u32[]{:S(2)}) copy-start(s32[64,8]{0,1:T(8,128)} %param.8) | copy-start | bytes 6148
  7.2 4.2 %copy-start.5 = (f32[64,8]{0,1:T(8,128)S(1)}, f32[64,8]{0,1:T(8,128)}, u32[]{:S(2)}) copy-start(f32[64,8]{0,1:T(8,128)} %param.7) | copy-start | bytes 6148
  7.2 96.9 %all-gather.3.cloned.1.call-start = ((), (), s32[]{:S(2)}) async-start(), calls=%async_computation.1 | async-start | bytes 4456448 | tf_op jit(solution)/shard_map/all_gather | solution.py:77
  9.1 1.5 %collective-permute-start = (bf16[64,1024]{1,0:T(8,128)(2,1)S(1)}, bf16[64,1024]{1,0:T(8,128)(2,1)S(1)}, u32[]{:S(2)}, u32[]{:S(2)}) collective-permute-start(bf16[64,1024]{1,0:T(8,128)(2,1)S(1)} %bitcast.38), channel_id=1, source_target_pairs={{0,4},{4,0},{1,5},{5,1},{2,6},{6,2},{3,7},{7,3},{8,12},{12,8},{9,1... | collective-permute-start | bytes 393224 | tf_op jit(solution)/shard_map/ppermute | solution.py:49
  77.2 3.4 %collective-permute-start.1 = (bf16[16,64,768]{2,1,0:T(8,128)(2,1)S(1)}, bf16[16,64,768]{2,1,0:T(8,128)(2,1)S(1)}, u32[]{:S(2)}, u32[]{:S(2)}) collective-permute-start(bf16[16,64,768]{2,1,0:T(8,128)(2,1)S(1)} %all_to_all.5), channel_id=1, source_target_pairs={{0,4},{4,0},{1,5},{5,1},{2,6},{6,2},{3,7},{7,3},{8,12},{12,8},{9,1... | collective-permute-start | bytes 4718600 | tf_op jit(solution)/shard_map/ppermute | solution.py:39
  104.1 6.4 %copy-start.3 = (f32[1024,768]{1,0:T(8,128)S(1)}, f32[1024,768]{1,0:T(8,128)}, u32[]{:S(2)}) copy-start(f32[1024,768]{1,0:T(8,128)} %param.9) | copy-start | bytes 9437188
  110.6 1.6 %copy-start.2 = (f32[1024,768]{1,0:T(8,128)}, f32[1024,768]{1,0:T(8,128)S(1)}, u32[]{:S(2)}) copy-start(f32[1024,768]{1,0:T(8,128)S(1)} %fusion.7) | copy-start | bytes 9437188
  112.1 1.7 %copy-start.1 = (f32[1024,768]{1,0:T(8,128)}, f32[1024,768]{1,0:T(8,128)S(1)}, u32[]{:S(2)}) copy-start(f32[1024,768]{1,0:T(8,128)S(1)} %get-tuple-element.11) | copy-start | bytes 9437188
  113.8 7.6 %collective-permute-start.3 = (bf16[768,768]{1,0:T(8,128)(2,1)S(1)}, bf16[768,768]{1,0:T(8,128)(2,1)S(1)}, u32[]{:S(2)}, u32[]{:S(2)}) collective-permute-start(bf16[768,768]{1,0:T(8,128)(2,1)S(1)} %fusion.2), channel_id=1, source_target_pairs={{0,4},{4,0},{1,5},{5,1},{2,6},{6,2},{3,7},{7,3},{8,12},{12,8},{9,1... | collective-permute-start | bytes 3538952 | tf_op jit(solution)/shard_map/ppermute | solution.py:58
  113.8 3.0 %collective-permute-start.2 = (f32[]{:T(128)}, f32[]{:T(128)}, u32[]{:S(2)}, u32[]{:S(2)}) collective-permute-start(f32[]{:T(128)} %get-tuple-element.10), channel_id=1, source_target_pairs={{0,4},{4,0},{1,5},{5,1},{2,6},{6,2},{3,7},{7,3},{8,12},{12,8},{9,1... | collective-permute-start | bytes 20 | tf_op jit(solution)/shard_map/ppermute | solution.py:58
  125.8 2.9 %collective-permute-start.4 = (bf16[768,768]{1,0:T(8,128)(2,1)S(1)}, bf16[768,768]{1,0:T(8,128)(2,1)S(1)}, u32[]{:S(2)}, u32[]{:S(2)}) collective-permute-start(bf16[768,768]{1,0:T(8,128)(2,1)S(1)} %convolution_convert_fusion), channel_id=1, source_target_pairs={{0,4},{4,0},{1,5},{5,1},{2,6},{6,2},{3,7},{7,3},{8,12},{12,8},{9,1... | collective-permute-start | bytes 3538952 | tf_op jit(solution)/shard_map/ppermute | solution.py:58
Sparse Core Ops, SparseCore 0:
  11.5 92.5 all-gather.2
